TPU v7x, 512 devices: a whole 4x4x16 slice. The times are simulated.
512 devices in a mesh: section: 8 (over x, core), dp: 64 (over y, z).
Axes of the slice: x: 4, y: 4, z: 16, core: 2. Of those that a mesh axis runs over, the one named last changes fastest.
Arguments:
- activations: bfloat16 [8, 8192, 5120], P('section', 'dp'), may hold values from -200 to 200, as said below
- upstream: bfloat16 [8, 8192, 5120], P('section', 'dp'), may hold values from -120 to 120, as said below
- section_norm_gain: float32 [8, 5120], P('section'), may hold values from 0.1 to 1.9
- adapter_down_weight: bfloat16 [8, 16, 5120], P('section'), may hold values from -0.078125 to 0.078125
- adapter_up_weight: bfloat16 [8, 16, 5120], P('section'), may hold values from -0.078125 to 0.078125
Outputs:
- passed: bfloat16 [8, 8192, 5120], P('section', 'dp')
- grad_pair: bfloat16 [8, 163840], P('section', 'dp')
Inputs may be any that keep to these rules, and one draw needn't show every extreme that they name: `activations`: activations of one token position share a part across replicas; rows and features have different scales. `upstream`: gradients of one token position share a part across replicas.
All inputs are finite; a program needn't handle non-finite values.
Results may differ from a plain program's by a relative error of at most 0.0034.
Values may be sent and summed in bfloat16 or wider, within the bound.
No kernel may reach another device: no remote copies, remote signals or barrier semaphores. Data moves between devices by JAX's collectives and lax.ppermute only.
A program may use at most 64 MiB of HBM per device.

v0:
```python
import jax
import jax.numpy as jnp
from jax import lax
from jax.sharding import PartitionSpec as P

norm_eps = 1e-05
pair_eps = 1e-06
adapter_scale = 2.0


def swapped(value, axis, bit):
    mask = 2**bit
    pairs = [(source, source ^ mask) for source in range(lax.axis_size(axis))]
    return lax.ppermute(value, axis, pairs)


def from_behind(x, axis, by):
    size = lax.axis_size(axis)
    pairs = [(i, i + by) for i in range(size) if 0 <= i + by < size]
    return lax.ppermute(x, axis, pairs)


def replica_backward(inputs, incoming_gradient, gain_row, down_rows, upward_rows):
    widened = inputs.astype(jnp.float32)
    inverse = lax.rsqrt(jnp.mean(widened * widened, axis=-1, keepdims=True) + norm_eps)
    scaled = widened * inverse
    normed = (scaled * gain_row).astype(jnp.bfloat16)
    reduced_gradient = jnp.einsum(
        "sh,gh->sg", normed, down_rows, preferred_element_type=jnp.float32
    ).astype(jnp.bfloat16)
    count_of_rows = inputs.shape[0]
    upward_term = (
        adapter_scale
        * jnp.einsum(
            "tk,td->kd", reduced_gradient, incoming_gradient, preferred_element_type=jnp.float32
        )
        / count_of_rows
    )
    backward_lowrank = (
        adapter_scale
        * jnp.einsum(
            "sh,gh->sg", incoming_gradient, upward_rows, preferred_element_type=jnp.float32
        )
    ).astype(jnp.bfloat16)
    down_term = (
        jnp.einsum("tk,td->kd", backward_lowrank, normed, preferred_element_type=jnp.float32)
        / count_of_rows
    )
    back_norm = (
        jnp.einsum("tk,kd->td", backward_lowrank, down_rows, preferred_element_type=jnp.float32)
        * gain_row
    )
    centre = jnp.mean(back_norm * scaled, axis=-1, keepdims=True)
    passed = incoming_gradient.astype(jnp.float32) + inverse * (back_norm - scaled * centre)
    return (passed.astype(jnp.bfloat16), jnp.stack([down_term, upward_term]))


def doubling_tree(grad_pair):
    vector = grad_pair.reshape(2, -1)
    devices = lax.axis_size("dp")
    tree_levels = devices.bit_length() - 1
    for level_bit in range(tree_levels):
        partner = swapped(vector, "dp", level_bit)
        inner_sum = jnp.sum(vector * partner, axis=1, keepdims=True)
        own_square = jnp.sum(vector * vector, axis=1, keepdims=True)
        far_square = jnp.sum(partner * partner, axis=1, keepdims=True)
        keep_coef = 1.0 - inner_sum / (2.0 * (own_square + pair_eps))
        take_coef = 1.0 - inner_sum / (2.0 * (far_square + pair_eps))
        vector = keep_coef * vector + take_coef * partner
    flat_vector = vector.reshape(-1)
    slice_width = flat_vector.shape[0] // devices
    own_slice = lax.dynamic_slice_in_dim(
        flat_vector, lax.axis_index("dp") * slice_width, slice_width, 0
    )
    return own_slice.astype(jnp.bfloat16)[None]


def per_device(activations, upstream, section_norm_gain, adapter_down_weight, adapter_up_weight):
    passed_local, grad_pair = replica_backward(
        activations[0],
        upstream[0],
        section_norm_gain[0],
        adapter_down_weight[0],
        adapter_up_weight[0],
    )
    shifted = from_behind(passed_local[None], "section", -1)
    merged_gradient = doubling_tree(grad_pair)
    return (shifted, merged_gradient)


def solution(mesh):
    return jax.shard_map(
        per_device,
        mesh=mesh,
        in_specs=(
            P("section", "dp", None),
            P("section", "dp", None),
            P("section", None),
            P("section", None, None),
            P("section", None, None),
        ),
        out_specs=(P("section", "dp", None), P("section", "dp")),
        check_vma=False,
    )
```

profile of v0, /device:TPU:6, one launch (start us, length us, event | category | flops | bytes accessed | tf_op | source)
XLA Modules:
  0.0 255.7 jit_solution(11757806291956692739)
XLA Ops:
  0.7 1.8 fusion.13
  2.5 1.8 fusion.34
  4.3 1.2 fusion
  5.9 0.5 fusion.1
  6.7 0.6 pad_maximum_fusion
  7.3 3.8 %collective-permute-start.1 = (f32[2,81920]{1,0:T(2,128)S(1)}, f32[2,81920]{1,0:T(2,128)S(1)}, u32[]{:S(2)}, u32[]{:S(2)}) collective-permute-start(f32[2,81920]{1,0:T(2,128)S(1)} %pad_maximum_fusion), channel_id=1, source_target_pairs={{0,1},{1,0},{2,3},{3,2},{4,5},{5,4},{6,7},{7,6},{8,9},{9,8},{10,11... | collective-permute-start | bytes 1966088 | tf_op jit(solution)/shard_map/ppermute | solution.py:14
  11.1 14.7 %collective-permute-done.1 = f32[2,81920]{1,0:T(2,128)S(1)} collective-permute-done((f32[2,81920]{1,0:T(2,128)S(1)}, f32[2,81920]{1,0:T(2,128)S(1)}, u32[]{:S(2)}, u32[]{:S(2)}) %collective-permute-start.1) | collective-permute-done | bytes 655392 | tf_op jit(solution)/shard_map/ppermute | solution.py:14
  25.8 1.5 multiply_reduce_fusion.16
  27.3 0.7 multiply_add_fusion.4
  28.1 5.2 %collective-permute-start.2 = (f32[2,81920]{1,0:T(2,128)S(1)}, f32[2,81920]{1,0:T(2,128)S(1)}, u32[]{:S(2)}, u32[]{:S(2)}) collective-permute-start(f32[2,81920]{1,0:T(2,128)S(1)} %multiply_add_fusion.4), channel_id=1, source_target_pairs={{0,2},{1,3},{2,0},{3,1},{4,6},{5,7},{6,4},{7,5},{8,10},{9,11},{10,... | collective-permute-start | bytes 1966088 | tf_op jit(solution)/shard_map/ppermute | solution.py:14
  33.3 28.1 %collective-permute-done.2 = f32[2,81920]{1,0:T(2,128)S(1)} collective-permute-done((f32[2,81920]{1,0:T(2,128)S(1)}, f32[2,81920]{1,0:T(2,128)S(1)}, u32[]{:S(2)}, u32[]{:S(2)}) %collective-permute-start.2) | collective-permute-done | bytes 655392 | tf_op jit(solution)/shard_map/ppermute | solution.py:14
  61.4 1.1 multiply_reduce_fusion.13
  62.4 0.4 multiply_add_fusion.3
  62.8 9.1 %collective-permute-start.3 = (f32[2,81920]{1,0:T(2,128)S(1)}, f32[2,81920]{1,0:T(2,128)S(1)}, u32[]{:S(2)}, u32[]{:S(2)}) collective-permute-start(f32[2,81920]{1,0:T(2,128)S(1)} %multiply_add_fusion.3), channel_id=1, source_target_pairs={{0,4},{1,5},{2,6},{3,7},{4,0},{5,1},{6,2},{7,3},{8,12},{9,13},{10,... | collective-permute-start | bytes 1966088 | tf_op jit(solution)/shard_map/ppermute | solution.py:14
  72.0 55.0 %collective-permute-done.3 = f32[2,81920]{1,0:T(2,128)S(1)} collective-permute-done((f32[2,81920]{1,0:T(2,128)S(1)}, f32[2,81920]{1,0:T(2,128)S(1)}, u32[]{:S(2)}, u32[]{:S(2)}) %collective-permute-start.3) | collective-permute-done | bytes 655392 | tf_op jit(solution)/shard_map/ppermute | solution.py:14
  127.0 1.1 multiply_reduce_fusion.10
  128.0 0.4 multiply_add_fusion.2
  128.5 55.6 %collective-permute-start.4 = (f32[2,81920]{1,0:T(2,128)S(1)}, f32[2,81920]{1,0:T(2,128)S(1)}, u32[]{:S(2)}, u32[]{:S(2)}) collective-permute-start(f32[2,81920]{1,0:T(2,128)S(1)} %multiply_add_fusion.2), channel_id=1, source_target_pairs={{0,8},{1,9},{2,10},{3,11},{4,12},{5,13},{6,14},{7,15},{8,0},{9,1},... | collective-permute-start | bytes 1966088 | tf_op jit(solution)/shard_map/ppermute | solution.py:14
  184.1 0.7 fusion.7
  184.8 28.3 %collective-permute-done.4 = f32[2,81920]{1,0:T(2,128)S(1)} collective-permute-done((f32[2,81920]{1,0:T(2,128)S(1)}, f32[2,81920]{1,0:T(2,128)S(1)}, u32[]{:S(2)}, u32[]{:S(2)}) %collective-permute-start.4) | collective-permute-done | bytes 655392 | tf_op jit(solution)/shard_map/ppermute | solution.py:14
  213.1 1.1 multiply_reduce_fusion.7
  214.6 3.5 %collective-permute-start.5 = (f32[2,81920]{1,0:T(2,128)S(1)}, f32[2,81920]{1,0:T(2,128)S(1)}, u32[]{:S(2)}, u32[]{:S(2)}) collective-permute-start(f32[2,81920]{1,0:T(2,128)S(1)} %multiply_add_fusion.1), channel_id=1, source_target_pairs={{0,16},{1,17},{2,18},{3,19},{4,20},{5,21},{6,22},{7,23},{8,24},{9,... | collective-permute-start | bytes 1966088 | tf_op jit(solution)/shard_map/ppermute | solution.py:14
  218.1 1.9 fusion.20
  219.9 2.1 collective-permute-start
  222.0 10.4 %collective-permute-done.5 = f32[2,81920]{1,0:T(2,128)S(1)} collective-permute-done((f32[2,81920]{1,0:T(2,128)S(1)}, f32[2,81920]{1,0:T(2,128)S(1)}, u32[]{:S(2)}, u32[]{:S(2)}) %collective-permute-start.5) | collective-permute-done | bytes 655392 | tf_op jit(solution)/shard_map/ppermute | solution.py:14
  232.4 1.1 multiply_reduce_fusion.4
  233.9 5.1 %collective-permute-start.6 = (f32[2,81920]{1,0:T(2,128)S(1)}, f32[2,81920]{1,0:T(2,128)S(1)}, u32[]{:S(2)}, u32[]{:S(2)}) collective-permute-start(f32[2,81920]{1,0:T(2,128)S(1)} %multiply_add_fusion), channel_id=1, source_target_pairs={{0,32},{1,33},{2,34},{3,35},{4,36},{5,37},{6,38},{7,39},{8,40},{9,... | collective-permute-start | bytes 1966088 | tf_op jit(solution)/shard_map/ppermute | solution.py:14
  239.0 13.4 %collective-permute-done.6 = f32[2,81920]{1,0:T(2,128)S(1)} collective-permute-done((f32[2,81920]{1,0:T(2,128)S(1)}, f32[2,81920]{1,0:T(2,128)S(1)}, u32[]{:S(2)}, u32[]{:S(2)}) %collective-permute-start.6) | collective-permute-done | bytes 655392 | tf_op jit(solution)/shard_map/ppermute | solution.py:14
  252.4 1.1 multiply_reduce_fusion.1
  253.4 0.4 add_bitcast_fusion
  254.0 0.6 broadcast_in_dim.5
  254.6 1.1 copy.11
  (23 shorter events, 1.8 us)
Async XLA Ops:
  0.6 3.6 %copy-start = (bf16[1,16,5120]{2,1,0:T(8,128)(2,1)S(1)}, bf16[1,16,5120]{2,1,0:T(8,128)(2,1)}, u32[]{:S(2)}) copy-start(bf16[1,16,5120]{2,1,0:T(8,128)(2,1)} %param.8) | copy-start | bytes 491524
  0.6 3.6 %copy-start.1 = (bf16[1,128,5120]{2,1,0:T(8,128)(2,1)S(1)}, bf16[1,128,5120]{2,1,0:T(8,128)(2,1)}, u32[]{:S(2)}) copy-start(bf16[1,128,5120]{2,1,0:T(8,128)(2,1)} %param.5) | copy-start | bytes 3932164
  0.7 3.6 %copy-start.2 = (bf16[1,128,5120]{2,1,0:T(8,128)(2,1)S(1)}, bf16[1,128,5120]{2,1,0:T(8,128)(2,1)}, u32[]{:S(2)}) copy-start(bf16[1,128,5120]{2,1,0:T(8,128)(2,1)} %param.6) | copy-start | bytes 3932164
  0.7 3.6 %copy-start.3 = (f32[1,5120]{1,0:T(1,128)S(1)}, f32[1,5120]{1,0:T(1,128)}, u32[]{:S(2)}) copy-start(f32[1,5120]{1,0:T(1,128)} %param.7) | copy-start | bytes 61444
  7.3 18.5 %collective-permute-start.1 = (f32[2,81920]{1,0:T(2,128)S(1)}, f32[2,81920]{1,0:T(2,128)S(1)}, u32[]{:S(2)}, u32[]{:S(2)}) collective-permute-start(f32[2,81920]{1,0:T(2,128)S(1)} %pad_maximum_fusion), channel_id=1, source_target_pairs={{0,1},{1,0},{2,3},{3,2},{4,5},{5,4},{6,7},{7,6},{8,9},{9,8},{10,11... | collective-permute-start | bytes 1966088 | tf_op jit(solution)/shard_map/ppermute | solution.py:14
  28.1 33.3 %collective-permute-start.2 = (f32[2,81920]{1,0:T(2,128)S(1)}, f32[2,81920]{1,0:T(2,128)S(1)}, u32[]{:S(2)}, u32[]{:S(2)}) collective-permute-start(f32[2,81920]{1,0:T(2,128)S(1)} %multiply_add_fusion.4), channel_id=1, source_target_pairs={{0,2},{1,3},{2,0},{3,1},{4,6},{5,7},{6,4},{7,5},{8,10},{9,11},{10,... | collective-permute-start | bytes 1966088 | tf_op jit(solution)/shard_map/ppermute | solution.py:14
  62.8 64.1 %collective-permute-start.3 = (f32[2,81920]{1,0:T(2,128)S(1)}, f32[2,81920]{1,0:T(2,128)S(1)}, u32[]{:S(2)}, u32[]{:S(2)}) collective-permute-start(f32[2,81920]{1,0:T(2,128)S(1)} %multiply_add_fusion.3), channel_id=1, source_target_pairs={{0,4},{1,5},{2,6},{3,7},{4,0},{5,1},{6,2},{7,3},{8,12},{9,13},{10,... | collective-permute-start | bytes 1966088 | tf_op jit(solution)/shard_map/ppermute | solution.py:14
  128.5 84.6 %collective-permute-start.4 = (f32[2,81920]{1,0:T(2,128)S(1)}, f32[2,81920]{1,0:T(2,128)S(1)}, u32[]{:S(2)}, u32[]{:S(2)}) collective-permute-start(f32[2,81920]{1,0:T(2,128)S(1)} %multiply_add_fusion.2), channel_id=1, source_target_pairs={{0,8},{1,9},{2,10},{3,11},{4,12},{5,13},{6,14},{7,15},{8,0},{9,1},... | collective-permute-start | bytes 1966088 | tf_op jit(solution)/shard_map/ppermute | solution.py:14
  214.6 17.8 %collective-permute-start.5 = (f32[2,81920]{1,0:T(2,128)S(1)}, f32[2,81920]{1,0:T(2,128)S(1)}, u32[]{:S(2)}, u32[]{:S(2)}) collective-permute-start(f32[2,81920]{1,0:T(2,128)S(1)} %multiply_add_fusion.1), channel_id=1, source_target_pairs={{0,16},{1,17},{2,18},{3,19},{4,20},{5,21},{6,22},{7,23},{8,24},{9,... | collective-permute-start | bytes 1966088 | tf_op jit(solution)/shard_map/ppermute | solution.py:14
  219.9 19.0 %collective-permute-start = (bf16[1,128,5120]{2,1,0:T(8,128)(2,1)}, bf16[1,128,5120]{2,1,0:T(8,128)(2,1)S(1)}, u32[]{:S(2)}, u32[]{:S(2)}) collective-permute-start(bf16[1,128,5120]{2,1,0:T(8,128)(2,1)} %fusion.20), channel_id=1, source_target_pairs={{64,0},{128,64},{192,128},{256,192},{320,256},{384,320},{448,384},... | collective-permute-start | bytes 3932168 | tf_op jit(solution)/shard_map/ppermute | solution.py:20
  233.9 18.5 %collective-permute-start.6 = (f32[2,81920]{1,0:T(2,128)S(1)}, f32[2,81920]{1,0:T(2,128)S(1)}, u32[]{:S(2)}, u32[]{:S(2)}) collective-permute-start(f32[2,81920]{1,0:T(2,128)S(1)} %multiply_add_fusion), channel_id=1, source_target_pairs={{0,32},{1,33},{2,34},{3,35},{4,36},{5,37},{6,38},{7,39},{8,40},{9,... | collective-permute-start | bytes 1966088 | tf_op jit(solution)/shard_map/ppermute | solution.py:14
where the time goes:
time: 256 us
  waiting for transfers between devices  150 us (59%)
  starting transfers between devices  84.4 us (33%)
  other arithmetic  13.9 us (5%)
  matrix products  4.13 us (2%)
    ppermute x6, waiting for transfers between devices, swapped(): return lax.ppermute(value, axis, pairs)  150 us
    ppermute x6, starting transfers between devices, swapped(): return lax.ppermute(value, axis, pairs)  82.3 us
    reduce_sum x6, other arithmetic, doubling_tree(): own_square = jnp.sum(vector * vector, axis=1, keepdims=True)  6.75 us
  transfers between devices with their start and end apart: 7, of which 6 were waited for; matrix products, arithmetic and copies ran while one was open for 2% of the time, Pallas kernels for 0%

commit v1 on v0

--- a/solution.py
+++ b/solution.py
@@ -6,12 +6,7 @@
 norm_eps = 1e-05
 pair_eps = 1e-06
 adapter_scale = 2.0
-
-
-def swapped(value, axis, bit):
-    mask = 2**bit
-    pairs = [(source, source ^ mask) for source in range(lax.axis_size(axis))]
-    return lax.ppermute(value, axis, pairs)
+HIGH = lax.Precision.HIGHEST
 
 
 def from_behind(x, axis, by):
@@ -55,24 +50,43 @@
     return (passed.astype(jnp.bfloat16), jnp.stack([down_term, upward_term]))
 
 
-def doubling_tree(grad_pair):
-    vector = grad_pair.reshape(2, -1)
-    devices = lax.axis_size("dp")
-    tree_levels = devices.bit_length() - 1
-    for level_bit in range(tree_levels):
-        partner = swapped(vector, "dp", level_bit)
-        inner_sum = jnp.sum(vector * partner, axis=1, keepdims=True)
-        own_square = jnp.sum(vector * vector, axis=1, keepdims=True)
-        far_square = jnp.sum(partner * partner, axis=1, keepdims=True)
+def swap_rows(c, level_bit):
+    t, n = c.shape[0], c.shape[1]
+    rest = c.shape[2:]
+    g = c.reshape((t, n // 2 ** (level_bit + 1), 2, 2 ** level_bit) + rest)
+    return g[:, :, ::-1].reshape(c.shape)
+
+
+def coefficient_tree(gram):
+    tensors, n = gram.shape[0], gram.shape[1]
+    coef = jnp.broadcast_to(jnp.eye(n, dtype=jnp.float32), (tensors, n, n))
+    for level_bit in range(n.bit_length() - 1):
+        partner = swap_rows(coef, level_bit)
+        gc = jnp.einsum("tra,tab->trb", coef, gram, precision=HIGH)
+        inner_sum = jnp.sum(gc * partner, axis=-1, keepdims=True)
+        own_square = jnp.sum(gc * coef, axis=-1, keepdims=True)
+        far_square = swap_rows(own_square, level_bit)
         keep_coef = 1.0 - inner_sum / (2.0 * (own_square + pair_eps))
         take_coef = 1.0 - inner_sum / (2.0 * (far_square + pair_eps))
-        vector = keep_coef * vector + take_coef * partner
-    flat_vector = vector.reshape(-1)
-    slice_width = flat_vector.shape[0] // devices
-    own_slice = lax.dynamic_slice_in_dim(
-        flat_vector, lax.axis_index("dp") * slice_width, slice_width, 0
-    )
-    return own_slice.astype(jnp.bfloat16)[None]
+        coef = keep_coef * coef + take_coef * partner
+    return coef[:, 0, :]
+
+
+def gram_adasum(grad_pair):
+    devices = lax.axis_size("dp")
+    me = lax.axis_index("dp")
+    flat = grad_pair.reshape(devices, -1)
+    chunks = lax.all_to_all(flat, "dp", 0, 0, tiled=True)
+    tensors = grad_pair.shape[0]
+    per_tensor = devices // tensors
+    mine = me // per_tensor
+    partial = jnp.dot(chunks, chunks.T, precision=HIGH, preferred_element_type=jnp.float32)
+    slot = (jnp.arange(tensors) == mine)[:, None, None]
+    gram = lax.psum(jnp.where(slot, partial[None], 0.0), "dp")
+    coef = coefficient_tree(gram)
+    own_coef = jnp.sum(jnp.where((jnp.arange(tensors) == mine)[:, None], coef, 0.0), axis=0)
+    combined = jnp.sum(own_coef[:, None] * chunks, axis=0)
+    return combined.astype(jnp.bfloat16)[None]
 
 
 def per_device(activations, upstream, section_norm_gain, adapter_down_weight, adapter_up_weight):
@@ -84,7 +98,7 @@
         adapter_up_weight[0],
     )
     shifted = from_behind(passed_local[None], "section", -1)
-    merged_gradient = doubling_tree(grad_pair)
+    merged_gradient = gram_adasum(grad_pair)
     return (shifted, merged_gradient)
 
 

time: 256 us -> 352 us (1.38)
  blocking collectives: 0 us -> 275 us
  waiting for transfers between devices: 150 us -> 32.1 us
  starting transfers between devices: 84.4 us -> 20.6 us
  local copies, waits for them, and re-layouts: 2.52 us -> 10.4 us
  other arithmetic: 13.9 us -> 6.14 us
    psum x0 -> x1, blocking collectives: none -> 275 us  [gram_adasum(): gram = lax.psum(jnp.where(slot, partial[None], 0.0), 'dp')]
    ppermute x6 -> x0, waiting for transfers between devices: 150 us -> none  [swapped(): return lax.ppermute(value, axis, pairs)]
    ppermute x6 -> x0, starting transfers between devices: 82.3 us -> none  [swapped(): return lax.ppermute(value, axis, pairs)]
    all_to_all x0 -> x1, starting transfers between devices: none -> 18.7 us  [gram_adasum(): chunks = lax.all_to_all(flat, 'dp', 0, 0, tiled=True)]
    all_to_all x0 -> x1, waiting for transfers between devices: none -> 17.5 us  [gram_adasum(): chunks = lax.all_to_all(flat, 'dp', 0, 0, tiled=True)]
    ppermute x1, waiting for transfers between devices: 0.01 us -> 14.6 us  [from_behind(): return lax.ppermute(x, axis, pairs)]
    reduce_sum x6 -> x2, other arithmetic: 6.75 us -> 0.23 us  [the longest x1 0.15 us: gram_adasum(): combined = jnp.sum(own_coef[:, None] * chunks, axis=0)]
  transfers between devices with their start and end apart: 7 -> 2, of which waited for: 6 -> 2; matrix products, arithmetic and copies ran while one was open for 2% -> 1% of each run, Pallas kernels for 0% -> 0%
where the time goes in v1:
time: 352 us
  blocking collectives  275 us (78%)
  waiting for transfers between devices  32.1 us (9%)
  starting transfers between devices  20.6 us (6%)
  local copies, waits for them, and re-layouts  10.4 us (3%)
  matrix products  6.79 us (2%)
  other arithmetic  6.14 us (2%)
    psum x1, blocking collectives, gram_adasum(): gram = lax.psum(jnp.where(slot, partial[None], 0.0), 'dp')  275 us
    all_to_all x1, starting transfers between devices, gram_adasum(): chunks = lax.all_to_all(flat, 'dp', 0, 0, tiled=True)  18.7 us
    all_to_all x1, waiting for transfers between devices, gram_adasum(): chunks = lax.all_to_all(flat, 'dp', 0, 0, tiled=True)  17.5 us
    ppermute x1, waiting for transfers between devices, from_behind(): return lax.ppermute(x, axis, pairs)  14.6 us
  transfers between devices with their start and end apart: 2, of which 2 were waited for; matrix products, arithmetic and copies ran while one was open for 1% of the time, Pallas kernels for 0%

profile of v1, /device:TPU:6, one launch (start us, length us, event | category | flops | bytes accessed | tf_op | source)
XLA Modules:
  0.0 352.2 jit_solution(4884689482944939448)
XLA Ops:
  0.7 1.8 fusion.13
  2.5 1.8 fusion.31
  4.3 1.9 fusion
  6.2 0.5 fusion.1
  6.7 0.5 copy-done.3
  7.2 1.6 all_to_all.11
  8.8 18.7 %all-to-all-start = ((f32[64,1,2560]{2,1,0:T(1,128)}), f32[64,1,2560]{2,1,0:T(1,128)S(1)}, u32[]{:S(2)}, u32[]{:S(2)}) async-start(f32[64,1,2560]{2,1,0:T(1,128)} %all_to_all.11), calls=%async_computation | async-start | bytes 1310720 | tf_op jit(solution)/shard_map/all_to_all | solution.py:79
  27.5 0.7 fusion.7
  28.2 1.9 fusion.20
  30.1 1.9 collective-permute-start
  32.8 14.6 %collective-permute-done = bf16[1,128,5120]{2,1,0:T(8,128)(2,1)S(1)} collective-permute-done((bf16[1,128,5120]{2,1,0:T(8,128)(2,1)}, bf16[1,128,5120]{2,1,0:T(8,128)(2,1)S(1)}, u32[]{:S(2)}, u32[]{:S(2)}) %collective-permute-start) | collective-permute-done | bytes 1310752 | tf_op jit(solution)/shard_map/ppermute | solution.py:15
  47.5 17.5 %all-to-all-done = f32[64,1,2560]{2,1,0:T(1,128)S(1)} async-done(((f32[64,1,2560]{2,1,0:T(1,128)}), f32[64,1,2560]{2,1,0:T(1,128)S(1)}, u32[]{:S(2)}, u32[]{:S(2)}) %all-to-all-start) | async-done | bytes 655392 | tf_op jit(solution)/shard_map/all_to_all | solution.py:79
  64.9 0.7 fusion.39
  65.7 274.8 %psum.7 = f32[2,64,64]{1,2,0:T(8,128)S(1)} all-reduce(f32[2,64,64]{1,2,0:T(8,128)S(1)} %broadcast_select_fusion), channel_id=1, replica_groups=mesh['section'=8,'dp'=64] {'dp'}, use_global_device_ids=true, to_apply=%region_2.3 | all-reduce | flops 8192 | bytes 65536 | tf_op jit(solution)/shard_map/psum | solution.py:85
  340.5 0.2 multiply_reduce_fusion.10
  340.7 0.1 reduce_sum.178
  341.3 0.1 mul.672
  342.1 0.2 multiply_add_fusion.6
  342.3 0.2 rev.38
  342.7 0.2 multiply_reduce_fusion.8
  342.9 0.1 reshape_broadcast_in_dim.19
  343.6 0.2 fusion.50
  344.0 0.2 multiply_reduce_fusion.6
  345.3 0.2 multiply_add_fusion.3
  345.6 0.2 multiply_reduce_fusion.4
  347.2 0.2 multiply_add_fusion.1
  347.6 0.2 multiply_reduce_fusion.2
  349.3 0.2 fusion.49
  349.7 0.2 multiply_reduce_fusion
  350.4 0.1 fusion.41
  350.5 0.6 convert_element_type.85
  351.1 1.1 copy.181
  (135 shorter events, 7.4 us)
Async XLA Ops:
  0.6 3.6 %copy-start = (bf16[1,16,5120]{2,1,0:T(8,128)(2,1)S(1)}, bf16[1,16,5120]{2,1,0:T(8,128)(2,1)}, u32[]{:S(2)}) copy-start(bf16[1,16,5120]{2,1,0:T(8,128)(2,1)} %param.8) | copy-start | bytes 491524
  0.6 3.6 %copy-start.1 = (bf16[1,128,5120]{2,1,0:T(8,128)(2,1)S(1)}, bf16[1,128,5120]{2,1,0:T(8,128)(2,1)}, u32[]{:S(2)}) copy-start(bf16[1,128,5120]{2,1,0:T(8,128)(2,1)} %param.5) | copy-start | bytes 3932164
  0.7 3.6 %copy-start.2 = (bf16[1,128,5120]{2,1,0:T(8,128)(2,1)S(1)}, bf16[1,128,5120]{2,1,0:T(8,128)(2,1)}, u32[]{:S(2)}) copy-start(bf16[1,128,5120]{2,1,0:T(8,128)(2,1)} %param.6) | copy-start | bytes 3932164
  0.7 3.6 %copy-start.4 = (f32[1,5120]{1,0:T(1,128)S(1)}, f32[1,5120]{1,0:T(1,128)}, u32[]{:S(2)}) copy-start(f32[1,5120]{1,0:T(1,128)} %param.7) | copy-start | bytes 61444
  6.2 1.0 copy-start.3
  8.8 56.1 %all-to-all-start = ((f32[64,1,2560]{2,1,0:T(1,128)}), f32[64,1,2560]{2,1,0:T(1,128)S(1)}, u32[]{:S(2)}, u32[]{:S(2)}) async-start(f32[64,1,2560]{2,1,0:T(1,128)} %all_to_all.11), calls=%async_computation | async-start | bytes 1310720 | tf_op jit(solution)/shard_map/all_to_all | solution.py:79
  30.1 17.3 %collective-permute-start = (bf16[1,128,5120]{2,1,0:T(8,128)(2,1)}, bf16[1,128,5120]{2,1,0:T(8,128)(2,1)S(1)}, u32[]{:S(2)}, u32[]{:S(2)}) collective-permute-start(bf16[1,128,5120]{2,1,0:T(8,128)(2,1)} %fusion.20), channel_id=1, source_target_pairs={{64,0},{128,64},{192,128},{256,192},{320,256},{384,320},{448,384},... | collective-permute-start | bytes 3932168 | tf_op jit(solution)/shard_map/ppermute | solution.py:15

commit v2 on v1

--- a/solution.py
+++ b/solution.py
@@ -81,8 +81,8 @@
     per_tensor = devices // tensors
     mine = me // per_tensor
     partial = jnp.dot(chunks, chunks.T, precision=HIGH, preferred_element_type=jnp.float32)
-    slot = (jnp.arange(tensors) == mine)[:, None, None]
-    gram = lax.psum(jnp.where(slot, partial[None], 0.0), "dp")
+    partials = lax.all_gather(partial, "dp", axis=0, tiled=False)
+    gram = jnp.sum(partials.reshape((tensors, per_tensor) + partial.shape), axis=1)
     coef = coefficient_tree(gram)
     own_coef = jnp.sum(jnp.where((jnp.arange(tensors) == mine)[:, None], coef, 0.0), axis=0)
     combined = jnp.sum(own_coef[:, None] * chunks, axis=0)

time: 352 us -> 229 us (0.65)
  blocking collectives: 275 us -> 0 us
  waiting for transfers between devices: 32.1 us -> 166 us
  between operations: 1.28 us -> 14.7 us
    psum x1 -> x0, blocking collectives: 275 us -> none  [gram_adasum(): gram = lax.psum(jnp.where(slot, partial[None], 0.0), 'dp')]
    all_gather x0 -> x1, waiting for transfers between devices: none -> 133 us  [gram_adasum(): partials = lax.all_gather(partial, 'dp', axis=0, tiled=False)]
    all_to_all x1, waiting for transfers between devices: 17.5 us -> 32.8 us  [gram_adasum(): chunks = lax.all_to_all(flat, 'dp', 0, 0, tiled=True)]
    ppermute x1, waiting for transfers between devices: 14.6 us -> 0.01 us  [from_behind(): return lax.ppermute(x, axis, pairs)]
  transfers between devices with their start and end apart: 2 -> 3, of which waited for: 2 -> 2; matrix products, arithmetic and copies ran while one was open for 1% -> 2% of each run, Pallas kernels for 0% -> 0%
where the time goes in v2:
time: 229 us; the launch traced here: 228 us
  waiting for transfers between devices  166 us (72%)
  starting transfers between devices  20.7 us (9%)
  between operations  14.7 us (6%)
  local copies, waits for them, and re-layouts  9.89 us (4%)
  other arithmetic  8.86 us (4%)
  matrix products  8.57 us (4%)
    all_gather x1, waiting for transfers between devices, gram_adasum(): partials = lax.all_gather(partial, 'dp', axis=0, tiled=False)  133 us
    all_to_all x1, waiting for transfers between devices, gram_adasum(): chunks = lax.all_to_all(flat, 'dp', 0, 0, tiled=True)  32.8 us
    all_to_all x1, starting transfers between devices, gram_adasum(): chunks = lax.all_to_all(flat, 'dp', 0, 0, tiled=True)  18.7 us
  transfers between devices with their start and end apart: 3, of which 2 were waited for; matrix products, arithmetic and copies ran while one was open for 2% of the time, Pallas kernels for 0%

profile of v2, /device:TPU:6, one launch (start us, length us, event | category | flops | bytes accessed | tf_op | source)
XLA Modules:
  0.0 228.3 jit_solution(2665588504793614964)
XLA Ops:
  7.2 1.8 fusion.13
  9.0 1.8 fusion.31
  10.8 1.2 fusion.1
  12.0 1.9 fusion
  13.9 1.1 pad_maximum_fusion
  15.0 1.6 all_to_all.11
  16.6 18.7 %all-to-all-start = ((f32[64,1,2560]{2,1,0:T(1,128)}), f32[64,1,2560]{2,1,0:T(1,128)S(1)}, u32[]{:S(2)}, u32[]{:S(2)}) async-start(f32[64,1,2560]{2,1,0:T(1,128)} %all_to_all.11), calls=%async_computation | async-start | bytes 1310720 | tf_op jit(solution)/shard_map/all_to_all | solution.py:79
  35.4 0.7 fusion.7
  36.1 1.9 fusion.20
  38.0 1.9 collective-permute-start
  39.9 32.8 %all-to-all-done = f32[64,1,2560]{2,1,0:T(1,128)S(1)} async-done(((f32[64,1,2560]{2,1,0:T(1,128)}), f32[64,1,2560]{2,1,0:T(1,128)S(1)}, u32[]{:S(2)}, u32[]{:S(2)}) %all-to-all-start) | async-done | bytes 655392 | tf_op jit(solution)/shard_map/all_to_all | solution.py:79
  72.7 1.3 fusion.39
  74.8 132.8 %all-gather.3.cloned.1.call-done = f32[4096,64]{1,0:T(8,128)} async-done(((f32[64,64]{1,0:T(8,128)}), f32[4096,64]{1,0:T(8,128)}) %all-gather.3.cloned.1.call-update) | async-done | bytes 1048592 | tf_op jit(solution)/shard_map/all_gather | solution.py:84
  207.6 1.8 reduce_sum.185
  209.3 0.3 multiply_reduce_fusion.10
  211.0 0.1 mul.672
  211.2 0.1 reduce_sum.188
  211.8 0.2 multiply_add_fusion.6
  212.0 0.2 rev.38
  212.3 0.3 multiply_reduce_fusion.8
  213.0 0.1 reshape_broadcast_in_dim.19
  214.2 0.2 fusion.50
  214.5 0.3 multiply_reduce_fusion.6
  216.0 0.2 multiply_add_fusion.3
  216.3 0.3 multiply_reduce_fusion.4
  217.4 0.2 multiply_add_fusion.1
  217.7 0.3 multiply_reduce_fusion.2
  218.6 0.2 fusion.49
  218.9 0.3 multiply_reduce_fusion
  219.7 0.1 fusion.41
  219.8 0.6 convert_element_type.85
  220.4 1.1 copy.193
  (135 shorter events, 7.3 us)
Async XLA Ops:
  7.2 4.9 %copy-start = (bf16[1,16,5120]{2,1,0:T(8,128)(2,1)S(1)}, bf16[1,16,5120]{2,1,0:T(8,128)(2,1)}, u32[]{:S(2)}) copy-start(bf16[1,16,5120]{2,1,0:T(8,128)(2,1)} %param.8) | copy-start | bytes 491524
  7.2 3.6 %copy-start.1 = (bf16[1,128,5120]{2,1,0:T(8,128)(2,1)S(1)}, bf16[1,128,5120]{2,1,0:T(8,128)(2,1)}, u32[]{:S(2)}) copy-start(bf16[1,128,5120]{2,1,0:T(8,128)(2,1)} %param.5) | copy-start | bytes 3932164
  7.2 4.8 %copy-start.2 = (bf16[1,128,5120]{2,1,0:T(8,128)(2,1)S(1)}, bf16[1,128,5120]{2,1,0:T(8,128)(2,1)}, u32[]{:S(2)}) copy-start(bf16[1,128,5120]{2,1,0:T(8,128)(2,1)} %param.6) | copy-start | bytes 3932164
  7.2 3.6 %copy-start.3 = (f32[1,5120]{1,0:T(1,128)S(1)}, f32[1,5120]{1,0:T(1,128)}, u32[]{:S(2)}) copy-start(f32[1,5120]{1,0:T(1,128)} %param.7) | copy-start | bytes 61444
  16.6 56.1 %all-to-all-start = ((f32[64,1,2560]{2,1,0:T(1,128)}), f32[64,1,2560]{2,1,0:T(1,128)S(1)}, u32[]{:S(2)}, u32[]{:S(2)}) async-start(f32[64,1,2560]{2,1,0:T(1,128)} %all_to_all.11), calls=%async_computation | async-start | bytes 1310720 | tf_op jit(solution)/shard_map/all_to_all | solution.py:79
  35.3 172.2 %all-gather.3.cloned.1.call-start = ((), (), s32[]{:S(2)}) async-start(), calls=%async_computation.1 | async-start | bytes 2129920 | tf_op jit(solution)/shard_map/all_gather | solution.py:84
  38.0 36.9 %collective-permute-start = (bf16[1,128,5120]{2,1,0:T(8,128)(2,1)}, bf16[1,128,5120]{2,1,0:T(8,128)(2,1)S(1)}, u32[]{:S(2)}, u32[]{:S(2)}) collective-permute-start(bf16[1,128,5120]{2,1,0:T(8,128)(2,1)} %fusion.20), channel_id=1, source_target_pairs={{64,0},{128,64},{192,128},{256,192},{320,256},{384,320},{448,384},... | collective-permute-start | bytes 3932168 | tf_op jit(solution)/shard_map/ppermute | solution.py:15
Sparse Core Ops, SparseCore 0:
  74.2 133.3 all-gather.2

commit v3 on v2

--- a/solution.py
+++ b/solution.py
@@ -7,6 +7,12 @@
 pair_eps = 1e-06
 adapter_scale = 2.0
 HIGH = lax.Precision.HIGHEST
+
+
+def swapped(value, axis, bit):
+    mask = 2**bit
+    pairs = [(source, source ^ mask) for source in range(lax.axis_size(axis))]
+    return lax.ppermute(value, axis, pairs)
 
 
 def from_behind(x, axis, by):
@@ -81,8 +87,11 @@
     per_tensor = devices // tensors
     mine = me // per_tensor
     partial = jnp.dot(chunks, chunks.T, precision=HIGH, preferred_element_type=jnp.float32)
-    partials = lax.all_gather(partial, "dp", axis=0, tiled=False)
-    gram = jnp.sum(partials.reshape((tensors, per_tensor) + partial.shape), axis=1)
+    half_bits = per_tensor.bit_length() - 1
+    for level_bit in range(half_bits):
+        partial = partial + swapped(partial, "dp", level_bit)
+    other = swapped(partial, "dp", half_bits)
+    gram = jnp.where(mine == 0, jnp.stack([partial, other]), jnp.stack([other, partial]))
     coef = coefficient_tree(gram)
     own_coef = jnp.sum(jnp.where((jnp.arange(tensors) == mine)[:, None], coef, 0.0), axis=0)
     combined = jnp.sum(own_coef[:, None] * chunks, axis=0)

time: 229 us -> 129 us (0.56)
  waiting for transfers between devices: 166 us -> 59 us
  starting transfers between devices: 20.7 us -> 43.5 us
  between operations: 14.7 us -> 1.33 us
  other arithmetic: 8.86 us -> 6.08 us
    all_gather x1 -> x0, waiting for transfers between devices: 133 us -> none  [gram_adasum(): partials = lax.all_gather(partial, 'dp', axis=0, tiled=False)]
    ppermute x0 -> x6, waiting for transfers between devices: none -> 26.5 us  [swapped(): return lax.ppermute(value, axis, pairs)]
    ppermute x0 -> x6, starting transfers between devices: none -> 22.9 us  [swapped(): return lax.ppermute(value, axis, pairs)]
  transfers between devices with their start and end apart: 3 -> 8, of which waited for: 2 -> 7; matrix products, arithmetic and copies ran while one was open for 2% -> 3% of each run, Pallas kernels for 0% -> 0%
where the time goes in v3:
time: 129 us; the launch traced here: 128 us
  waiting for transfers between devices  59 us (46%)
  starting transfers between devices  43.5 us (34%)
  local copies, waits for them, and re-layouts  10.4 us (8%)
  matrix products  7.3 us (6%)
  other arithmetic  6.08 us (5%)
  between operations  1.33 us (1%)
    all_to_all x1, waiting for transfers between devices, gram_adasum(): chunks = lax.all_to_all(flat, 'dp', 0, 0, tiled=True)  32.5 us
    ppermute x6, waiting for transfers between devices, swapped(): return lax.ppermute(value, axis, pairs)  26.5 us
    ppermute x6, starting transfers between devices, swapped(): return lax.ppermute(value, axis, pairs)  22.9 us
    all_to_all x1, starting transfers between devices, gram_adasum(): chunks = lax.all_to_all(flat, 'dp', 0, 0, tiled=True)  18.7 us
  transfers between devices with their start and end apart: 8, of which 7 were waited for; matrix products, arithmetic and copies ran while one was open for 3% of the time, Pallas kernels for 0%

profile of v3, /device:TPU:6, one launch (start us, length us, event | category | flops | bytes accessed | tf_op | source)
XLA Modules:
  0.0 127.6 jit_solution(896125882157038928)
XLA Ops:
  0.7 1.8 %fusion.13 = f32[128]{0:T(128)S(1)} fusion(bf16[1,128,5120]{2,1,0:T(8,128)(2,1)} %param.5), kind=kLoop, calls=%fused_computation.18 | loop fusion | flops 1965952 | bytes 1311232 | tf_op jit(solution)/shard_map/reduce_sum | solution.py:26
  2.5 1.8 %fusion.31 = bf16[128,16]{0,1:T(8,128)(2,1)S(1)} fusion(bf16[1,128,5120]{2,1,0:T(8,128)(2,1)} %param.6, bf16[1,16,5120]{2,1,0:T(8,128)(2,1)} %param.9), kind=kOutput, calls=%fused_computation.32 | convolution fusion | flops 20975616 | bytes 1478656 | tf_op jit(solution)/shard_map/sh,gh->sg/dot_general | solution.py:42
  4.3 1.9 %fusion = f32[1,16,5120]{2,1,0:T(8,128)} fusion(bf16[1,128,5120]{2,1,0:T(8,128)(2,1)S(1)} %copy-done.2, bf16[1,128,5120]{2,1,0:T(8,128)(2,1)S(1)} %copy-done.1, f32[5120]{0:T(1024)S(1)} %bitcast.188, f32[128]{0:T(128)S(1)} %add_rsqrt_fusion, bf16[1,16,5120]{2,1,0:T(8,128)(2,1)S(1)} %copy-done), kind=kOutput, calls=%fused_computation.2 | convolution fusion | flops 44648448 | bytes 3133952 | tf_op jit(solution)/shard_map/tk,td->kd/dot_general | solution.py:35
  6.2 0.5 fusion.1
  6.7 0.5 copy-done.3
  7.2 1.6 %all_to_all.11 = f32[64,1,2560]{2,1,0:T(1,128)} reshape(f32[2,16,5120]{2,1,0:T(8,128)S(1)} %pad_maximum_fusion) | data formatting | bytes 1310720 | tf_op jit(solution)/shard_map/all_to_all | solution.py:85
  8.8 18.7 %all-to-all-start = ((f32[64,1,2560]{2,1,0:T(1,128)}), f32[64,1,2560]{2,1,0:T(1,128)S(1)}, u32[]{:S(2)}, u32[]{:S(2)}) async-start(f32[64,1,2560]{2,1,0:T(1,128)} %all_to_all.11), calls=%async_computation | async-start | bytes 1310720 | tf_op jit(solution)/shard_map/all_to_all | solution.py:85
  27.5 0.7 fusion.7
  28.2 1.9 %fusion.20 = bf16[1,128,5120]{2,1,0:T(8,128)(2,1)} fusion(f32[128,5120]{1,0:T(8,128)S(1)} %get-tuple-element.62, bf16[1,128,5120]{2,1,0:T(8,128)(2,1)S(1)} %copy-done.1, bf16[1,128,5120]{2,1,0:T(8,128)(2,1)S(1)} %copy-done.2, f32[128]{0:T(128)S(1)} %broadcast_multiply_fusion, f32[128]{0:T(128)S(1)} %add_rsqrt_fusion), kind=kLoop, calls=%fused_computation.23 | loop fusion | flops 5242880 | bytes 6554624 | tf_op jit(solution)/shard_map/broadcast_in_dim | solution.py:109
  30.1 1.9 %collective-permute-start = (bf16[1,128,5120]{2,1,0:T(8,128)(2,1)}, bf16[1,128,5120]{2,1,0:T(8,128)(2,1)S(1)}, u32[]{:S(2)}, u32[]{:S(2)}) collective-permute-start(bf16[1,128,5120]{2,1,0:T(8,128)(2,1)} %fusion.20), channel_id=1, source_target_pairs={{64,0},{128,64},{192,128},{256,192},{320,256},{384,320},{448,384},... | collective-permute-start | bytes 3932168 | tf_op jit(solution)/shard_map/ppermute | solution.py:21
  32.4 32.5 %all-to-all-done = f32[64,1,2560]{2,1,0:T(1,128)S(1)} async-done(((f32[64,1,2560]{2,1,0:T(1,128)}), f32[64,1,2560]{2,1,0:T(1,128)S(1)}, u32[]{:S(2)}, u32[]{:S(2)}) %all-to-all-start) | async-done | bytes 655392 | tf_op jit(solution)/shard_map/all_to_all | solution.py:85
  64.9 0.7 fusion.39
  65.6 2.8 %collective-permute-start.1 = (f32[64,64]{1,0:T(8,128)S(1)}, f32[64,64]{1,0:T(8,128)S(1)}, u32[]{:S(2)}, u32[]{:S(2)}) collective-permute-start(f32[64,64]{1,0:T(8,128)S(1)} %fusion.39), channel_id=1, source_target_pairs={{0,1},{1,0},{2,3},{3,2},{4,5},{5,4},{6,7},{7,6},{8,9},{9,8},{10,11... | collective-permute-start | bytes 49160 | tf_op jit(solution)/shard_map/ppermute | solution.py:15
  68.5 3.0 %collective-permute-done.1 = f32[64,64]{1,0:T(8,128)S(1)} collective-permute-done((f32[64,64]{1,0:T(8,128)S(1)}, f32[64,64]{1,0:T(8,128)S(1)}, u32[]{:S(2)}, u32[]{:S(2)}) %collective-permute-start.1) | collective-permute-done | bytes 16416 | tf_op jit(solution)/shard_map/ppermute | solution.py:15
  71.4 3.3 %collective-permute-start.2 = (f32[64,64]{1,0:T(8,128)S(1)}, f32[64,64]{1,0:T(8,128)S(1)}, u32[]{:S(2)}, u32[]{:S(2)}) collective-permute-start(f32[64,64]{1,0:T(8,128)S(1)} %add.328), channel_id=1, source_target_pairs={{0,2},{1,3},{2,0},{3,1},{4,6},{5,7},{6,4},{7,5},{8,10},{9,11},{10,... | collective-permute-start | bytes 49160 | tf_op jit(solution)/shard_map/ppermute | solution.py:15
  74.8 3.3 %collective-permute-done.2 = f32[64,64]{1,0:T(8,128)S(1)} collective-permute-done((f32[64,64]{1,0:T(8,128)S(1)}, f32[64,64]{1,0:T(8,128)S(1)}, u32[]{:S(2)}, u32[]{:S(2)}) %collective-permute-start.2) | collective-permute-done | bytes 16416 | tf_op jit(solution)/shard_map/ppermute | solution.py:15
  78.1 3.2 %collective-permute-start.3 = (f32[64,64]{1,0:T(8,128)S(1)}, f32[64,64]{1,0:T(8,128)S(1)}, u32[]{:S(2)}, u32[]{:S(2)}) collective-permute-start(f32[64,64]{1,0:T(8,128)S(1)} %add.329), channel_id=1, source_target_pairs={{0,4},{1,5},{2,6},{3,7},{4,0},{5,1},{6,2},{7,3},{8,12},{9,13},{10,... | collective-permute-start | bytes 49160 | tf_op jit(solution)/shard_map/ppermute | solution.py:15
  81.3 6.5 %collective-permute-done.3 = f32[64,64]{1,0:T(8,128)S(1)} collective-permute-done((f32[64,64]{1,0:T(8,128)S(1)}, f32[64,64]{1,0:T(8,128)S(1)}, u32[]{:S(2)}, u32[]{:S(2)}) %collective-permute-start.3) | collective-permute-done | bytes 16416 | tf_op jit(solution)/shard_map/ppermute | solution.py:15
  87.8 5.4 %collective-permute-start.4 = (f32[64,64]{1,0:T(8,128)S(1)}, f32[64,64]{1,0:T(8,128)S(1)}, u32[]{:S(2)}, u32[]{:S(2)}) collective-permute-start(f32[64,64]{1,0:T(8,128)S(1)} %add.330), channel_id=1, source_target_pairs={{0,8},{1,9},{2,10},{3,11},{4,12},{5,13},{6,14},{7,15},{8,0},{9,1},... | collective-permute-start | bytes 49160 | tf_op jit(solution)/shard_map/ppermute | solution.py:15
  93.3 9.0 %collective-permute-done.4 = f32[64,64]{1,0:T(8,128)S(1)} collective-permute-done((f32[64,64]{1,0:T(8,128)S(1)}, f32[64,64]{1,0:T(8,128)S(1)}, u32[]{:S(2)}, u32[]{:S(2)}) %collective-permute-start.4) | collective-permute-done | bytes 16416 | tf_op jit(solution)/shard_map/ppermute | solution.py:15
  102.3 3.3 %collective-permute-start.5 = (f32[64,64]{1,0:T(8,128)S(1)}, f32[64,64]{1,0:T(8,128)S(1)}, u32[]{:S(2)}, u32[]{:S(2)}) collective-permute-start(f32[64,64]{1,0:T(8,128)S(1)} %add.331), channel_id=1, source_target_pairs={{0,16},{1,17},{2,18},{3,19},{4,20},{5,21},{6,22},{7,23},{8,24},{9,... | collective-permute-start | bytes 49160 | tf_op jit(solution)/shard_map/ppermute | solution.py:15
  105.7 2.5 %collective-permute-done.5 = f32[64,64]{1,0:T(8,128)S(1)} collective-permute-done((f32[64,64]{1,0:T(8,128)S(1)}, f32[64,64]{1,0:T(8,128)S(1)}, u32[]{:S(2)}, u32[]{:S(2)}) %collective-permute-start.5) | collective-permute-done | bytes 16416 | tf_op jit(solution)/shard_map/ppermute | solution.py:15
  108.2 4.9 %collective-permute-start.6 = (f32[64,64]{1,0:T(8,128)S(1)}, f32[64,64]{1,0:T(8,128)S(1)}, u32[]{:S(2)}, u32[]{:S(2)}) collective-permute-start(f32[64,64]{1,0:T(8,128)S(1)} %add.332), channel_id=1, source_target_pairs={{0,32},{1,33},{2,34},{3,35},{4,36},{5,37},{6,38},{7,39},{8,40},{9,... | collective-permute-start | bytes 49160 | tf_op jit(solution)/shard_map/ppermute | solution.py:15
  113.2 2.2 %collective-permute-done.6 = f32[64,64]{1,0:T(8,128)S(1)} collective-permute-done((f32[64,64]{1,0:T(8,128)S(1)}, f32[64,64]{1,0:T(8,128)S(1)}, u32[]{:S(2)}, u32[]{:S(2)}) %collective-permute-start.6) | collective-permute-done | bytes 16416 | tf_op jit(solution)/shard_map/ppermute | solution.py:15
  115.5 0.3 multiply_reduce_fusion.10
  117.7 0.3 multiply_reduce_fusion.8
  119.1 0.3 multiply_reduce_fusion.6
  120.8 0.3 multiply_reduce_fusion.4
  122.8 0.3 multiply_reduce_fusion.2
  125.1 0.3 multiply_reduce_fusion
  126.0 0.6 convert_element_type.85
  126.6 1.1 copy.211
  (150 shorter events, 9.0 us)
Async XLA Ops:
  0.6 3.6 %copy-start = (bf16[1,16,5120]{2,1,0:T(8,128)(2,1)S(1)}, bf16[1,16,5120]{2,1,0:T(8,128)(2,1)}, u32[]{:S(2)}) copy-start(bf16[1,16,5120]{2,1,0:T(8,128)(2,1)} %param.8) | copy-start | bytes 491524
  0.6 3.6 %copy-start.1 = (bf16[1,128,5120]{2,1,0:T(8,128)(2,1)S(1)}, bf16[1,128,5120]{2,1,0:T(8,128)(2,1)}, u32[]{:S(2)}) copy-start(bf16[1,128,5120]{2,1,0:T(8,128)(2,1)} %param.5) | copy-start | bytes 3932164
  0.7 3.6 %copy-start.2 = (bf16[1,128,5120]{2,1,0:T(8,128)(2,1)S(1)}, bf16[1,128,5120]{2,1,0:T(8,128)(2,1)}, u32[]{:S(2)}) copy-start(bf16[1,128,5120]{2,1,0:T(8,128)(2,1)} %param.6) | copy-start | bytes 3932164
  0.7 3.6 %copy-start.4 = (f32[1,5120]{1,0:T(1,128)S(1)}, f32[1,5120]{1,0:T(1,128)}, u32[]{:S(2)}) copy-start(f32[1,5120]{1,0:T(1,128)} %param.7) | copy-start | bytes 61444
  6.2 1.0 copy-start.3
  8.8 56.1 %all-to-all-start = ((f32[64,1,2560]{2,1,0:T(1,128)}), f32[64,1,2560]{2,1,0:T(1,128)S(1)}, u32[]{:S(2)}, u32[]{:S(2)}) async-start(f32[64,1,2560]{2,1,0:T(1,128)} %all_to_all.11), calls=%async_computation | async-start | bytes 1310720 | tf_op jit(solution)/shard_map/all_to_all | solution.py:85
  30.1 83.1 %collective-permute-start = (bf16[1,128,5120]{2,1,0:T(8,128)(2,1)}, bf16[1,128,5120]{2,1,0:T(8,128)(2,1)S(1)}, u32[]{:S(2)}, u32[]{:S(2)}) collective-permute-start(bf16[1,128,5120]{2,1,0:T(8,128)(2,1)} %fusion.20), channel_id=1, source_target_pairs={{64,0},{128,64},{192,128},{256,192},{320,256},{384,320},{448,384},... | collective-permute-start | bytes 3932168 | tf_op jit(solution)/shard_map/ppermute | solution.py:21
  65.6 5.8 %collective-permute-start.1 = (f32[64,64]{1,0:T(8,128)S(1)}, f32[64,64]{1,0:T(8,128)S(1)}, u32[]{:S(2)}, u32[]{:S(2)}) collective-permute-start(f32[64,64]{1,0:T(8,128)S(1)} %fusion.39), channel_id=1, source_target_pairs={{0,1},{1,0},{2,3},{3,2},{4,5},{5,4},{6,7},{7,6},{8,9},{9,8},{10,11... | collective-permute-start | bytes 49160 | tf_op jit(solution)/shard_map/ppermute | solution.py:15
  71.4 6.7 %collective-permute-start.2 = (f32[64,64]{1,0:T(8,128)S(1)}, f32[64,64]{1,0:T(8,128)S(1)}, u32[]{:S(2)}, u32[]{:S(2)}) collective-permute-start(f32[64,64]{1,0:T(8,128)S(1)} %add.328), channel_id=1, source_target_pairs={{0,2},{1,3},{2,0},{3,1},{4,6},{5,7},{6,4},{7,5},{8,10},{9,11},{10,... | collective-permute-start | bytes 49160 | tf_op jit(solution)/shard_map/ppermute | solution.py:15
  78.1 9.7 %collective-permute-start.3 = (f32[64,64]{1,0:T(8,128)S(1)}, f32[64,64]{1,0:T(8,128)S(1)}, u32[]{:S(2)}, u32[]{:S(2)}) collective-permute-start(f32[64,64]{1,0:T(8,128)S(1)} %add.329), channel_id=1, source_target_pairs={{0,4},{1,5},{2,6},{3,7},{4,0},{5,1},{6,2},{7,3},{8,12},{9,13},{10,... | collective-permute-start | bytes 49160 | tf_op jit(solution)/shard_map/ppermute | solution.py:15
  87.8 14.5 %collective-permute-start.4 = (f32[64,64]{1,0:T(8,128)S(1)}, f32[64,64]{1,0:T(8,128)S(1)}, u32[]{:S(2)}, u32[]{:S(2)}) collective-permute-start(f32[64,64]{1,0:T(8,128)S(1)} %add.330), channel_id=1, source_target_pairs={{0,8},{1,9},{2,10},{3,11},{4,12},{5,13},{6,14},{7,15},{8,0},{9,1},... | collective-permute-start | bytes 49160 | tf_op jit(solution)/shard_map/ppermute | solution.py:15
  102.3 5.8 %collective-permute-start.5 = (f32[64,64]{1,0:T(8,128)S(1)}, f32[64,64]{1,0:T(8,128)S(1)}, u32[]{:S(2)}, u32[]{:S(2)}) collective-permute-start(f32[64,64]{1,0:T(8,128)S(1)} %add.331), channel_id=1, source_target_pairs={{0,16},{1,17},{2,18},{3,19},{4,20},{5,21},{6,22},{7,23},{8,24},{9,... | collective-permute-start | bytes 49160 | tf_op jit(solution)/shard_map/ppermute | solution.py:15
  108.2 7.3 %collective-permute-start.6 = (f32[64,64]{1,0:T(8,128)S(1)}, f32[64,64]{1,0:T(8,128)S(1)}, u32[]{:S(2)}, u32[]{:S(2)}) collective-permute-start(f32[64,64]{1,0:T(8,128)S(1)} %add.332), channel_id=1, source_target_pairs={{0,32},{1,33},{2,34},{3,35},{4,36},{5,37},{6,38},{7,39},{8,40},{9,... | collective-permute-start | bytes 49160 | tf_op jit(solution)/shard_map/ppermute | solution.py:15

commit v4 on v3

--- a/solution.py
+++ b/solution.py
@@ -87,11 +87,11 @@
     per_tensor = devices // tensors
     mine = me // per_tensor
     partial = jnp.dot(chunks, chunks.T, precision=HIGH, preferred_element_type=jnp.float32)
-    half_bits = per_tensor.bit_length() - 1
-    for level_bit in range(half_bits):
-        partial = partial + swapped(partial, "dp", level_bit)
-    other = swapped(partial, "dp", half_bits)
-    gram = jnp.where(mine == 0, jnp.stack([partial, other]), jnp.stack([other, partial]))
+    rows = lax.all_to_all(partial[:, None, :], "dp", 0, 0, tiled=True)
+    rows = jnp.sum(rows.reshape(tensors, per_tensor, partial.shape[1]), axis=1)
+    spread = jnp.broadcast_to(rows[None], (devices, tensors, partial.shape[1]))
+    gathered = lax.all_to_all(spread, "dp", 0, 0, tiled=True)
+    gram = jnp.swapaxes(gathered, 0, 1)
     coef = coefficient_tree(gram)
     own_coef = jnp.sum(jnp.where((jnp.arange(tensors) == mine)[:, None], coef, 0.0), axis=0)
     combined = jnp.sum(own_coef[:, None] * chunks, axis=0)

time: 129 us -> 120 us (0.930)
  starting transfers between devices: 43.5 us -> 31.9 us
  waiting for transfers between devices: 59 us -> 60.6 us
  local copies, waits for them, and re-layouts: 10.4 us -> 11.8 us
    all_to_all x0 -> x2, waiting for transfers between devices: none -> 28.1 us  [the longest x1 14.2 us: gram_adasum(): rows = lax.all_to_all(partial[:, None, :], 'dp', 0, 0, tiled=True)]
    ppermute x6 -> x0, waiting for transfers between devices: 26.5 us -> none  [swapped(): return lax.ppermute(value, axis, pairs)]
    ppermute x6 -> x0, starting transfers between devices: 22.9 us -> none  [swapped(): return lax.ppermute(value, axis, pairs)]
    all_to_all x0 -> x2, starting transfers between devices: none -> 11.3 us  [the longest x1 6.46 us: gram_adasum(): rows = lax.all_to_all(partial[:, None, :], 'dp', 0, 0, tiled=True)]
  transfers between devices with their start and end apart: 8 -> 4, of which waited for: 7 -> 3; matrix products, arithmetic and copies ran while one was open for 3% -> 4% of each run, Pallas kernels for 0% -> 0%
where the time goes in v4:
time: 120 us
  waiting for transfers between devices  60.6 us (50%)
  starting transfers between devices  31.9 us (27%)
  local copies, waits for them, and re-layouts  11.8 us (10%)
  matrix products  7.38 us (6%)
  other arithmetic  6.8 us (6%)
  between operations  1.3 us (1%)
    all_to_all x1, waiting for transfers between devices, gram_adasum(): chunks = lax.all_to_all(flat, 'dp', 0, 0, tiled=True)  32.4 us
    all_to_all x1, starting transfers between devices, gram_adasum(): chunks = lax.all_to_all(flat, 'dp', 0, 0, tiled=True)  18.7 us
    all_to_all x1, waiting for transfers between devices, gram_adasum(): rows = lax.all_to_all(partial[:, None, :], 'dp', 0, 0, tiled=True)  14.2 us
    all_to_all x1, waiting for transfers between devices, gram_adasum(): gathered = lax.all_to_all(spread, 'dp', 0, 0, tiled=True)  13.9 us
    all_to_all x1, starting transfers between devices, gram_adasum(): rows = lax.all_to_all(partial[:, None, :], 'dp', 0, 0, tiled=True)  6.46 us
    all_to_all x1, starting transfers between devices, gram_adasum(): gathered = lax.all_to_all(spread, 'dp', 0, 0, tiled=True)  4.8 us
  transfers between devices with their start and end apart: 4, of which 3 were waited for; matrix products, arithmetic and copies ran while one was open for 4% of the time, Pallas kernels for 0%

profile of v4, /device:TPU:6, one launch (start us, length us, event | category | flops | bytes accessed | tf_op | source)
XLA Modules:
  0.0 119.7 jit_solution(9060837857221892156)
XLA Ops:
  0.7 1.8 %fusion.13 = f32[128]{0:T(128)S(1)} fusion(bf16[1,128,5120]{2,1,0:T(8,128)(2,1)} %param.5), kind=kLoop, calls=%fused_computation.18 | loop fusion | flops 1965952 | bytes 1311232 | tf_op jit(solution)/shard_map/reduce_sum | solution.py:26
  2.5 1.8 %fusion.31 = bf16[128,16]{0,1:T(8,128)(2,1)S(1)} fusion(bf16[1,128,5120]{2,1,0:T(8,128)(2,1)} %param.6, bf16[1,16,5120]{2,1,0:T(8,128)(2,1)} %param.9), kind=kOutput, calls=%fused_computation.32 | convolution fusion | flops 20975616 | bytes 1478656 | tf_op jit(solution)/shard_map/sh,gh->sg/dot_general | solution.py:42
  4.3 1.9 %fusion = f32[1,16,5120]{2,1,0:T(8,128)} fusion(bf16[1,128,5120]{2,1,0:T(8,128)(2,1)S(1)} %copy-done.2, bf16[1,128,5120]{2,1,0:T(8,128)(2,1)S(1)} %copy-done.1, f32[5120]{0:T(1024)S(1)} %bitcast.206, f32[128]{0:T(128)S(1)} %add_rsqrt_fusion, bf16[1,16,5120]{2,1,0:T(8,128)(2,1)S(1)} %copy-done), kind=kOutput, calls=%fused_computation.2 | convolution fusion | flops 44648448 | bytes 3133952 | tf_op jit(solution)/shard_map/tk,td->kd/dot_general | solution.py:35
  6.2 0.5 fusion.1
  6.7 0.5 copy-done.3
  7.2 1.6 %all_to_all.19 = f32[64,1,2560]{2,1,0:T(1,128)} reshape(f32[2,16,5120]{2,1,0:T(8,128)S(1)} %pad_maximum_fusion) | data formatting | bytes 1310720 | tf_op jit(solution)/shard_map/all_to_all | solution.py:85
  8.8 18.7 %all-to-all-start = ((f32[64,1,2560]{2,1,0:T(1,128)}), f32[64,1,2560]{2,1,0:T(1,128)S(1)}, u32[]{:S(2)}, u32[]{:S(2)}) async-start(f32[64,1,2560]{2,1,0:T(1,128)} %all_to_all.19), calls=%async_computation | async-start | bytes 1310720 | tf_op jit(solution)/shard_map/all_to_all | solution.py:85
  27.5 0.7 fusion.7
  28.2 1.9 %fusion.20 = bf16[1,128,5120]{2,1,0:T(8,128)(2,1)} fusion(f32[128,5120]{1,0:T(8,128)S(1)} %get-tuple-element.62, bf16[1,128,5120]{2,1,0:T(8,128)(2,1)S(1)} %copy-done.1, bf16[1,128,5120]{2,1,0:T(8,128)(2,1)S(1)} %copy-done.2, f32[128]{0:T(128)S(1)} %broadcast_multiply_fusion, f32[128]{0:T(128)S(1)} %add_rsqrt_fusion), kind=kLoop, calls=%fused_computation.23 | loop fusion | flops 5242880 | bytes 6554624 | tf_op jit(solution)/shard_map/broadcast_in_dim | solution.py:109
  30.1 1.9 %collective-permute-start = (bf16[1,128,5120]{2,1,0:T(8,128)(2,1)}, bf16[1,128,5120]{2,1,0:T(8,128)(2,1)S(1)}, u32[]{:S(2)}, u32[]{:S(2)}) collective-permute-start(bf16[1,128,5120]{2,1,0:T(8,128)(2,1)} %fusion.20), channel_id=1, source_target_pairs={{64,0},{128,64},{192,128},{256,192},{320,256},{384,320},{448,384},... | collective-permute-start | bytes 3932168 | tf_op jit(solution)/shard_map/ppermute | solution.py:21
  32.5 32.4 %all-to-all-done = f32[64,1,2560]{2,1,0:T(1,128)S(1)} async-done(((f32[64,1,2560]{2,1,0:T(1,128)}), f32[64,1,2560]{2,1,0:T(1,128)S(1)}, u32[]{:S(2)}, u32[]{:S(2)}) %all-to-all-start) | async-done | bytes 655392 | tf_op jit(solution)/shard_map/all_to_all | solution.py:85
  64.9 1.3 %fusion.39 = f32[64,64]{1,0:T(8,128)} fusion(f32[64,1,2560]{2,1,0:T(1,128)S(1)} %all-to-all-done), kind=kOutput, calls=%fused_computation.36 | convolution fusion | flops 125829120 | bytes 671744 | tf_op jit(solution)/shard_map/dot_general | solution.py:89
  66.2 6.5 %all-to-all-start.1 = ((f32[64,1,64]{2,1,0:T(1,128)}), f32[64,1,64]{2,1,0:T(1,128)S(1)}, u32[]{:S(2)}, u32[]{:S(2)}) async-start(f32[64,1,64]{2,1,0:T(1,128)} %bitcast.10), calls=%async_computation.1 | async-start | bytes 65536 | tf_op jit(solution)/shard_map/all_to_all | solution.py:90
  72.7 14.2 %all-to-all-done.1 = f32[64,1,64]{2,1,0:T(1,128)S(1)} async-done(((f32[64,1,64]{2,1,0:T(1,128)}), f32[64,1,64]{2,1,0:T(1,128)S(1)}, u32[]{:S(2)}, u32[]{:S(2)}) %all-to-all-start.1) | async-done | bytes 16416 | tf_op jit(solution)/shard_map/all_to_all | solution.py:90
  87.0 0.7 reshape.736
  87.7 4.8 %all-to-all-start.2 = ((f32[64,1,128]{2,1,0:T(1,128)}), f32[64,1,128]{2,1,0:T(1,128)S(1)}, u32[]{:S(2)}, u32[]{:S(2)}) async-start(f32[64,1,128]{2,1,0:T(1,128)} %reshape.736), calls=%async_computation.2 | async-start | bytes 65536 | tf_op jit(solution)/shard_map/all_to_all | solution.py:93
  92.7 13.9 %all-to-all-done.2 = f32[64,1,128]{2,1,0:T(1,128)S(1)} async-done(((f32[64,1,128]{2,1,0:T(1,128)}), f32[64,1,128]{2,1,0:T(1,128)S(1)}, u32[]{:S(2)}, u32[]{:S(2)}) %all-to-all-start.2) | async-done | bytes 32800 | tf_op jit(solution)/shard_map/all_to_all | solution.py:93
  106.7 0.5 broadcast.709
  107.2 0.7 reduce.2
  108.1 0.2 multiply_reduce_fusion.10
  109.7 0.2 multiply_add_fusion.6
  110.2 0.2 multiply_reduce_fusion.8
  111.2 0.2 fusion.62
  111.5 0.2 multiply_reduce_fusion.6
  112.9 0.2 multiply_add_fusion.3
  113.2 0.2 multiply_reduce_fusion.4
  114.8 0.2 multiply_add_fusion.1
  115.1 0.2 multiply_reduce_fusion.2
  116.9 0.2 fusion.49
  117.3 0.2 multiply_reduce_fusion
  118.1 0.6 convert_element_type.85
  118.7 1.1 copy.179
  (144 shorter events, 8.2 us)
Async XLA Ops:
  0.6 3.6 %copy-start = (bf16[1,16,5120]{2,1,0:T(8,128)(2,1)S(1)}, bf16[1,16,5120]{2,1,0:T(8,128)(2,1)}, u32[]{:S(2)}) copy-start(bf16[1,16,5120]{2,1,0:T(8,128)(2,1)} %param.8) | copy-start | bytes 491524
  0.6 3.6 %copy-start.1 = (bf16[1,128,5120]{2,1,0:T(8,128)(2,1)S(1)}, bf16[1,128,5120]{2,1,0:T(8,128)(2,1)}, u32[]{:S(2)}) copy-start(bf16[1,128,5120]{2,1,0:T(8,128)(2,1)} %param.5) | copy-start | bytes 3932164
  0.7 3.6 %copy-start.2 = (bf16[1,128,5120]{2,1,0:T(8,128)(2,1)S(1)}, bf16[1,128,5120]{2,1,0:T(8,128)(2,1)}, u32[]{:S(2)}) copy-start(bf16[1,128,5120]{2,1,0:T(8,128)(2,1)} %param.6) | copy-start | bytes 3932164
  0.7 3.6 %copy-start.4 = (f32[1,5120]{1,0:T(1,128)S(1)}, f32[1,5120]{1,0:T(1,128)}, u32[]{:S(2)}) copy-start(f32[1,5120]{1,0:T(1,128)} %param.7) | copy-start | bytes 61444
  6.2 1.0 copy-start.3
  8.8 56.1 %all-to-all-start = ((f32[64,1,2560]{2,1,0:T(1,128)}), f32[64,1,2560]{2,1,0:T(1,128)S(1)}, u32[]{:S(2)}, u32[]{:S(2)}) async-start(f32[64,1,2560]{2,1,0:T(1,128)} %all_to_all.19), calls=%async_computation | async-start | bytes 1310720 | tf_op jit(solution)/shard_map/all_to_all | solution.py:85
  30.1 62.6 %collective-permute-start = (bf16[1,128,5120]{2,1,0:T(8,128)(2,1)}, bf16[1,128,5120]{2,1,0:T(8,128)(2,1)S(1)}, u32[]{:S(2)}, u32[]{:S(2)}) collective-permute-start(bf16[1,128,5120]{2,1,0:T(8,128)(2,1)} %fusion.20), channel_id=1, source_target_pairs={{64,0},{128,64},{192,128},{256,192},{320,256},{384,320},{448,384},... | collective-permute-start | bytes 3932168 | tf_op jit(solution)/shard_map/ppermute | solution.py:21
  66.2 20.8 %all-to-all-start.1 = ((f32[64,1,64]{2,1,0:T(1,128)}), f32[64,1,64]{2,1,0:T(1,128)S(1)}, u32[]{:S(2)}, u32[]{:S(2)}) async-start(f32[64,1,64]{2,1,0:T(1,128)} %bitcast.10), calls=%async_computation.1 | async-start | bytes 65536 | tf_op jit(solution)/shard_map/all_to_all | solution.py:90
  87.7 18.9 %all-to-all-start.2 = ((f32[64,1,128]{2,1,0:T(1,128)}), f32[64,1,128]{2,1,0:T(1,128)S(1)}, u32[]{:S(2)}, u32[]{:S(2)}) async-start(f32[64,1,128]{2,1,0:T(1,128)} %reshape.736), calls=%async_computation.2 | async-start | bytes 65536 | tf_op jit(solution)/shard_map/all_to_all | solution.py:93

commit v5 on v4

--- a/solution.py
+++ b/solution.py
@@ -2,6 +2,7 @@
 import jax.numpy as jnp
 from jax import lax
 from jax.sharding import PartitionSpec as P
+from jax.experimental import pallas as pl
 
 norm_eps = 1e-05
 pair_eps = 1e-06
@@ -78,6 +79,38 @@
     return coef[:, 0, :]
 
 
+def tree_kernel(gram_ref, out_ref):
+    n = gram_ref.shape[1]
+    rows = lax.broadcasted_iota(jnp.int32, (n, n), 0)
+    cols = lax.broadcasted_iota(jnp.int32, (n, n), 1)
+    eye = (rows == cols).astype(jnp.float32)
+    for t in range(gram_ref.shape[0]):
+        gram = gram_ref[t]
+        coef = eye
+        for level_bit in range(n.bit_length() - 1):
+            swap = (cols == jnp.bitwise_xor(rows, 2**level_bit)).astype(jnp.float32)
+            partner = jnp.dot(swap, coef, precision=HIGH, preferred_element_type=jnp.float32)
+            gc = jnp.dot(coef, gram, precision=HIGH, preferred_element_type=jnp.float32)
+            gp = jnp.dot(partner, gram, precision=HIGH, preferred_element_type=jnp.float32)
+            inner_sum = jnp.sum(gc * partner, axis=1, keepdims=True)
+            own_square = jnp.sum(gc * coef, axis=1, keepdims=True)
+            far_square = jnp.sum(gp * partner, axis=1, keepdims=True)
+            keep_coef = 1.0 - inner_sum / (2.0 * (own_square + pair_eps))
+            take_coef = 1.0 - inner_sum / (2.0 * (far_square + pair_eps))
+            coef = keep_coef * coef + take_coef * partner
+        out_ref[t] = coef[0:8, :]
+
+
+def tree_coefficients(gram, interpret=False):
+    tensors, n = gram.shape[0], gram.shape[1]
+    rows = pl.pallas_call(
+        tree_kernel,
+        out_shape=jax.ShapeDtypeStruct((tensors, 8, n), jnp.float32),
+        interpret=interpret,
+    )(gram)
+    return rows[:, 0, :]
+
+
 def gram_adasum(grad_pair):
     devices = lax.axis_size("dp")
     me = lax.axis_index("dp")
@@ -92,7 +125,7 @@
     spread = jnp.broadcast_to(rows[None], (devices, tensors, partial.shape[1]))
     gathered = lax.all_to_all(spread, "dp", 0, 0, tiled=True)
     gram = jnp.swapaxes(gathered, 0, 1)
-    coef = coefficient_tree(gram)
+    coef = tree_coefficients(gram)
     own_coef = jnp.sum(jnp.where((jnp.arange(tensors) == mine)[:, None], coef, 0.0), axis=0)
     combined = jnp.sum(own_coef[:, None] * chunks, axis=0)
     return combined.astype(jnp.bfloat16)[None]

time: 120 us -> 117 us (0.975)
  blocking collectives: 0 us -> 20.7 us
  waiting for transfers between devices: 60.6 us -> 47.2 us
  starting transfers between devices: 31.9 us -> 25.3 us
  Pallas kernels: 0 us -> 6.29 us
  local copies, waits for them, and re-layouts: 11.8 us -> 6.47 us
  other arithmetic: 6.8 us -> 4.73 us
  matrix products: 7.38 us -> 5.51 us
    all_to_all x0 -> x1, blocking collectives: none -> 20.7 us  [gram_adasum(): rows = lax.all_to_all(partial[:, None, :], 'dp', 0, 0, tiled=True)]
    all_to_all x1 -> x0, waiting for transfers between devices: 14.2 us -> none  [gram_adasum(): rows = lax.all_to_all(partial[:, None, :], 'dp', 0, 0, tiled=True)]
    all_to_all x1 -> x0, starting transfers between devices: 6.46 us -> none  [gram_adasum(): rows = lax.all_to_all(partial[:, None, :], 'dp', 0, 0, tiled=True)]
    pallas_call x0 -> x1, Pallas kernels: none -> 6.29 us  [tree_coefficients(): pl.pallas_call(tree_kernel, out_shape=jax.ShapeDtypeStruct((tensors, 8, n...]
    mul x37 -> x0, local copies, waits for them, and re-layouts: 3.34 us -> none  [the longest x21 1.94 us: coefficient_tree(): take_coef = 1.0 - inner_sum / (2.0 * (far_square + pair_eps))]
    reduce_sum x16 -> x0, local copies, waits for them, and re-layouts: 1.4 us -> none  [coefficient_tree(): inner_sum = jnp.sum(gc * partner, axis=-1, keepdims=True)]
    dot_general x6 -> x0, matrix products: 1.34 us -> none  [coefficient_tree(): gc = jnp.einsum('tra,tab->trb', coef, gram, precision=HIGH)]
  transfers between devices with their start and end apart: 4 -> 3, of which waited for: 3 -> 2; matrix products, arithmetic and copies ran while one was open for 4% -> 3% of each run, Pallas kernels for 0% -> 0%
where the time goes in v5:
time: 117 us
  waiting for transfers between devices  47.2 us (40%)
  starting transfers between devices  25.3 us (22%)
  blocking collectives  20.7 us (18%)
  local copies, waits for them, and re-layouts  6.47 us (6%)
  Pallas kernels  6.29 us (5%)
  matrix products  5.51 us (5%)
  other arithmetic  4.73 us (4%)
    all_to_all x1, waiting for transfers between devices, gram_adasum(): chunks = lax.all_to_all(flat, 'dp', 0, 0, tiled=True)  32.9 us
    all_to_all x1, blocking collectives, gram_adasum(): rows = lax.all_to_all(partial[:, None, :], 'dp', 0, 0, tiled=True)  20.7 us
    all_to_all x1, starting transfers between devices, gram_adasum(): chunks = lax.all_to_all(flat, 'dp', 0, 0, tiled=True)  18.7 us
    all_to_all x1, waiting for transfers between devices, gram_adasum(): gathered = lax.all_to_all(spread, 'dp', 0, 0, tiled=True)  14.3 us
    pallas_call x1, Pallas kernels, tree_coefficients(): pl.pallas_call(tree_kernel, out_shape=jax.ShapeDtypeStruct((tensors, 8, n...  6.29 us
    all_to_all x1, starting transfers between devices, gram_adasum(): gathered = lax.all_to_all(spread, 'dp', 0, 0, tiled=True)  4.61 us
    unnamed x13, local copies, waits for them, and re-layouts  2.39 us
  transfers between devices with their start and end apart: 3, of which 2 were waited for; matrix products, arithmetic and copies ran while one was open for 3% of the time, Pallas kernels for 0%

profile of v5, /device:TPU:6, one launch (start us, length us, event | category | flops | bytes accessed | tf_op | source)
XLA Modules:
  0.0 116.9 jit_solution(15893241994922130531)
XLA Ops:
  0.6 0.0 copy-start
  0.6 0.0 copy-start.1
  0.7 0.0 copy-start.2
  0.7 1.8 %fusion.13 = f32[128]{0:T(128)S(1)} fusion(bf16[1,128,5120]{2,1,0:T(8,128)(2,1)} %param.5), kind=kLoop, calls=%fused_computation.18 | loop fusion | flops 1965952 | bytes 1311232 | tf_op jit(solution)/shard_map/reduce_sum | solution.py:27
  2.5 1.8 %fusion.34 = bf16[128,16]{0,1:T(8,128)(2,1)S(1)} fusion(bf16[1,128,5120]{2,1,0:T(8,128)(2,1)} %param.6, bf16[1,16,5120]{2,1,0:T(8,128)(2,1)} %param.9), kind=kOutput, calls=%fused_computation.33 | convolution fusion | flops 20975616 | bytes 1478656 | tf_op jit(solution)/shard_map/sh,gh->sg/dot_general | solution.py:43
  4.3 0.0 copy-done
  4.3 0.0 copy-done.1
  4.3 1.9 %fusion = f32[1,16,5120]{2,1,0:T(8,128)} fusion(bf16[1,128,5120]{2,1,0:T(8,128)(2,1)S(1)} %copy-done.2, bf16[1,128,5120]{2,1,0:T(8,128)(2,1)S(1)} %copy-done.1, f32[5120]{0:T(1024)S(1)} %bitcast.85, f32[128]{0:T(128)S(1)} %add_rsqrt_fusion, bf16[1,16,5120]{2,1,0:T(8,128)(2,1)S(1)} %copy-done), kind=kOutput, calls=%fused_computation.2 | convolution fusion | flops 44648448 | bytes 3133952 | tf_op jit(solution)/shard_map/tk,td->kd/dot_general | solution.py:36
  6.2 0.5 fusion.1
  6.7 0.5 copy-done.3
  7.3 1.6 %all_to_all.19 = f32[64,1,2560]{2,1,0:T(1,128)} reshape(f32[2,16,5120]{2,1,0:T(8,128)S(1)} %pad_maximum_fusion) | data formatting | bytes 1310720 | tf_op jit(solution)/shard_map/all_to_all | solution.py:118
  8.9 18.7 %all-to-all-start = ((f32[64,1,2560]{2,1,0:T(1,128)}), f32[64,1,2560]{2,1,0:T(1,128)S(1)}, u32[]{:S(2)}, u32[]{:S(2)}) async-start(f32[64,1,2560]{2,1,0:T(1,128)} %all_to_all.19), calls=%async_computation | async-start | bytes 1310720 | tf_op jit(solution)/shard_map/all_to_all | solution.py:118
  27.6 0.7 fusion.7
  28.3 1.9 %fusion.20 = bf16[1,128,5120]{2,1,0:T(8,128)(2,1)} fusion(f32[128,5120]{1,0:T(8,128)S(1)} %get-tuple-element.3, bf16[1,128,5120]{2,1,0:T(8,128)(2,1)S(1)} %copy-done.1, bf16[1,128,5120]{2,1,0:T(8,128)(2,1)S(1)} %copy-done.2, f32[128]{0:T(128)S(1)} %broadcast_multiply_fusion, f32[128]{0:T(128)S(1)} %add_rsqrt_fusion), kind=kLoop, calls=%fused_computation.23 | loop fusion | flops 5242880 | bytes 6554624 | tf_op jit(solution)/shard_map/broadcast_in_dim | solution.py:142
  30.2 1.9 %collective-permute-start = (bf16[1,128,5120]{2,1,0:T(8,128)(2,1)}, bf16[1,128,5120]{2,1,0:T(8,128)(2,1)S(1)}, u32[]{:S(2)}, u32[]{:S(2)}) collective-permute-start(bf16[1,128,5120]{2,1,0:T(8,128)(2,1)} %fusion.20), channel_id=1, source_target_pairs={{64,0},{128,64},{192,128},{256,192},{320,256},{384,320},{448,384},... | collective-permute-start | bytes 3932168 | tf_op jit(solution)/shard_map/ppermute | solution.py:22
  32.1 32.9 %all-to-all-done = f32[64,1,2560]{2,1,0:T(1,128)S(1)} async-done(((f32[64,1,2560]{2,1,0:T(1,128)}), f32[64,1,2560]{2,1,0:T(1,128)S(1)}, u32[]{:S(2)}, u32[]{:S(2)}) %all-to-all-start) | async-done | bytes 655392 | tf_op jit(solution)/shard_map/all_to_all | solution.py:118
  65.0 0.7 fusion.39
  65.7 20.7 %all_to_all.23 = f32[64,1,64]{2,1,0:T(1,128)S(1)} all-to-all(f32[64,1,64]{2,1,0:T(1,128)S(1)} %bitcast.84), channel_id=1, replica_groups=mesh['section'=8,'dp'=64] {'dp'}, dimensions={0} | all-to-all | bytes 32768 | tf_op jit(solution)/shard_map/all_to_all | solution.py:123
  86.4 0.7 reshape.55
  87.1 4.6 %all-to-all-start.2 = ((f32[64,1,128]{2,1,0:T(1,128)}), f32[64,1,128]{2,1,0:T(1,128)S(1)}, u32[]{:S(2)}, u32[]{:S(2)}) async-start(f32[64,1,128]{2,1,0:T(1,128)} %reshape.55), calls=%async_computation.2 | async-start | bytes 65536 | tf_op jit(solution)/shard_map/all_to_all | solution.py:126
  91.8 0.0 collective-permute-done
  91.8 14.3 %all-to-all-done.2 = f32[64,1,128]{2,1,0:T(1,128)S(1)} async-done(((f32[64,1,128]{2,1,0:T(1,128)}), f32[64,1,128]{2,1,0:T(1,128)S(1)}, u32[]{:S(2)}, u32[]{:S(2)}) %all-to-all-start.2) | async-done | bytes 32800 | tf_op jit(solution)/shard_map/all_to_all | solution.py:126
  106.1 0.5 broadcast.45
  106.6 0.7 reduce
  107.3 0.1 reshape.56
  107.4 0.6 copy.17
  108.0 6.3 %shard_map.68 = f32[2,8,64]{2,1,0:T(8,128)} custom-call(f32[2,64,64]{2,1,0:T(8,128)} %bitcast.82), custom_call_target="tpu_custom_call" | custom-call | tf_op jit(solution)/shard_map/pallas_call | solution.py:106
  114.3 0.7 slice.4
  115.0 0.1 select_reduce_fusion
  115.1 0.1 fusion.41
  115.3 0.6 convert_element_type.53
  115.9 1.1 copy.19
  (10 shorter events, 0.1 us)
Async XLA Ops:
  0.6 3.6 %copy-start = (bf16[1,16,5120]{2,1,0:T(8,128)(2,1)S(1)}, bf16[1,16,5120]{2,1,0:T(8,128)(2,1)}, u32[]{:S(2)}) copy-start(bf16[1,16,5120]{2,1,0:T(8,128)(2,1)} %param.8) | copy-start | bytes 491524
  0.6 3.6 %copy-start.1 = (bf16[1,128,5120]{2,1,0:T(8,128)(2,1)S(1)}, bf16[1,128,5120]{2,1,0:T(8,128)(2,1)}, u32[]{:S(2)}) copy-start(bf16[1,128,5120]{2,1,0:T(8,128)(2,1)} %param.5) | copy-start | bytes 3932164
  0.7 3.6 %copy-start.2 = (bf16[1,128,5120]{2,1,0:T(8,128)(2,1)S(1)}, bf16[1,128,5120]{2,1,0:T(8,128)(2,1)}, u32[]{:S(2)}) copy-start(bf16[1,128,5120]{2,1,0:T(8,128)(2,1)} %param.6) | copy-start | bytes 3932164
  0.7 3.6 %copy-start.4 = (f32[1,5120]{1,0:T(1,128)S(1)}, f32[1,5120]{1,0:T(1,128)}, u32[]{:S(2)}) copy-start(f32[1,5120]{1,0:T(1,128)} %param.7) | copy-start | bytes 61444
  6.2 1.0 copy-start.3
  8.9 56.1 %all-to-all-start = ((f32[64,1,2560]{2,1,0:T(1,128)}), f32[64,1,2560]{2,1,0:T(1,128)S(1)}, u32[]{:S(2)}, u32[]{:S(2)}) async-start(f32[64,1,2560]{2,1,0:T(1,128)} %all_to_all.19), calls=%async_computation | async-start | bytes 1310720 | tf_op jit(solution)/shard_map/all_to_all | solution.py:118
  30.2 61.6 %collective-permute-start = (bf16[1,128,5120]{2,1,0:T(8,128)(2,1)}, bf16[1,128,5120]{2,1,0:T(8,128)(2,1)S(1)}, u32[]{:S(2)}, u32[]{:S(2)}) collective-permute-start(bf16[1,128,5120]{2,1,0:T(8,128)(2,1)} %fusion.20), channel_id=1, source_target_pairs={{64,0},{128,64},{192,128},{256,192},{320,256},{384,320},{448,384},... | collective-permute-start | bytes 3932168 | tf_op jit(solution)/shard_map/ppermute | solution.py:22
  87.1 18.9 %all-to-all-start.2 = ((f32[64,1,128]{2,1,0:T(1,128)}), f32[64,1,128]{2,1,0:T(1,128)S(1)}, u32[]{:S(2)}, u32[]{:S(2)}) async-start(f32[64,1,128]{2,1,0:T(1,128)} %reshape.55), calls=%async_computation.2 | async-start | bytes 65536 | tf_op jit(solution)/shard_map/all_to_all | solution.py:126

commit v6 on v4

--- a/solution.py
+++ b/solution.py
@@ -1,7 +1,9 @@
+import numpy as np
 import jax
 import jax.numpy as jnp
 from jax import lax
 from jax.sharding import PartitionSpec as P
+from jax.experimental import pallas as pl
 
 norm_eps = 1e-05
 pair_eps = 1e-06
@@ -78,6 +80,52 @@
     return coef[:, 0, :]
 
 
+def bit_reversed_eye(n):
+    bits = n.bit_length() - 1
+    order = [int(format(i, f"0{bits}b")[::-1], 2) for i in range(n)]
+    return np.eye(n, dtype=np.float32)[order]
+
+
+def combine_kernel(start_ref, gram_ref, sel_ref, chunks_ref, out_ref):
+    n = gram_ref.shape[0]
+    finals = []
+    for t in range(gram_ref.shape[1] // n):
+        gram = gram_ref[:, t * n:(t + 1) * n]
+        coef = start_ref[...]
+        while coef.shape[0] > 1:
+            half = coef.shape[0] // 2
+            first, second = coef[:half], coef[half:]
+            g_first = jnp.dot(first, gram, precision=HIGH, preferred_element_type=jnp.float32)
+            g_second = jnp.dot(second, gram, precision=HIGH, preferred_element_type=jnp.float32)
+            inner_sum = jnp.sum(g_first * second, axis=1, keepdims=True)
+            own_square = jnp.sum(g_first * first, axis=1, keepdims=True)
+            far_square = jnp.sum(g_second * second, axis=1, keepdims=True)
+            keep_coef = 1.0 - inner_sum / (2.0 * (own_square + pair_eps))
+            take_coef = 1.0 - inner_sum / (2.0 * (far_square + pair_eps))
+            coef = keep_coef * first + take_coef * second
+        finals.append(coef)
+    sel = sel_ref[0:1, 0:n]
+    row = sel * finals[0] + (1.0 - sel) * finals[1]
+    eye = start_ref[...] * 0.0 + (
+        lax.broadcasted_iota(jnp.int32, (n, n), 0) == lax.broadcasted_iota(jnp.int32, (n, n), 1)
+    ).astype(jnp.float32)
+    column = lax.dot_general(
+        eye, row, (((1,), (1,)), ((), ())), precision=HIGH, preferred_element_type=jnp.float32
+    )
+    combined = jnp.sum(column * chunks_ref[...], axis=0, keepdims=True)
+    out_ref[...] = combined.astype(out_ref.dtype)
+
+
+def combine(gram_rows, first_tensor, chunks, interpret=False):
+    n = gram_rows.shape[0]
+    sel = jnp.broadcast_to(first_tensor.astype(jnp.float32), (8, 128))
+    return pl.pallas_call(
+        combine_kernel,
+        out_shape=jax.ShapeDtypeStruct((1, chunks.shape[1]), jnp.bfloat16),
+        interpret=interpret,
+    )(jnp.asarray(bit_reversed_eye(n)), gram_rows, sel, chunks)
+
+
 def gram_adasum(grad_pair):
     devices = lax.axis_size("dp")
     me = lax.axis_index("dp")
@@ -89,13 +137,9 @@
     partial = jnp.dot(chunks, chunks.T, precision=HIGH, preferred_element_type=jnp.float32)
     rows = lax.all_to_all(partial[:, None, :], "dp", 0, 0, tiled=True)
     rows = jnp.sum(rows.reshape(tensors, per_tensor, partial.shape[1]), axis=1)
-    spread = jnp.broadcast_to(rows[None], (devices, tensors, partial.shape[1]))
-    gathered = lax.all_to_all(spread, "dp", 0, 0, tiled=True)
-    gram = jnp.swapaxes(gathered, 0, 1)
-    coef = coefficient_tree(gram)
-    own_coef = jnp.sum(jnp.where((jnp.arange(tensors) == mine)[:, None], coef, 0.0), axis=0)
-    combined = jnp.sum(own_coef[:, None] * chunks, axis=0)
-    return combined.astype(jnp.bfloat16)[None]
+    spread = jnp.broadcast_to(rows.reshape(1, -1), (devices, tensors * partial.shape[1]))
+    gram_rows = lax.all_to_all(spread, "dp", 0, 0, tiled=True)
+    return combine(gram_rows, mine == 0, chunks)
 
 
 def per_device(activations, upstream, section_norm_gain, adapter_down_weight, adapter_up_weight):

time: 120 us -> 113 us (0.942)
  blocking collectives: 0 us -> 20.7 us
  waiting for transfers between devices: 60.6 us -> 46.3 us
  starting transfers between devices: 31.9 us -> 25.2 us
  local copies, waits for them, and re-layouts: 11.8 us -> 5.38 us
  Pallas kernels: 0 us -> 4.71 us
  other arithmetic: 6.8 us -> 3.77 us
  matrix products: 7.38 us -> 5.52 us
    all_to_all x0 -> x1, blocking collectives: none -> 20.7 us  [gram_adasum(): rows = lax.all_to_all(partial[:, None, :], 'dp', 0, 0, tiled=True)]
    all_to_all x2 -> x1, waiting for transfers between devices: 28.1 us -> 13.4 us  [gram_adasum(): gram_rows = lax.all_to_all(spread, 'dp', 0, 0, tiled=True)]
    all_to_all x2 -> x1, starting transfers between devices: 11.3 us -> 4.57 us  [gram_adasum(): gram_rows = lax.all_to_all(spread, 'dp', 0, 0, tiled=True)]
    pallas_call x0 -> x1, Pallas kernels: none -> 4.71 us  [combine(): pl.pallas_call(combine_kernel, out_shape=jax.ShapeDtypeStruct((1, chunks....]
    mul x37 -> x0, local copies, waits for them, and re-layouts: 3.34 us -> none  [the longest x21 1.94 us: coefficient_tree(): take_coef = 1.0 - inner_sum / (2.0 * (far_square + pair_eps))]
    reduce_sum x16 -> x0, local copies, waits for them, and re-layouts: 1.4 us -> none  [coefficient_tree(): inner_sum = jnp.sum(gc * partner, axis=-1, keepdims=True)]
    dot_general x6 -> x0, matrix products: 1.34 us -> none  [coefficient_tree(): gc = jnp.einsum('tra,tab->trb', coef, gram, precision=HIGH)]
    broadcast_in_dim x2 -> x3, local copies, waits for them, and re-layouts: 0.03 us -> 1.31 us  [the longest x2 0.7 us: gram_adasum(): jnp.broadcast_to(rows.reshape(1, -1), (devices, tensors * partial.shape[1]))]
  transfers between devices with their start and end apart: 4 -> 3, of which waited for: 3 -> 2; matrix products, arithmetic and copies ran while one was open for 4% -> 4% of each run, Pallas kernels for 0% -> 0%
where the time goes in v6:
time: 113 us; the launch traced here: 112 us
  waiting for transfers between devices  46.3 us (41%)
  starting transfers between devices  25.2 us (22%)
  blocking collectives  20.7 us (18%)
  matrix products  5.52 us (5%)
  local copies, waits for them, and re-layouts  5.38 us (5%)
  Pallas kernels  4.71 us (4%)
  other arithmetic  3.77 us (3%)
    all_to_all x1, waiting for transfers between devices, gram_adasum(): chunks = lax.all_to_all(flat, 'dp', 0, 0, tiled=True)  32.9 us
    all_to_all x1, blocking collectives, gram_adasum(): rows = lax.all_to_all(partial[:, None, :], 'dp', 0, 0, tiled=True)  20.7 us
    all_to_all x1, starting transfers between devices, gram_adasum(): chunks = lax.all_to_all(flat, 'dp', 0, 0, tiled=True)  18.7 us
    all_to_all x1, waiting for transfers between devices, gram_adasum(): gram_rows = lax.all_to_all(spread, 'dp', 0, 0, tiled=True)  13.4 us
    pallas_call x1, Pallas kernels, combine(): pl.pallas_call(combine_kernel, out_shape=jax.ShapeDtypeStruct((1, chunks....  4.71 us
    all_to_all x1, starting transfers between devices, gram_adasum(): gram_rows = lax.all_to_all(spread, 'dp', 0, 0, tiled=True)  4.57 us
    unnamed x14, local copies, waits for them, and re-layouts  2.46 us
  transfers between devices with their start and end apart: 3, of which 2 were waited for; matrix products, arithmetic and copies ran while one was open for 4% of the time, Pallas kernels for 0%

profile of v6, /device:TPU:6, one launch (start us, length us, event | category | flops | bytes accessed | tf_op | source)
XLA Modules:
  0.0 112.4 jit_solution(9053000281119341648)
XLA Ops:
  0.6 0.0 copy-start
  0.6 0.0 copy-start.1
  0.7 0.0 copy-start.2
  0.7 0.0 copy-start.5
  0.7 1.8 %fusion.13 = f32[128]{0:T(128)S(1)} fusion(bf16[1,128,5120]{2,1,0:T(8,128)(2,1)} %param.6), kind=kLoop, calls=%fused_computation.18 | loop fusion | flops 1965952 | bytes 1311232 | tf_op jit(solution)/shard_map/reduce_sum | solution.py:28
  2.5 1.8 %fusion.34 = bf16[128,16]{0,1:T(8,128)(2,1)S(1)} fusion(bf16[1,128,5120]{2,1,0:T(8,128)(2,1)} %param.7, bf16[1,16,5120]{2,1,0:T(8,128)(2,1)} %param.10), kind=kOutput, calls=%fused_computation.33 | convolution fusion | flops 20975616 | bytes 1478656 | tf_op jit(solution)/shard_map/sh,gh->sg/dot_general | solution.py:44
  4.3 0.0 copy-done
  4.3 0.0 copy-done.1
  4.3 0.0 copy-done.2
  4.3 0.0 copy-done.5
  4.3 1.9 %fusion = f32[1,16,5120]{2,1,0:T(8,128)} fusion(bf16[1,128,5120]{2,1,0:T(8,128)(2,1)S(1)} %copy-done.2, bf16[1,128,5120]{2,1,0:T(8,128)(2,1)S(1)} %copy-done.1, f32[5120]{0:T(1024)S(1)} %bitcast.81, f32[128]{0:T(128)S(1)} %add_rsqrt_fusion, bf16[1,16,5120]{2,1,0:T(8,128)(2,1)S(1)} %copy-done), kind=kOutput, calls=%fused_computation.2 | convolution fusion | flops 44648448 | bytes 3133952 | tf_op jit(solution)/shard_map/tk,td->kd/dot_general | solution.py:37
  6.2 0.0 copy-start.3
  6.2 0.5 fusion.1
  6.7 0.5 copy-done.3
  7.3 1.6 %all_to_all.21 = f32[64,1,2560]{2,1,0:T(1,128)} reshape(f32[2,16,5120]{2,1,0:T(8,128)S(1)} %pad_maximum_fusion) | data formatting | bytes 1310720 | tf_op jit(solution)/shard_map/all_to_all | solution.py:133
  8.9 18.7 %all-to-all-start = ((f32[64,1,2560]{2,1,0:T(1,128)}), f32[64,1,2560]{2,1,0:T(1,128)S(1)}, u32[]{:S(2)}, u32[]{:S(2)}) async-start(f32[64,1,2560]{2,1,0:T(1,128)} %all_to_all.21), calls=%async_computation | async-start | bytes 1310720 | tf_op jit(solution)/shard_map/all_to_all | solution.py:133
  27.6 0.7 fusion.7
  28.3 1.9 %fusion.20 = bf16[1,128,5120]{2,1,0:T(8,128)(2,1)} fusion(f32[128,5120]{1,0:T(8,128)S(1)} %get-tuple-element.3, bf16[1,128,5120]{2,1,0:T(8,128)(2,1)S(1)} %copy-done.1, bf16[1,128,5120]{2,1,0:T(8,128)(2,1)S(1)} %copy-done.2, f32[128]{0:T(128)S(1)} %broadcast_multiply_fusion, f32[128]{0:T(128)S(1)} %add_rsqrt_fusion), kind=kLoop, calls=%fused_computation.23 | loop fusion | flops 5242880 | bytes 6554624 | tf_op jit(solution)/shard_map/broadcast_in_dim | solution.py:153
  30.2 1.9 %collective-permute-start = (bf16[1,128,5120]{2,1,0:T(8,128)(2,1)}, bf16[1,128,5120]{2,1,0:T(8,128)(2,1)S(1)}, u32[]{:S(2)}, u32[]{:S(2)}) collective-permute-start(bf16[1,128,5120]{2,1,0:T(8,128)(2,1)} %fusion.20), channel_id=1, source_target_pairs={{64,0},{128,64},{192,128},{256,192},{320,256},{384,320},{448,384},... | collective-permute-start | bytes 3932168 | tf_op jit(solution)/shard_map/ppermute | solution.py:23
  32.1 32.9 %all-to-all-done = f32[64,1,2560]{2,1,0:T(1,128)S(1)} async-done(((f32[64,1,2560]{2,1,0:T(1,128)}), f32[64,1,2560]{2,1,0:T(1,128)S(1)}, u32[]{:S(2)}, u32[]{:S(2)}) %all-to-all-start) | async-done | bytes 655392 | tf_op jit(solution)/shard_map/all_to_all | solution.py:133
  65.0 0.7 fusion.43
  65.7 20.7 %all_to_all.25 = f32[64,1,64]{2,1,0:T(1,128)S(1)} all-to-all(f32[64,1,64]{2,1,0:T(1,128)S(1)} %bitcast.80), channel_id=1, replica_groups=mesh['section'=8,'dp'=64] {'dp'}, dimensions={0} | all-to-all | bytes 32768 | tf_op jit(solution)/shard_map/all_to_all | solution.py:138
  86.4 0.1 broadcast_in_dim.20
  86.5 0.6 broadcast_in_dim.21
  87.1 4.6 %all-to-all-start.2 = ((f32[64,1,128]{2,1,0:T(1,128)}), f32[64,1,128]{2,1,0:T(1,128)S(1)}, u32[]{:S(2)}, u32[]{:S(2)}) async-start(f32[64,1,128]{2,1,0:T(1,128)} %broadcast_in_dim.21), calls=%async_computation.2 | async-start | bytes 65536 | tf_op jit(solution)/shard_map/all_to_all | solution.py:141
  91.7 0.0 collective-permute-done
  91.7 0.9 copy.13
  92.6 13.4 %all-to-all-done.2 = f32[64,1,128]{2,1,0:T(1,128)S(1)} async-done(((f32[64,1,128]{2,1,0:T(1,128)}), f32[64,1,128]{2,1,0:T(1,128)S(1)}, u32[]{:S(2)}, u32[]{:S(2)}) %all-to-all-start.2) | async-done | bytes 32800 | tf_op jit(solution)/shard_map/all_to_all | solution.py:141
  106.0 0.6 broadcast_in_dim.22.sel_ref
  106.6 0.0 copy-done.4
  106.6 4.7 %shard_map.77 = bf16[1,2560]{1,0:T(2,128)(2,1)} custom-call(f32[64,64]{1,0:T(8,128)} %constant.40.clone.start_ref, f32[64,128]{1,0:T(8,128)} %bitcast.78, f32[8,128]{1,0:T(8,128)} %broadcast_in_dim.22.sel_ref, f32[64,2560]{1,0:T(8,128)} %bitcast.77), custom_call_target="tpu_custom_call" | custom-call | tf_op jit(solution)/shard_map/pallas_call | solution.py:122
  111.3 1.1 copy.15
  (5 shorter events, 0.1 us)
Async XLA Ops:
  0.6 3.6 %copy-start = (bf16[1,16,5120]{2,1,0:T(8,128)(2,1)S(1)}, bf16[1,16,5120]{2,1,0:T(8,128)(2,1)}, u32[]{:S(2)}) copy-start(bf16[1,16,5120]{2,1,0:T(8,128)(2,1)} %param.9) | copy-start | bytes 491524
  0.6 3.6 %copy-start.1 = (bf16[1,128,5120]{2,1,0:T(8,128)(2,1)S(1)}, bf16[1,128,5120]{2,1,0:T(8,128)(2,1)}, u32[]{:S(2)}) copy-start(bf16[1,128,5120]{2,1,0:T(8,128)(2,1)} %param.6) | copy-start | bytes 3932164
  0.7 3.6 %copy-start.2 = (bf16[1,128,5120]{2,1,0:T(8,128)(2,1)S(1)}, bf16[1,128,5120]{2,1,0:T(8,128)(2,1)}, u32[]{:S(2)}) copy-start(bf16[1,128,5120]{2,1,0:T(8,128)(2,1)} %param.7) | copy-start | bytes 3932164
  0.7 3.6 %copy-start.5 = (f32[1,5120]{1,0:T(1,128)S(1)}, f32[1,5120]{1,0:T(1,128)}, u32[]{:S(2)}) copy-start(f32[1,5120]{1,0:T(1,128)} %param.8) | copy-start | bytes 61444
  6.2 1.0 copy-start.3
  8.9 56.1 %all-to-all-start = ((f32[64,1,2560]{2,1,0:T(1,128)}), f32[64,1,2560]{2,1,0:T(1,128)S(1)}, u32[]{:S(2)}, u32[]{:S(2)}) async-start(f32[64,1,2560]{2,1,0:T(1,128)} %all_to_all.21), calls=%async_computation | async-start | bytes 1310720 | tf_op jit(solution)/shard_map/all_to_all | solution.py:133
  30.2 61.5 %collective-permute-start = (bf16[1,128,5120]{2,1,0:T(8,128)(2,1)}, bf16[1,128,5120]{2,1,0:T(8,128)(2,1)S(1)}, u32[]{:S(2)}, u32[]{:S(2)}) collective-permute-start(bf16[1,128,5120]{2,1,0:T(8,128)(2,1)} %fusion.20), channel_id=1, source_target_pairs={{64,0},{128,64},{192,128},{256,192},{320,256},{384,320},{448,384},... | collective-permute-start | bytes 3932168 | tf_op jit(solution)/shard_map/ppermute | solution.py:23
  87.1 18.9 %all-to-all-start.2 = ((f32[64,1,128]{2,1,0:T(1,128)}), f32[64,1,128]{2,1,0:T(1,128)S(1)}, u32[]{:S(2)}, u32[]{:S(2)}) async-start(f32[64,1,128]{2,1,0:T(1,128)} %broadcast_in_dim.21), calls=%async_computation.2 | async-start | bytes 65536 | tf_op jit(solution)/shard_map/all_to_all | solution.py:141
  106.0 0.6 copy-start.4

commit v7 on v6

--- a/solution.py
+++ b/solution.py
@@ -2,7 +2,7 @@
 import jax
 import jax.numpy as jnp
 from jax import lax
-from jax.sharding import PartitionSpec as P
+from jax.sharding import Mesh, PartitionSpec as P
 from jax.experimental import pallas as pl
 
 norm_eps = 1e-05
@@ -127,18 +127,25 @@
 
 
 def gram_adasum(grad_pair):
-    devices = lax.axis_size("dp")
-    me = lax.axis_index("dp")
+    ny, nz = lax.axis_size("y"), lax.axis_size("z")
+    devices = ny * nz
+    me = lax.axis_index("y") * nz + lax.axis_index("z")
     flat = grad_pair.reshape(devices, -1)
-    chunks = lax.all_to_all(flat, "dp", 0, 0, tiled=True)
+    chunks = lax.all_to_all(flat, ("y", "z"), 0, 0, tiled=True)
     tensors = grad_pair.shape[0]
     per_tensor = devices // tensors
     mine = me // per_tensor
+    n = devices
     partial = jnp.dot(chunks, chunks.T, precision=HIGH, preferred_element_type=jnp.float32)
-    rows = lax.all_to_all(partial[:, None, :], "dp", 0, 0, tiled=True)
-    rows = jnp.sum(rows.reshape(tensors, per_tensor, partial.shape[1]), axis=1)
-    spread = jnp.broadcast_to(rows.reshape(1, -1), (devices, tensors * partial.shape[1]))
-    gram_rows = lax.all_to_all(spread, "dp", 0, 0, tiled=True)
+    part_z = lax.all_to_all(partial.reshape(nz, ny, n), "z", 0, 0, tiled=True)
+    part_z = jnp.sum(part_z.reshape(nz, ny, n), axis=0)
+    part_y = lax.all_to_all(part_z, "y", 0, 0, tiled=True)
+    rows = jnp.sum(part_y.reshape(tensors, ny // tensors, n), axis=1)
+    spread_y = jnp.broadcast_to(rows.reshape(1, tensors * n), (ny, tensors * n))
+    got_y = lax.all_to_all(spread_y, "y", 0, 0, tiled=True)
+    spread_z = jnp.broadcast_to(got_y.reshape(1, ny * tensors * n), (nz, ny * tensors * n))
+    got_z = lax.all_to_all(spread_z, "z", 0, 0, tiled=True)
+    gram_rows = got_z.reshape(n, tensors * n)
     return combine(gram_rows, mine == 0, chunks)
 
 
@@ -156,16 +163,21 @@
 
 
 def solution(mesh):
+    sections, replicas = mesh.devices.shape
+    z_size = 16 if replicas % 16 == 0 else replicas
+    grid = Mesh(
+        mesh.devices.reshape(sections, replicas // z_size, z_size), ("section", "y", "z")
+    )
     return jax.shard_map(
         per_device,
-        mesh=mesh,
+        mesh=grid,
         in_specs=(
-            P("section", "dp", None),
-            P("section", "dp", None),
+            P("section", ("y", "z"), None),
+            P("section", ("y", "z"), None),
             P("section", None),
             P("section", None, None),
             P("section", None, None),
         ),
-        out_specs=(P("section", "dp", None), P("section", "dp")),
+        out_specs=(P("section", ("y", "z"), None), P("section", ("y", "z"))),
         check_vma=False,
     )

time: 113 us -> 125 us (1.11)
  blocking collectives: 20.7 us -> 32.8 us
  other arithmetic: 3.77 us -> 6.03 us
  waiting for transfers between devices: 46.3 us -> 44.5 us
    all_to_all x1 -> x3, blocking collectives: 20.7 us -> 32.8 us  [the longest x1 17.6 us: gram_adasum(): part_z = lax.all_to_all(partial.reshape(nz, ny, n), 'z', 0, 0, tiled=True)]
    all_to_all x0 -> x2, other arithmetic: none -> 2.23 us  [the longest x1 1.55 us: gram_adasum(): chunks = lax.all_to_all(flat, ('y', 'z'), 0, 0, tiled=True)]
    all_to_all x2, waiting for transfers between devices: 46.3 us -> 44.5 us  [the longest x1 32.9 us: gram_adasum(): chunks = lax.all_to_all(flat, ('y', 'z'), 0, 0, tiled=True)]
    unnamed x14 -> x16, local copies, waits for them, and re-layouts: 2.46 us -> 2.64 us
  transfers between devices with their start and end apart: 3 -> 3, of which waited for: 2 -> 2; matrix products, arithmetic and copies ran while one was open for 4% -> 7% of each run, Pallas kernels for 0% -> 0%
where the time goes in v7:
time: 125 us
  waiting for transfers between devices  44.5 us (36%)
  blocking collectives  32.8 us (26%)
  starting transfers between devices  24.1 us (19%)
  local copies, waits for them, and re-layouts  6.28 us (5%)
  other arithmetic  6.03 us (5%)
  matrix products  5.6 us (4%)
  Pallas kernels  4.71 us (4%)
    all_to_all x1, waiting for transfers between devices, gram_adasum(): chunks = lax.all_to_all(flat, ('y', 'z'), 0, 0, tiled=True)  32.9 us
    all_to_all x1, starting transfers between devices, gram_adasum(): chunks = lax.all_to_all(flat, ('y', 'z'), 0, 0, tiled=True)  18.7 us
    all_to_all x1, blocking collectives, gram_adasum(): part_z = lax.all_to_all(partial.reshape(nz, ny, n), 'z', 0, 0, tiled=True)  17.6 us
    all_to_all x1, waiting for transfers between devices, gram_adasum(): got_z = lax.all_to_all(spread_z, 'z', 0, 0, tiled=True)  11.6 us
    all_to_all x1, blocking collectives, gram_adasum(): part_y = lax.all_to_all(part_z, 'y', 0, 0, tiled=True)  7.62 us
    all_to_all x1, blocking collectives, gram_adasum(): got_y = lax.all_to_all(spread_y, 'y', 0, 0, tiled=True)  7.61 us
    pallas_call x1, Pallas kernels, combine(): pl.pallas_call(combine_kernel, out_shape=jax.ShapeDtypeStruct((1, chunks....  4.71 us
    all_to_all x1, starting transfers between devices, gram_adasum(): got_z = lax.all_to_all(spread_z, 'z', 0, 0, tiled=True)  3.5 us
  transfers between devices with their start and end apart: 3, of which 2 were waited for; matrix products, arithmetic and copies ran while one was open for 7% of the time, Pallas kernels for 0%

profile of v7, /device:TPU:6, one launch (start us, length us, event | category | flops | bytes accessed | tf_op | source)
XLA Modules:
  0.0 124.9 jit_solution(3491621010678733326)
XLA Ops:
  0.6 0.0 copy-start
  0.7 0.0 copy-start.2
  0.7 1.8 %fusion.13 = f32[128]{0:T(128)S(1)} fusion(bf16[1,128,5120]{2,1,0:T(8,128)(2,1)} %param.6), kind=kLoop, calls=%fused_computation.18 | loop fusion | flops 1965952 | bytes 1311232 | tf_op jit(solution)/shard_map/reduce_sum | solution.py:28
  2.5 1.8 %fusion.31 = bf16[128,16]{0,1:T(8,128)(2,1)S(1)} fusion(bf16[1,128,5120]{2,1,0:T(8,128)(2,1)} %param.7, bf16[1,16,5120]{2,1,0:T(8,128)(2,1)} %param.10), kind=kOutput, calls=%fused_computation.32 | convolution fusion | flops 20975616 | bytes 1478656 | tf_op jit(solution)/shard_map/sh,gh->sg/dot_general | solution.py:44
  4.3 0.0 copy-done.1
  4.3 1.9 %fusion = f32[1,16,5120]{2,1,0:T(8,128)} fusion(bf16[1,128,5120]{2,1,0:T(8,128)(2,1)S(1)} %copy-done.2, bf16[1,128,5120]{2,1,0:T(8,128)(2,1)S(1)} %copy-done.1, f32[5120]{0:T(1024)S(1)} %bitcast.78, f32[128]{0:T(128)S(1)} %add_rsqrt_fusion, bf16[1,16,5120]{2,1,0:T(8,128)(2,1)S(1)} %copy-done), kind=kOutput, calls=%fused_computation.2 | convolution fusion | flops 44648448 | bytes 3133952 | tf_op jit(solution)/shard_map/tk,td->kd/dot_general | solution.py:37
  6.2 0.5 fusion.1
  6.7 0.5 copy-done.3
  7.2 1.6 %all_to_all.32 = f32[64,1,2560]{2,1,0:T(1,128)} reshape(f32[2,16,5120]{2,1,0:T(8,128)S(1)} %pad_maximum_fusion) | data formatting | bytes 1310720 | tf_op jit(solution)/shard_map/all_to_all | solution.py:134
  8.8 18.7 %all-to-all-start = ((f32[64,1,2560]{2,1,0:T(1,128)}), f32[64,1,2560]{2,1,0:T(1,128)S(1)}, u32[]{:S(2)}, u32[]{:S(2)}) async-start(f32[64,1,2560]{2,1,0:T(1,128)} %all_to_all.32), calls=%async_computation | async-start | bytes 1310720 | tf_op jit(solution)/shard_map/all_to_all | solution.py:134
  27.5 0.7 fusion.7
  28.2 1.9 %fusion.20 = bf16[1,128,5120]{2,1,0:T(8,128)(2,1)} fusion(f32[128,5120]{1,0:T(8,128)S(1)} %get-tuple-element.3, bf16[1,128,5120]{2,1,0:T(8,128)(2,1)S(1)} %copy-done.1, bf16[1,128,5120]{2,1,0:T(8,128)(2,1)S(1)} %copy-done.2, f32[128]{0:T(128)S(1)} %broadcast_multiply_fusion, f32[128]{0:T(128)S(1)} %add_rsqrt_fusion), kind=kLoop, calls=%fused_computation.23 | loop fusion | flops 5242880 | bytes 6554624 | tf_op jit(solution)/shard_map/broadcast_in_dim | solution.py:160
  30.1 1.9 %collective-permute-start = (bf16[1,128,5120]{2,1,0:T(8,128)(2,1)}, bf16[1,128,5120]{2,1,0:T(8,128)(2,1)S(1)}, u32[]{:S(2)}, u32[]{:S(2)}) collective-permute-start(bf16[1,128,5120]{2,1,0:T(8,128)(2,1)} %fusion.20), channel_id=1, source_target_pairs={{64,0},{128,64},{192,128},{256,192},{320,256},{384,320},{448,384},... | collective-permute-start | bytes 3932168 | tf_op jit(solution)/shard_map/ppermute | solution.py:23
  32.0 32.9 %all-to-all-done = f32[64,1,2560]{2,1,0:T(1,128)S(1)} async-done(((f32[64,1,2560]{2,1,0:T(1,128)}), f32[64,1,2560]{2,1,0:T(1,128)S(1)}, u32[]{:S(2)}, u32[]{:S(2)}) %all-to-all-start) | async-done | bytes 655392 | tf_op jit(solution)/shard_map/all_to_all | solution.py:134
  64.9 1.6 %reduce = f32[64,2560]{1,0:T(8,128)S(1)} reduce(f32[64,1,2560]{2,1,0:T(1,128)S(1)} %all-to-all-done, f32[]{:T(128)} %constant.53), dimensions={1}, to_apply=%all_to_all.25.reduce_sub_computation | reduce | bytes 1310724 | tf_op jit(solution)/shard_map/all_to_all | solution.py:134
  66.5 0.2 dot_general.25
  66.7 0.8 fusion.39
  67.5 0.1 reshape.74
  67.6 17.6 %all_to_all.38 = f32[16,1,256]{2,1,0:T(1,128)S(1)} all-to-all(f32[16,1,256]{2,1,0:T(1,128)S(1)} %reshape.74), channel_id=1, replica_groups=mesh['section'=8,'y'=4,'z'=16] {'z'}, dimensions={0} | all-to-all | bytes 32768 | tf_op jit(solution)/shard_map/all_to_all | solution.py:140
  85.2 0.5 broadcast.46
  85.7 0.7 reduce.1
  86.4 0.1 reshape.75
  86.5 7.6 %all_to_all.39 = f32[4,1,64]{2,1,0:T(1,128)S(1)} all-to-all(f32[4,1,64]{2,1,0:T(1,128)S(1)} %bitcast.81), channel_id=1, replica_groups=mesh['section'=8,'y'=4,'z'=16] {'y'}, dimensions={0} | all-to-all | bytes 2048 | tf_op jit(solution)/shard_map/all_to_all | solution.py:142
  94.2 0.1 broadcast_in_dim.23
  94.2 7.6 %all_to_all.40 = f32[4,1,128]{2,1,0:T(1,128)S(1)} all-to-all(f32[4,1,128]{2,1,0:T(1,128)S(1)} %broadcast_in_dim.24), channel_id=1, replica_groups=mesh['section'=8,'y'=4,'z'=16] {'y'}, dimensions={0} | all-to-all | bytes 4096 | tf_op jit(solution)/shard_map/all_to_all | solution.py:145
  101.9 0.6 broadcast_in_dim.26
  102.5 3.5 %all-to-all-start.4 = ((f32[16,1,512]{2,1,0:T(1,128)}), f32[16,1,512]{2,1,0:T(1,128)S(1)}, u32[]{:S(2)}, u32[]{:S(2)}) async-start(f32[16,1,512]{2,1,0:T(1,128)} %broadcast_in_dim.26), calls=%async_computation.4 | async-start | bytes 65536 | tf_op jit(solution)/shard_map/all_to_all | solution.py:147
  106.0 0.9 copy.24
  106.9 11.6 %all-to-all-done.4 = f32[16,1,512]{2,1,0:T(1,128)S(1)} async-done(((f32[16,1,512]{2,1,0:T(1,128)}), f32[16,1,512]{2,1,0:T(1,128)S(1)}, u32[]{:S(2)}, u32[]{:S(2)}) %all-to-all-start.4) | async-done | bytes 32800 | tf_op jit(solution)/shard_map/all_to_all | solution.py:147
  118.5 0.6 broadcast_in_dim.27.sel_ref
  119.2 4.7 %shard_map.77 = bf16[1,2560]{1,0:T(2,128)(2,1)} custom-call(f32[64,64]{1,0:T(8,128)} %constant.47.clone.start_ref, f32[64,128]{1,0:T(8,128)} %bitcast.77, f32[8,128]{1,0:T(8,128)} %broadcast_in_dim.27.sel_ref, f32[64,2560]{1,0:T(8,128)} %bitcast.76), custom_call_target="tpu_custom_call" | custom-call | tf_op jit(solution)/shard_map/pallas_call | solution.py:122
  123.9 1.1 copy.26
  (16 shorter events, 0.1 us)
Async XLA Ops:
  0.6 3.6 %copy-start = (bf16[1,16,5120]{2,1,0:T(8,128)(2,1)S(1)}, bf16[1,16,5120]{2,1,0:T(8,128)(2,1)}, u32[]{:S(2)}) copy-start(bf16[1,16,5120]{2,1,0:T(8,128)(2,1)} %param.9) | copy-start | bytes 491524
  0.6 3.6 %copy-start.1 = (bf16[1,128,5120]{2,1,0:T(8,128)(2,1)S(1)}, bf16[1,128,5120]{2,1,0:T(8,128)(2,1)}, u32[]{:S(2)}) copy-start(bf16[1,128,5120]{2,1,0:T(8,128)(2,1)} %param.6) | copy-start | bytes 3932164
  0.7 3.6 %copy-start.2 = (bf16[1,128,5120]{2,1,0:T(8,128)(2,1)S(1)}, bf16[1,128,5120]{2,1,0:T(8,128)(2,1)}, u32[]{:S(2)}) copy-start(bf16[1,128,5120]{2,1,0:T(8,128)(2,1)} %param.7) | copy-start | bytes 3932164
  0.7 3.6 %copy-start.5 = (f32[1,5120]{1,0:T(1,128)S(1)}, f32[1,5120]{1,0:T(1,128)}, u32[]{:S(2)}) copy-start(f32[1,5120]{1,0:T(1,128)} %param.8) | copy-start | bytes 61444
  6.2 1.0 copy-start.3
  8.8 56.1 %all-to-all-start = ((f32[64,1,2560]{2,1,0:T(1,128)}), f32[64,1,2560]{2,1,0:T(1,128)S(1)}, u32[]{:S(2)}, u32[]{:S(2)}) async-start(f32[64,1,2560]{2,1,0:T(1,128)} %all_to_all.32), calls=%async_computation | async-start | bytes 1310720 | tf_op jit(solution)/shard_map/all_to_all | solution.py:134
  30.1 75.9 %collective-permute-start = (bf16[1,128,5120]{2,1,0:T(8,128)(2,1)}, bf16[1,128,5120]{2,1,0:T(8,128)(2,1)S(1)}, u32[]{:S(2)}, u32[]{:S(2)}) collective-permute-start(bf16[1,128,5120]{2,1,0:T(8,128)(2,1)} %fusion.20), channel_id=1, source_target_pairs={{64,0},{128,64},{192,128},{256,192},{320,256},{384,320},{448,384},... | collective-permute-start | bytes 3932168 | tf_op jit(solution)/shard_map/ppermute | solution.py:23
  102.5 16.1 %all-to-all-start.4 = ((f32[16,1,512]{2,1,0:T(1,128)}), f32[16,1,512]{2,1,0:T(1,128)S(1)}, u32[]{:S(2)}, u32[]{:S(2)}) async-start(f32[16,1,512]{2,1,0:T(1,128)} %broadcast_in_dim.26), calls=%async_computation.4 | async-start | bytes 65536 | tf_op jit(solution)/shard_map/all_to_all | solution.py:147
  118.5 0.6 copy-start.4

commit v8 on v6

--- a/solution.py
+++ b/solution.py
@@ -86,7 +86,7 @@
     return np.eye(n, dtype=np.float32)[order]
 
 
-def combine_kernel(start_ref, gram_ref, sel_ref, chunks_ref, out_ref):
+def combine_kernel(start_ref, gram_ref, sel_ref, high_ref, low_ref, out_ref):
     n = gram_ref.shape[0]
     finals = []
     for t in range(gram_ref.shape[1] // n):
@@ -112,34 +112,56 @@
     column = lax.dot_general(
         eye, row, (((1,), (1,)), ((), ())), precision=HIGH, preferred_element_type=jnp.float32
     )
-    combined = jnp.sum(column * chunks_ref[...], axis=0, keepdims=True)
+    chunks = high_ref[...].astype(jnp.float32) + low_ref[...].astype(jnp.float32)
+    combined = jnp.sum(column * chunks, axis=0, keepdims=True)
     out_ref[...] = combined.astype(out_ref.dtype)
 
 
-def combine(gram_rows, first_tensor, chunks, interpret=False):
+def combine(gram_rows, first_tensor, high_chunks, low_chunks, interpret=False):
     n = gram_rows.shape[0]
     sel = jnp.broadcast_to(first_tensor.astype(jnp.float32), (8, 128))
     return pl.pallas_call(
         combine_kernel,
-        out_shape=jax.ShapeDtypeStruct((1, chunks.shape[1]), jnp.bfloat16),
+        out_shape=jax.ShapeDtypeStruct((1, high_chunks.shape[1]), jnp.bfloat16),
         interpret=interpret,
-    )(jnp.asarray(bit_reversed_eye(n)), gram_rows, sel, chunks)
+    )(jnp.asarray(bit_reversed_eye(n)), gram_rows, sel, high_chunks, low_chunks)
+
+
+def split_three(x):
+    one = x.astype(jnp.bfloat16)
+    rest = x - one.astype(jnp.float32)
+    two = rest.astype(jnp.bfloat16)
+    three = (rest - two.astype(jnp.float32)).astype(jnp.bfloat16)
+    return one, two, three
 
 
 def gram_adasum(grad_pair):
     devices = lax.axis_size("dp")
     me = lax.axis_index("dp")
     flat = grad_pair.reshape(devices, -1)
-    chunks = lax.all_to_all(flat, "dp", 0, 0, tiled=True)
+    width = flat.shape[1]
+    high = flat.astype(jnp.bfloat16)
+    low = (flat - high.astype(jnp.float32)).astype(jnp.bfloat16)
+    high_chunks = lax.all_to_all(high, "dp", 0, 0, tiled=True)
     tensors = grad_pair.shape[0]
     per_tensor = devices // tensors
     mine = me // per_tensor
-    partial = jnp.dot(chunks, chunks.T, precision=HIGH, preferred_element_type=jnp.float32)
-    rows = lax.all_to_all(partial[:, None, :], "dp", 0, 0, tiled=True)
-    rows = jnp.sum(rows.reshape(tensors, per_tensor, partial.shape[1]), axis=1)
-    spread = jnp.broadcast_to(rows.reshape(1, -1), (devices, tensors * partial.shape[1]))
+    n = devices
+    partial = lax.dot_general(
+        high_chunks, high_chunks, (((1,), (1,)), ((), ())), preferred_element_type=jnp.float32
+    )
+    pad = (-(width + 3 * n)) % 128
+    payload = jnp.concatenate(
+        [low, *split_three(partial), jnp.zeros((devices, pad), jnp.bfloat16)], axis=1
+    )
+    got = lax.all_to_all(payload, "dp", 0, 0, tiled=True)
+    low_chunks = got[:, :width]
+    pieces = got[:, width:width + 3 * n].astype(jnp.float32).reshape(devices, 3, n)
+    row_parts = (pieces[:, 0] + pieces[:, 1]) + pieces[:, 2]
+    rows = jnp.sum(row_parts.reshape(tensors, per_tensor, n), axis=1)
+    spread = jnp.broadcast_to(rows.reshape(1, -1), (devices, tensors * n))
     gram_rows = lax.all_to_all(spread, "dp", 0, 0, tiled=True)
-    return combine(gram_rows, mine == 0, chunks)
+    return combine(gram_rows, mine == 0, high_chunks, low_chunks)
 
 
 def per_device(activations, upstream, section_norm_gain, adapter_down_weight, adapter_up_weight):

time: 113 us -> 125 us (1.11)
  blocking collectives: 20.7 us -> 0 us
  local copies, waits for them, and re-layouts: 5.38 us -> 15.2 us
  other arithmetic: 3.77 us -> 13.2 us
  starting transfers between devices: 25.2 us -> 33.9 us
  waiting for transfers between devices: 46.3 us -> 50.2 us
    all_to_all x1 -> x0, blocking collectives: 20.7 us -> none  [gram_adasum(): rows = lax.all_to_all(partial[:, None, :], 'dp', 0, 0, tiled=True)]
    all_to_all x1 -> x2, starting transfers between devices: 18.7 us -> 25.4 us  [the longest x1 19 us: gram_adasum(): high_chunks = lax.all_to_all(high, 'dp', 0, 0, tiled=True)]
    unnamed x14 -> x21, local copies, waits for them, and re-layouts: 2.46 us -> 9.16 us
    convert_element_type x0 -> x3, other arithmetic: none -> 4.34 us  [the longest x2 3.58 us: gram_adasum(): high = flat.astype(jnp.bfloat16)]
    all_to_all x1 -> x2, waiting for transfers between devices: 32.9 us -> 36.5 us  [the longest x1 18.9 us: gram_adasum(): got = lax.all_to_all(payload, 'dp', 0, 0, tiled=True)]
    all_to_all x1, starting transfers between devices: 4.57 us -> 6.59 us  [gram_adasum(): gram_rows = lax.all_to_all(spread, 'dp', 0, 0, tiled=True)]
    another operation x1, other arithmetic: 0.04 us -> 1.85 us  [replica_backward(): return (passed.astype(jnp.bfloat16), jnp.stack([down_term, upward_term]))]
    broadcast_in_dim x1, other arithmetic: 1.89 us -> 3.55 us  [per_device(): shifted = from_behind(passed_local[None], 'section', -1)]
  transfers between devices with their start and end apart: 3 -> 4, of which waited for: 2 -> 3; matrix products, arithmetic and copies ran while one was open for 4% -> 9% of each run, Pallas kernels for 0% -> 0%
where the time goes in v8:
time: 125 us; the launch traced here: 124 us
  waiting for transfers between devices  50.2 us (40%)
  starting transfers between devices  33.9 us (27%)
  local copies, waits for them, and re-layouts  15.2 us (12%)
  other arithmetic  13.2 us (11%)
  matrix products  5.71 us (5%)
  Pallas kernels  4.72 us (4%)
    all_to_all x1, starting transfers between devices, gram_adasum(): high_chunks = lax.all_to_all(high, 'dp', 0, 0, tiled=True)  19 us
    all_to_all x1, waiting for transfers between devices, gram_adasum(): got = lax.all_to_all(payload, 'dp', 0, 0, tiled=True)  18.9 us
    all_to_all x1, waiting for transfers between devices, gram_adasum(): high_chunks = lax.all_to_all(high, 'dp', 0, 0, tiled=True)  17.6 us
    all_to_all x1, waiting for transfers between devices, gram_adasum(): gram_rows = lax.all_to_all(spread, 'dp', 0, 0, tiled=True)  13.7 us
    unnamed x21, local copies, waits for them, and re-layouts  9.16 us
    all_to_all x1, starting transfers between devices, gram_adasum(): gram_rows = lax.all_to_all(spread, 'dp', 0, 0, tiled=True)  6.59 us
    all_to_all x1, starting transfers between devices, gram_adasum(): got = lax.all_to_all(payload, 'dp', 0, 0, tiled=True)  6.48 us
    pallas_call x1, Pallas kernels, combine(): pl.pallas_call(combine_kernel, out_shape=jax.ShapeDtypeStruct((1, high_ch...  4.72 us
  transfers between devices with their start and end apart: 4, of which 3 were waited for; matrix products, arithmetic and copies ran while one was open for 9% of the time, Pallas kernels for 0%

profile of v8, /device:TPU:6, one launch (start us, length us, event | category | flops | bytes accessed | tf_op | source)
XLA Modules:
  0.0 123.8 jit_solution(191924865315862308)
XLA Ops:
  0.7 1.8 %fusion.13 = f32[128]{0:T(128)S(1)} fusion(bf16[1,128,5120]{2,1,0:T(8,128)(2,1)} %param.6), kind=kLoop, calls=%fused_computation.18 | loop fusion | flops 1965952 | bytes 1311232 | tf_op jit(solution)/shard_map/reduce_sum | solution.py:28
  2.5 1.8 %fusion.31 = bf16[128,16]{0,1:T(8,128)(2,1)S(1)} fusion(bf16[1,128,5120]{2,1,0:T(8,128)(2,1)} %param.7, bf16[1,16,5120]{2,1,0:T(8,128)(2,1)} %param.10), kind=kOutput, calls=%fused_computation.32 | convolution fusion | flops 20975616 | bytes 1478656 | tf_op jit(solution)/shard_map/sh,gh->sg/dot_general | solution.py:44
  4.3 1.1 fusion
  5.4 0.5 fusion.1
  5.9 0.7 copy-done.4
  6.7 1.0 convert_element_type.91
  7.7 0.5 broadcast.42
  8.2 3.5 %reduce = bf16[64,2560]{1,0:T(8,128)(2,1)S(1)} reduce(bf16[64,1,2560]{2,1,0:T(2,128)(2,1)} %convert_element_type.91, bf16[]{:T(256)} %broadcast.42), dimensions={1}, to_apply=%convert_element_type.91.reduce_sub_computation | reduce | bytes 655362 | tf_op jit(solution)/shard_map/convert_element_type | solution.py:143
  11.8 0.8 reshape.78
  12.6 19.0 %all-to-all-start = ((bf16[64,2,1280]{2,1,0:T(2,128)(2,1)}), bf16[64,2,1280]{2,1,0:T(2,128)(2,1)}, u32[]{:S(2)}, u32[]{:S(2)}) async-start(bf16[64,2,1280]{2,1,0:T(2,128)(2,1)} %reshape.78), calls=%async_computation | async-start | bytes 655360 | tf_op jit(solution)/shard_map/all_to_all | solution.py:145
  31.5 1.9 %pad_maximum_fusion = f32[2,16,5120]{2,1,0:T(8,128)} fusion(f32[1,16,5120]{2,1,0:T(8,128)S(1)} %fusion, f32[1,16,5120]{2,1,0:T(8,128)} %copy-done.4), kind=kLoop, calls=%fused_computation.34 | loop fusion | flops 163840 | bytes 1310720 | tf_op jit(solution)/shard_map/stack | solution.py:58
  33.4 1.2 reshape.71
  34.6 2.1 %fusion.7 = (f32[128]{0:T(128)S(1)}, f32[128,5120]{1,0:T(8,128)}) fusion(bf16[1,128,5120]{2,1,0:T(8,128)(2,1)S(1)} %copy-done.1, f32[128]{0:T(128)S(1)} %add_rsqrt_fusion, f32[5120]{0:T(1024)S(1)} %bitcast.88, bf16[128,16]{0,1:T(8,128)(2,1)S(1)} %fusion.31, bf16[1,16,5120]{2,1,0:T(8,128)(2,1)S(1)} %copy-done), kind=kOutput, calls=%fused_computation.12 | convolution fusion | flops 24248192 | bytes 4121600 | tf_op jit(solution)/shard_map/tk,kd->td/dot_general | solution.py:53
  36.7 0.8 subtract_convert_fusion
  37.5 17.6 %all-to-all-done = bf16[64,2,1280]{2,1,0:T(2,128)(2,1)} async-done(((bf16[64,2,1280]{2,1,0:T(2,128)(2,1)}), bf16[64,2,1280]{2,1,0:T(2,128)(2,1)}, u32[]{:S(2)}, u32[]{:S(2)}) %all-to-all-start) | async-done | bytes 327712 | tf_op jit(solution)/shard_map/all_to_all | solution.py:145
  55.1 3.2 %reshape.79 = bf16[64,1,2560]{2,1,0:T(2,128)(2,1)} reshape(bf16[64,2,1280]{2,1,0:T(2,128)(2,1)} %all-to-all-done) | data formatting | bytes 655360
  58.3 1.1 copy.23
  59.7 1.1 concatenate.3
  60.8 1.6 %reduce.1 = bf16[64,2816]{1,0:T(8,128)(2,1)} reduce(bf16[64,1,2816]{2,0,1:T(8,128)(2,1)S(1)} %bitcast.82, bf16[]{:T(256)} %broadcast.42), dimensions={1}, to_apply=%copy.15.reduce_sub_computation | reduce | bytes 720898 | tf_op jit(solution)/shard_map/all_to_all | solution.py:157
  62.4 1.8 %reshape.80 = bf16[64,2,1408]{2,1,0:T(2,128)(2,1)} reshape(bf16[64,2816]{1,0:T(8,128)(2,1)} %reduce.1) | data formatting | bytes 720896
  64.2 6.5 %all-to-all-start.1 = ((bf16[64,2,1408]{2,1,0:T(2,128)(2,1)}), bf16[64,2,1408]{2,1,0:T(2,128)(2,1)S(1)}, u32[]{:S(2)}, u32[]{:S(2)}) async-start(bf16[64,2,1408]{2,1,0:T(2,128)(2,1)} %reshape.80), calls=%async_computation.1 | async-start | bytes 720896 | tf_op jit(solution)/shard_map/all_to_all | solution.py:157
  70.7 3.6 %fusion.20 = bf16[1,128,5120]{2,1,0:T(8,128)(2,1)} fusion(f32[128,5120]{1,0:T(8,128)} %get-tuple-element.6, bf16[1,128,5120]{2,1,0:T(8,128)(2,1)S(1)} %copy-done.1, bf16[1,128,5120]{2,1,0:T(8,128)(2,1)S(1)} %copy-done.2, f32[128]{0:T(128)S(1)} %broadcast_multiply_fusion, f32[128]{0:T(128)S(1)} %add_rsqrt_fusion), kind=kLoop, calls=%fused_computation.23 | loop fusion | flops 5242880 | bytes 6554624 | tf_op jit(solution)/shard_map/broadcast_in_dim | solution.py:175
  74.2 1.9 %collective-permute-start = (bf16[1,128,5120]{2,1,0:T(8,128)(2,1)}, bf16[1,128,5120]{2,1,0:T(8,128)(2,1)S(1)}, u32[]{:S(2)}, u32[]{:S(2)}) collective-permute-start(bf16[1,128,5120]{2,1,0:T(8,128)(2,1)} %fusion.20), channel_id=1, source_target_pairs={{64,0},{128,64},{192,128},{256,192},{320,256},{384,320},{448,384},... | collective-permute-start | bytes 3932168 | tf_op jit(solution)/shard_map/ppermute | solution.py:23
  76.2 18.9 %all-to-all-done.1 = bf16[64,2,1408]{2,1,0:T(2,128)(2,1)S(1)} async-done(((bf16[64,2,1408]{2,1,0:T(2,128)(2,1)}), bf16[64,2,1408]{2,1,0:T(2,128)(2,1)S(1)}, u32[]{:S(2)}, u32[]{:S(2)}) %all-to-all-start.1) | async-done | bytes 360480 | tf_op jit(solution)/shard_map/all_to_all | solution.py:157
  95.0 0.3 reshape.81
  95.7 0.6 broadcast_in_dim.21
  96.3 6.6 %all-to-all-start.2 = ((f32[64,1,128]{2,1,0:T(1,128)}), f32[64,1,128]{2,1,0:T(1,128)S(1)}, u32[]{:S(2)}, u32[]{:S(2)}) async-start(f32[64,1,128]{2,1,0:T(1,128)} %broadcast_in_dim.21), calls=%async_computation.2 | async-start | bytes 65536 | tf_op jit(solution)/shard_map/all_to_all | solution.py:163
  103.0 0.7 slice.24.low_ref
  103.7 13.7 %all-to-all-done.2 = f32[64,1,128]{2,1,0:T(1,128)S(1)} async-done(((f32[64,1,128]{2,1,0:T(1,128)}), f32[64,1,128]{2,1,0:T(1,128)S(1)}, u32[]{:S(2)}, u32[]{:S(2)}) %all-to-all-start.2) | async-done | bytes 32800 | tf_op jit(solution)/shard_map/all_to_all | solution.py:163
  117.4 0.6 broadcast_in_dim.22.sel_ref
  118.0 4.7 %shard_map.77 = bf16[1,2560]{1,0:T(2,128)(2,1)} custom-call(f32[64,64]{1,0:T(8,128)} %constant.42.clone.start_ref, f32[64,128]{1,0:T(8,128)} %bitcast.84, f32[8,128]{1,0:T(8,128)} %broadcast_in_dim.22.sel_ref, bf16[64,2560]{1,0:T(8,128)(2,1)} %bitcast.79, bf16[64,2560]{1,0:T(8,128)(2,1)} %slice.24.low_ref), custom_call_target="tpu_custom_call" | custom-call | tf_op jit(solution)/shard_map/pallas_call | solution.py:123
  122.7 1.1 copy.26
  (26 shorter events, 0.7 us)
Async XLA Ops:
  0.6 3.6 %copy-start = (bf16[1,16,5120]{2,1,0:T(8,128)(2,1)S(1)}, bf16[1,16,5120]{2,1,0:T(8,128)(2,1)}, u32[]{:S(2)}) copy-start(bf16[1,16,5120]{2,1,0:T(8,128)(2,1)} %param.9) | copy-start | bytes 491524
  0.6 3.6 %copy-start.1 = (bf16[1,128,5120]{2,1,0:T(8,128)(2,1)S(1)}, bf16[1,128,5120]{2,1,0:T(8,128)(2,1)}, u32[]{:S(2)}) copy-start(bf16[1,128,5120]{2,1,0:T(8,128)(2,1)} %param.6) | copy-start | bytes 3932164
  0.7 3.6 %copy-start.2 = (bf16[1,128,5120]{2,1,0:T(8,128)(2,1)S(1)}, bf16[1,128,5120]{2,1,0:T(8,128)(2,1)}, u32[]{:S(2)}) copy-start(bf16[1,128,5120]{2,1,0:T(8,128)(2,1)} %param.7) | copy-start | bytes 3932164
  0.7 3.6 %copy-start.6 = (f32[1,5120]{1,0:T(1,128)S(1)}, f32[1,5120]{1,0:T(1,128)}, u32[]{:S(2)}) copy-start(f32[1,5120]{1,0:T(1,128)} %param.8) | copy-start | bytes 61444
  5.9 0.7 copy-start.4
  12.6 42.5 %all-to-all-start = ((bf16[64,2,1280]{2,1,0:T(2,128)(2,1)}), bf16[64,2,1280]{2,1,0:T(2,128)(2,1)}, u32[]{:S(2)}, u32[]{:S(2)}) async-start(bf16[64,2,1280]{2,1,0:T(2,128)(2,1)} %reshape.78), calls=%async_computation | async-start | bytes 655360 | tf_op jit(solution)/shard_map/all_to_all | solution.py:145
  59.5 14.8 %copy-start.3 = (bf16[64,1,2560]{2,0,1:T(8,128)(2,1)}, bf16[64,1,2560]{2,0,1:T(8,128)(2,1)S(1)}, u32[]{:S(2)}) copy-start(bf16[64,1,2560]{2,0,1:T(8,128)(2,1)S(1)} %copy.23) | copy-start | bytes 983044
  64.2 30.8 %all-to-all-start.1 = ((bf16[64,2,1408]{2,1,0:T(2,128)(2,1)}), bf16[64,2,1408]{2,1,0:T(2,128)(2,1)S(1)}, u32[]{:S(2)}, u32[]{:S(2)}) async-start(bf16[64,2,1408]{2,1,0:T(2,128)(2,1)} %reshape.80), calls=%async_computation.1 | async-start | bytes 720896 | tf_op jit(solution)/shard_map/all_to_all | solution.py:157
  74.2 28.7 %collective-permute-start = (bf16[1,128,5120]{2,1,0:T(8,128)(2,1)}, bf16[1,128,5120]{2,1,0:T(8,128)(2,1)S(1)}, u32[]{:S(2)}, u32[]{:S(2)}) collective-permute-start(bf16[1,128,5120]{2,1,0:T(8,128)(2,1)} %fusion.20), channel_id=1, source_target_pairs={{64,0},{128,64},{192,128},{256,192},{320,256},{384,320},{448,384},... | collective-permute-start | bytes 3932168 | tf_op jit(solution)/shard_map/ppermute | solution.py:23
  96.3 21.1 %all-to-all-start.2 = ((f32[64,1,128]{2,1,0:T(1,128)}), f32[64,1,128]{2,1,0:T(1,128)S(1)}, u32[]{:S(2)}, u32[]{:S(2)}) async-start(f32[64,1,128]{2,1,0:T(1,128)} %broadcast_in_dim.21), calls=%async_computation.2 | async-start | bytes 65536 | tf_op jit(solution)/shard_map/all_to_all | solution.py:163
  117.4 0.6 copy-start.5

commit v9 on v8

--- a/solution.py
+++ b/solution.py
@@ -112,7 +112,8 @@
     column = lax.dot_general(
         eye, row, (((1,), (1,)), ((), ())), precision=HIGH, preferred_element_type=jnp.float32
     )
-    chunks = high_ref[...].astype(jnp.float32) + low_ref[...].astype(jnp.float32)
+    width = high_ref.shape[1]
+    chunks = high_ref[...].astype(jnp.float32) + low_ref[:, 0:width].astype(jnp.float32)
     combined = jnp.sum(column * chunks, axis=0, keepdims=True)
     out_ref[...] = combined.astype(out_ref.dtype)
 
@@ -127,12 +128,16 @@
     )(jnp.asarray(bit_reversed_eye(n)), gram_rows, sel, high_chunks, low_chunks)
 
 
+def to_bf16_grid(x):
+    return lax.reduce_precision(x, exponent_bits=8, mantissa_bits=7)
+
+
 def split_three(x):
-    one = x.astype(jnp.bfloat16)
-    rest = x - one.astype(jnp.float32)
-    two = rest.astype(jnp.bfloat16)
-    three = (rest - two.astype(jnp.float32)).astype(jnp.bfloat16)
-    return one, two, three
+    one = to_bf16_grid(x)
+    rest = x - one
+    two = to_bf16_grid(rest)
+    three = rest - two
+    return [part.astype(jnp.bfloat16) for part in (one, two, three)]
 
 
 def gram_adasum(grad_pair):
@@ -140,8 +145,9 @@
     me = lax.axis_index("dp")
     flat = grad_pair.reshape(devices, -1)
     width = flat.shape[1]
-    high = flat.astype(jnp.bfloat16)
-    low = (flat - high.astype(jnp.float32)).astype(jnp.bfloat16)
+    high_grid = to_bf16_grid(flat)
+    high = high_grid.astype(jnp.bfloat16)
+    low = (flat - high_grid).astype(jnp.bfloat16)
     high_chunks = lax.all_to_all(high, "dp", 0, 0, tiled=True)
     tensors = grad_pair.shape[0]
     per_tensor = devices // tensors
@@ -155,13 +161,12 @@
         [low, *split_three(partial), jnp.zeros((devices, pad), jnp.bfloat16)], axis=1
     )
     got = lax.all_to_all(payload, "dp", 0, 0, tiled=True)
-    low_chunks = got[:, :width]
     pieces = got[:, width:width + 3 * n].astype(jnp.float32).reshape(devices, 3, n)
     row_parts = (pieces[:, 0] + pieces[:, 1]) + pieces[:, 2]
     rows = jnp.sum(row_parts.reshape(tensors, per_tensor, n), axis=1)
     spread = jnp.broadcast_to(rows.reshape(1, -1), (devices, tensors * n))
     gram_rows = lax.all_to_all(spread, "dp", 0, 0, tiled=True)
-    return combine(gram_rows, mine == 0, high_chunks, low_chunks)
+    return combine(gram_rows, mine == 0, high_chunks, got)
 
 
 def per_device(activations, upstream, section_norm_gain, adapter_down_weight, adapter_up_weight):

time: 125 us -> 128 us (1.024)
  waiting for transfers between devices: 50.2 us -> 53 us
    all_to_all x1, waiting for transfers between devices: 17.6 us -> 19.7 us  [gram_adasum(): high_chunks = lax.all_to_all(high, 'dp', 0, 0, tiled=True)]
    another operation x1 -> x0, other arithmetic: 1.85 us -> none  [replica_backward(): return (passed.astype(jnp.bfloat16), jnp.stack([down_term, upward_term]))]
    convert_element_type x3, other arithmetic: 4.34 us -> 5.83 us  [the longest x2 5.05 us: gram_adasum(): high = high_grid.astype(jnp.bfloat16)]
    unnamed x21 -> x25, local copies, waits for them, and re-layouts: 9.16 us -> 9.86 us
  transfers between devices with their start and end apart: 4 -> 4, of which waited for: 3 -> 3; matrix products, arithmetic and copies ran while one was open for 9% -> 7% of each run, Pallas kernels for 0% -> 0%
where the time goes in v9:
time: 128 us
  waiting for transfers between devices  53 us (41%)
  starting transfers between devices  33.9 us (26%)
  local copies, waits for them, and re-layouts  15.8 us (12%)
  other arithmetic  12.9 us (10%)
  matrix products  6.45 us (5%)
  Pallas kernels  4.73 us (4%)
    all_to_all x1, waiting for transfers between devices, gram_adasum(): high_chunks = lax.all_to_all(high, 'dp', 0, 0, tiled=True)  19.7 us
    all_to_all x1, starting transfers between devices, gram_adasum(): high_chunks = lax.all_to_all(high, 'dp', 0, 0, tiled=True)  19 us
    all_to_all x1, waiting for transfers between devices, gram_adasum(): got = lax.all_to_all(payload, 'dp', 0, 0, tiled=True)  18.9 us
    all_to_all x1, waiting for transfers between devices, gram_adasum(): gram_rows = lax.all_to_all(spread, 'dp', 0, 0, tiled=True)  14.4 us
    unnamed x25, local copies, waits for them, and re-layouts  9.86 us
    all_to_all x1, starting transfers between devices, gram_adasum(): gram_rows = lax.all_to_all(spread, 'dp', 0, 0, tiled=True)  6.59 us
    all_to_all x1, starting transfers between devices, gram_adasum(): got = lax.all_to_all(payload, 'dp', 0, 0, tiled=True)  6.48 us
    convert_element_type x2, other arithmetic, gram_adasum(): high = high_grid.astype(jnp.bfloat16)  5.05 us
  transfers between devices with their start and end apart: 4, of which 3 were waited for; matrix products, arithmetic and copies ran while one was open for 7% of the time, Pallas kernels for 0%

profile of v9, /device:TPU:6, one launch (start us, length us, event | category | flops | bytes accessed | tf_op | source)
XLA Modules:
  0.0 127.6 jit_solution(15128123459384523451)
XLA Ops:
  0.7 1.8 %fusion.13 = f32[128]{0:T(128)S(1)} fusion(bf16[1,128,5120]{2,1,0:T(8,128)(2,1)} %param.6), kind=kLoop, calls=%fused_computation.18 | loop fusion | flops 1965952 | bytes 1311232 | tf_op jit(solution)/shard_map/reduce_sum | solution.py:28
  2.5 1.8 %fusion.31 = bf16[128,16]{0,1:T(8,128)(2,1)S(1)} fusion(bf16[1,128,5120]{2,1,0:T(8,128)(2,1)} %param.7, bf16[1,16,5120]{2,1,0:T(8,128)(2,1)} %param.10), kind=kOutput, calls=%fused_computation.32 | convolution fusion | flops 20975616 | bytes 1478656 | tf_op jit(solution)/shard_map/sh,gh->sg/dot_general | solution.py:44
  4.3 1.9 %fusion = f32[1,16,5120]{2,1,0:T(8,128)} fusion(bf16[1,128,5120]{2,1,0:T(8,128)(2,1)S(1)} %copy-done.2, bf16[1,128,5120]{2,1,0:T(8,128)(2,1)S(1)} %copy-done.1, f32[5120]{0:T(1024)S(1)} %bitcast.86, f32[128]{0:T(128)S(1)} %add_rsqrt_fusion, bf16[1,16,5120]{2,1,0:T(8,128)(2,1)S(1)} %copy-done), kind=kOutput, calls=%fused_computation.2 | convolution fusion | flops 44648448 | bytes 3133952 | tf_op jit(solution)/shard_map/tk,td->kd/dot_general | solution.py:37
  6.2 0.5 fusion.1
  6.7 0.5 copy-done.6
  7.1 0.8 reduce-precision_convert_fusion
  7.9 1.9 %convert_element_type.76 = bf16[64,1,2560]{2,1,0:T(2,128)(2,1)} reshape(bf16[2,16,5120]{2,1,0:T(8,128)(2,1)} %get-tuple-element.2) | data formatting | bytes 655360 | tf_op jit(solution)/shard_map/convert_element_type | solution.py:149
  9.8 0.5 broadcast.42
  10.3 4.3 %reduce = bf16[64,2560]{1,0:T(8,128)(2,1)} reduce(bf16[64,1,2560]{2,1,0:T(2,128)(2,1)} %convert_element_type.76, bf16[]{:T(256)} %broadcast.42), dimensions={1}, to_apply=%convert_element_type.76.reduce_sub_computation | reduce | bytes 655362 | tf_op jit(solution)/shard_map/convert_element_type | solution.py:149
  14.6 1.8 %reshape.82 = bf16[64,2,1280]{2,1,0:T(2,128)(2,1)} reshape(bf16[64,2560]{1,0:T(8,128)(2,1)} %reduce) | data formatting | bytes 655360
  16.4 19.0 %all-to-all-start = ((bf16[64,2,1280]{2,1,0:T(2,128)(2,1)}), bf16[64,2,1280]{2,1,0:T(2,128)(2,1)}, u32[]{:S(2)}, u32[]{:S(2)}) async-start(bf16[64,2,1280]{2,1,0:T(2,128)(2,1)} %reshape.82), calls=%async_computation | async-start | bytes 655360 | tf_op jit(solution)/shard_map/all_to_all | solution.py:151
  35.3 0.9 reshape.75
  36.3 2.1 %fusion.7 = (f32[128]{0:T(128)S(1)}, f32[128,5120]{1,0:T(8,128)}) fusion(bf16[1,128,5120]{2,1,0:T(8,128)(2,1)S(1)} %copy-done.1, f32[128]{0:T(128)S(1)} %add_rsqrt_fusion, f32[5120]{0:T(1024)S(1)} %bitcast.88, bf16[128,16]{0,1:T(8,128)(2,1)S(1)} %fusion.31, bf16[1,16,5120]{2,1,0:T(8,128)(2,1)S(1)} %copy-done), kind=kOutput, calls=%fused_computation.12 | convolution fusion | flops 24248192 | bytes 4121600 | tf_op jit(solution)/shard_map/tk,kd->td/dot_general | solution.py:53
  38.4 0.8 fusion.39
  39.2 19.7 %all-to-all-done = bf16[64,2,1280]{2,1,0:T(2,128)(2,1)} async-done(((bf16[64,2,1280]{2,1,0:T(2,128)(2,1)}), bf16[64,2,1280]{2,1,0:T(2,128)(2,1)}, u32[]{:S(2)}, u32[]{:S(2)}) %all-to-all-start) | async-done | bytes 327712 | tf_op jit(solution)/shard_map/all_to_all | solution.py:151
  58.9 3.2 %reshape.83 = bf16[64,1,2560]{2,1,0:T(2,128)(2,1)} reshape(bf16[64,2,1280]{2,1,0:T(2,128)(2,1)} %all-to-all-done) | data formatting | bytes 655360
  62.1 1.1 copy.23
  63.2 0.2 fusion.44
  63.5 1.1 concatenate.3
  64.6 1.6 %reduce.1 = bf16[64,2816]{1,0:T(8,128)(2,1)} reduce(bf16[64,1,2816]{2,0,1:T(8,128)(2,1)S(1)} %bitcast.82, bf16[]{:T(256)} %broadcast.42), dimensions={1}, to_apply=%copy.15.reduce_sub_computation | reduce | bytes 720898 | tf_op jit(solution)/shard_map/all_to_all | solution.py:163
  66.2 1.8 %reshape.84 = bf16[64,2,1408]{2,1,0:T(2,128)(2,1)} reshape(bf16[64,2816]{1,0:T(8,128)(2,1)} %reduce.1) | data formatting | bytes 720896
  68.0 6.5 %all-to-all-start.1 = ((bf16[64,2,1408]{2,1,0:T(2,128)(2,1)}), bf16[64,2,1408]{2,1,0:T(2,128)(2,1)S(1)}, u32[]{:S(2)}, u32[]{:S(2)}) async-start(bf16[64,2,1408]{2,1,0:T(2,128)(2,1)} %reshape.84), calls=%async_computation.1 | async-start | bytes 720896 | tf_op jit(solution)/shard_map/all_to_all | solution.py:163
  74.5 3.6 %fusion.20 = bf16[1,128,5120]{2,1,0:T(8,128)(2,1)} fusion(f32[128,5120]{1,0:T(8,128)} %get-tuple-element.8, bf16[1,128,5120]{2,1,0:T(8,128)(2,1)S(1)} %copy-done.1, bf16[1,128,5120]{2,1,0:T(8,128)(2,1)S(1)} %copy-done.2, f32[128]{0:T(128)S(1)} %broadcast_multiply_fusion, f32[128]{0:T(128)S(1)} %add_rsqrt_fusion), kind=kLoop, calls=%fused_computation.23 | loop fusion | flops 5242880 | bytes 6554624 | tf_op jit(solution)/shard_map/broadcast_in_dim | solution.py:180
  78.0 1.9 %collective-permute-start = (bf16[1,128,5120]{2,1,0:T(8,128)(2,1)}, bf16[1,128,5120]{2,1,0:T(8,128)(2,1)S(1)}, u32[]{:S(2)}, u32[]{:S(2)}) collective-permute-start(bf16[1,128,5120]{2,1,0:T(8,128)(2,1)} %fusion.20), channel_id=1, source_target_pairs={{64,0},{128,64},{192,128},{256,192},{320,256},{384,320},{448,384},... | collective-permute-start | bytes 3932168 | tf_op jit(solution)/shard_map/ppermute | solution.py:23
  80.0 18.9 %all-to-all-done.1 = bf16[64,2,1408]{2,1,0:T(2,128)(2,1)S(1)} async-done(((bf16[64,2,1408]{2,1,0:T(2,128)(2,1)}), bf16[64,2,1408]{2,1,0:T(2,128)(2,1)S(1)}, u32[]{:S(2)}, u32[]{:S(2)}) %all-to-all-start.1) | async-done | bytes 360480 | tf_op jit(solution)/shard_map/all_to_all | solution.py:163
  98.8 0.3 reshape.85
  99.5 0.6 broadcast_in_dim.21
  100.1 6.6 %all-to-all-start.2 = ((f32[64,1,128]{2,1,0:T(1,128)}), f32[64,1,128]{2,1,0:T(1,128)S(1)}, u32[]{:S(2)}, u32[]{:S(2)}) async-start(f32[64,1,128]{2,1,0:T(1,128)} %broadcast_in_dim.21), calls=%async_computation.2 | async-start | bytes 65536 | tf_op jit(solution)/shard_map/all_to_all | solution.py:168
  106.8 14.4 %all-to-all-done.2 = f32[64,1,128]{2,1,0:T(1,128)S(1)} async-done(((f32[64,1,128]{2,1,0:T(1,128)}), f32[64,1,128]{2,1,0:T(1,128)S(1)}, u32[]{:S(2)}, u32[]{:S(2)}) %all-to-all-start.2) | async-done | bytes 32800 | tf_op jit(solution)/shard_map/all_to_all | solution.py:168
  121.2 0.6 broadcast_in_dim.22.sel_ref
  121.8 4.7 %shard_map.77 = bf16[1,2560]{1,0:T(2,128)(2,1)} custom-call(f32[64,64]{1,0:T(8,128)} %constant.42.clone.start_ref, f32[64,128]{1,0:T(8,128)} %bitcast.84, f32[8,128]{1,0:T(8,128)} %broadcast_in_dim.22.sel_ref, bf16[64,2560]{1,0:T(8,128)(2,1)} %bitcast.79, bf16[64,2816]{1,0:T(8,128)(2,1)} %bitcast.81), custom_call_target="tpu_custom_call" | custom-call | tf_op jit(solution)/shard_map/pallas_call | solution.py:124
  126.6 1.1 copy.26
  (28 shorter events, 0.4 us)
Async XLA Ops:
  0.6 3.6 %copy-start = (bf16[1,16,5120]{2,1,0:T(8,128)(2,1)S(1)}, bf16[1,16,5120]{2,1,0:T(8,128)(2,1)}, u32[]{:S(2)}) copy-start(bf16[1,16,5120]{2,1,0:T(8,128)(2,1)} %param.9) | copy-start | bytes 491524
  0.6 3.6 %copy-start.1 = (bf16[1,128,5120]{2,1,0:T(8,128)(2,1)S(1)}, bf16[1,128,5120]{2,1,0:T(8,128)(2,1)}, u32[]{:S(2)}) copy-start(bf16[1,128,5120]{2,1,0:T(8,128)(2,1)} %param.6) | copy-start | bytes 3932164
  0.7 3.6 %copy-start.2 = (bf16[1,128,5120]{2,1,0:T(8,128)(2,1)S(1)}, bf16[1,128,5120]{2,1,0:T(8,128)(2,1)}, u32[]{:S(2)}) copy-start(bf16[1,128,5120]{2,1,0:T(8,128)(2,1)} %param.7) | copy-start | bytes 3932164
  0.7 3.6 %copy-start.8 = (f32[1,5120]{1,0:T(1,128)S(1)}, f32[1,5120]{1,0:T(1,128)}, u32[]{:S(2)}) copy-start(f32[1,5120]{1,0:T(1,128)} %param.8) | copy-start | bytes 61444
  6.2 1.0 copy-start.6
  16.4 42.5 %all-to-all-start = ((bf16[64,2,1280]{2,1,0:T(2,128)(2,1)}), bf16[64,2,1280]{2,1,0:T(2,128)(2,1)}, u32[]{:S(2)}, u32[]{:S(2)}) async-start(bf16[64,2,1280]{2,1,0:T(2,128)(2,1)} %reshape.82), calls=%async_computation | async-start | bytes 655360 | tf_op jit(solution)/shard_map/all_to_all | solution.py:151
  36.3 2.1 %copy-start.4 = (f32[64,2560]{1,0:T(8,128)S(1)}, f32[64,2560]{1,0:T(8,128)}, u32[]{:S(2)}) copy-start(f32[64,2560]{1,0:T(8,128)} %reshape.75) | copy-start | bytes 1966084
  63.2 14.8 %copy-start.3 = (bf16[64,1,2560]{2,0,1:T(8,128)(2,1)}, bf16[64,1,2560]{2,0,1:T(8,128)(2,1)S(1)}, u32[]{:S(2)}) copy-start(bf16[64,1,2560]{2,0,1:T(8,128)(2,1)S(1)} %copy.23) | copy-start | bytes 983044
  68.0 30.8 %all-to-all-start.1 = ((bf16[64,2,1408]{2,1,0:T(2,128)(2,1)}), bf16[64,2,1408]{2,1,0:T(2,128)(2,1)S(1)}, u32[]{:S(2)}, u32[]{:S(2)}) async-start(bf16[64,2,1408]{2,1,0:T(2,128)(2,1)} %reshape.84), calls=%async_computation.1 | async-start | bytes 720896 | tf_op jit(solution)/shard_map/all_to_all | solution.py:163
  78.0 28.7 %collective-permute-start = (bf16[1,128,5120]{2,1,0:T(8,128)(2,1)}, bf16[1,128,5120]{2,1,0:T(8,128)(2,1)S(1)}, u32[]{:S(2)}, u32[]{:S(2)}) collective-permute-start(bf16[1,128,5120]{2,1,0:T(8,128)(2,1)} %fusion.20), channel_id=1, source_target_pairs={{64,0},{128,64},{192,128},{256,192},{320,256},{384,320},{448,384},... | collective-permute-start | bytes 3932168 | tf_op jit(solution)/shard_map/ppermute | solution.py:23
  99.2 22.6 %copy-start.5 = (bf16[64,1,2816]{2,0,1:T(8,128)(2,1)}, bf16[64,1,2816]{2,0,1:T(8,128)(2,1)S(1)}, u32[]{:S(2)}) copy-start(bf16[64,1,2816]{2,0,1:T(8,128)(2,1)S(1)} %copy.22) | copy-start | bytes 1081348
  100.1 21.1 %all-to-all-start.2 = ((f32[64,1,128]{2,1,0:T(1,128)}), f32[64,1,128]{2,1,0:T(1,128)S(1)}, u32[]{:S(2)}, u32[]{:S(2)}) async-start(f32[64,1,128]{2,1,0:T(1,128)} %broadcast_in_dim.21), calls=%async_computation.2 | async-start | bytes 65536 | tf_op jit(solution)/shard_map/all_to_all | solution.py:168
  121.2 0.6 copy-start.7

commit v10 on v6

--- a/solution.py
+++ b/solution.py
@@ -86,7 +86,7 @@
     return np.eye(n, dtype=np.float32)[order]
 
 
-def combine_kernel(start_ref, gram_ref, sel_ref, chunks_ref, out_ref):
+def combine_kernel(start_ref, gram_ref, chunks_ref, out_ref):
     n = gram_ref.shape[0]
     finals = []
     for t in range(gram_ref.shape[1] // n):
@@ -104,7 +104,7 @@
             take_coef = 1.0 - inner_sum / (2.0 * (far_square + pair_eps))
             coef = keep_coef * first + take_coef * second
         finals.append(coef)
-    sel = sel_ref[0:1, 0:n]
+    sel = jnp.where(lax.axis_index("dp") < lax.axis_size("dp") // 2, 1.0, 0.0)
     row = sel * finals[0] + (1.0 - sel) * finals[1]
     eye = start_ref[...] * 0.0 + (
         lax.broadcasted_iota(jnp.int32, (n, n), 0) == lax.broadcasted_iota(jnp.int32, (n, n), 1)
@@ -116,17 +116,16 @@
     out_ref[...] = combined.astype(out_ref.dtype)
 
 
-def combine(gram_rows, first_tensor, chunks, interpret=False):
+def combine(gram_rows, chunks, interpret=False):
     n = gram_rows.shape[0]
-    sel = jnp.broadcast_to(first_tensor.astype(jnp.float32), (8, 128))
     return pl.pallas_call(
         combine_kernel,
         out_shape=jax.ShapeDtypeStruct((1, chunks.shape[1]), jnp.bfloat16),
         interpret=interpret,
-    )(jnp.asarray(bit_reversed_eye(n)), gram_rows, sel, chunks)
+    )(jnp.asarray(bit_reversed_eye(n)), gram_rows, chunks)
 
 
-def gram_adasum(grad_pair):
+def gram_adasum(grad_pair, passed):
     devices = lax.axis_size("dp")
     me = lax.axis_index("dp")
     flat = grad_pair.reshape(devices, -1)
@@ -138,8 +137,11 @@
     rows = lax.all_to_all(partial[:, None, :], "dp", 0, 0, tiled=True)
     rows = jnp.sum(rows.reshape(tensors, per_tensor, partial.shape[1]), axis=1)
     spread = jnp.broadcast_to(rows.reshape(1, -1), (devices, tensors * partial.shape[1]))
+    spread, passed = lax.optimization_barrier((spread, passed))
+    has_next = lax.axis_index("section") < lax.axis_size("section") - 1
+    passed = jnp.where(has_next, passed, jnp.zeros_like(passed))
     gram_rows = lax.all_to_all(spread, "dp", 0, 0, tiled=True)
-    return combine(gram_rows, mine == 0, chunks)
+    return combine(gram_rows, chunks), passed
 
 
 def per_device(activations, upstream, section_norm_gain, adapter_down_weight, adapter_up_weight):
@@ -151,7 +153,7 @@
         adapter_up_weight[0],
     )
     shifted = from_behind(passed_local[None], "section", -1)
-    merged_gradient = gram_adasum(grad_pair)
+    merged_gradient, shifted = gram_adasum(grad_pair, shifted)
     return (shifted, merged_gradient)
 
 

time: 113 us -> 114 us (level)
  blocking collectives: 20.7 us -> 0 us
  waiting for transfers between devices: 46.3 us -> 59.8 us
  starting transfers between devices: 25.2 us -> 31.6 us
  other arithmetic: 3.77 us -> 5.99 us
  local copies, waits for them, and re-layouts: 5.38 us -> 3.87 us
  matrix products: 5.52 us -> 6.85 us
    all_to_all x1 -> x0, blocking collectives: 20.7 us -> none  [gram_adasum(): rows = lax.all_to_all(partial[:, None, :], 'dp', 0, 0, tiled=True)]
    all_to_all x0 -> x1, waiting for transfers between devices: none -> 13.6 us  [gram_adasum(): rows = lax.all_to_all(partial[:, None, :], 'dp', 0, 0, tiled=True)]
    all_to_all x0 -> x1, starting transfers between devices: none -> 6.46 us  [gram_adasum(): rows = lax.all_to_all(partial[:, None, :], 'dp', 0, 0, tiled=True)]
    select_n x0 -> x1, other arithmetic: none -> 1.15 us  [gram_adasum(): passed = jnp.where(has_next, passed, jnp.zeros_like(passed))]
    unnamed x14 -> x11, local copies, waits for them, and re-layouts: 2.46 us -> 1.54 us
  transfers between devices with their start and end apart: 3 -> 4, of which waited for: 2 -> 3; matrix products, arithmetic and copies ran while one was open for 4% -> 5% of each run, Pallas kernels for 0% -> 0%
where the time goes in v10:
time: 114 us
  waiting for transfers between devices  59.8 us (52%)
  starting transfers between devices  31.6 us (28%)
  matrix products  6.85 us (6%)
  other arithmetic  5.99 us (5%)
  Pallas kernels  4.7 us (4%)
  local copies, waits for them, and re-layouts  3.87 us (3%)
    all_to_all x1, waiting for transfers between devices, gram_adasum(): chunks = lax.all_to_all(flat, 'dp', 0, 0, tiled=True)  32.9 us
    all_to_all x1, starting transfers between devices, gram_adasum(): chunks = lax.all_to_all(flat, 'dp', 0, 0, tiled=True)  18.7 us
    all_to_all x1, waiting for transfers between devices, gram_adasum(): rows = lax.all_to_all(partial[:, None, :], 'dp', 0, 0, tiled=True)  13.6 us
    all_to_all x1, waiting for transfers between devices, gram_adasum(): gram_rows = lax.all_to_all(spread, 'dp', 0, 0, tiled=True)  13.3 us
    all_to_all x1, starting transfers between devices, gram_adasum(): rows = lax.all_to_all(partial[:, None, :], 'dp', 0, 0, tiled=True)  6.46 us
    pallas_call x1, Pallas kernels, combine(): pl.pallas_call(combine_kernel, out_shape=jax.ShapeDtypeStruct((1, chunks....  4.7 us
    all_to_all x1, starting transfers between devices, gram_adasum(): gram_rows = lax.all_to_all(spread, 'dp', 0, 0, tiled=True)  4.54 us
  transfers between devices with their start and end apart: 4, of which 3 were waited for; matrix products, arithmetic and copies ran while one was open for 5% of the time, Pallas kernels for 0%

profile of v10, /device:TPU:6, one launch (start us, length us, event | category | flops | bytes accessed | tf_op | source)
XLA Modules:
  0.0 113.6 jit_solution(1116891225240181555)
XLA Ops:
  0.6 0.0 copy-start
  0.6 0.0 copy-start.1
  0.7 0.0 copy-start.2
  0.7 0.0 copy-start.4
  0.7 1.8 %fusion.13 = f32[128]{0:T(128)S(1)} fusion(bf16[1,128,5120]{2,1,0:T(8,128)(2,1)} %param.6), kind=kLoop, calls=%fused_computation.18 | loop fusion | flops 1965952 | bytes 1311232 | tf_op jit(solution)/shard_map/reduce_sum | solution.py:28
  2.5 1.8 %fusion.34 = bf16[128,16]{0,1:T(8,128)(2,1)S(1)} fusion(bf16[1,128,5120]{2,1,0:T(8,128)(2,1)} %param.7, bf16[1,16,5120]{2,1,0:T(8,128)(2,1)} %param.10), kind=kOutput, calls=%fused_computation.34 | convolution fusion | flops 20975616 | bytes 1478656 | tf_op jit(solution)/shard_map/sh,gh->sg/dot_general | solution.py:44
  4.3 0.0 copy-done.1
  4.3 0.0 copy-done.4
  4.3 1.2 %fusion.1 = f32[1,16,5120]{2,1,0:T(8,128)} fusion(bf16[128,16]{0,1:T(8,128)(2,1)S(1)} %fusion.34, bf16[1,128,5120]{2,1,0:T(8,128)(2,1)S(1)} %copy-done.1, f32[5120]{0:T(1024)S(1)} %bitcast.81, f32[128]{0:T(128)S(1)} %add_rsqrt_fusion), kind=kOutput, calls=%fused_computation.4 | convolution fusion | flops 23674880 | bytes 1663488 | tf_op jit(solution)/shard_map/tk,td->kd/dot_general | solution.py:49
  5.5 0.0 copy-done
  5.5 0.0 copy-done.2
  5.5 1.9 %fusion = f32[1,16,5120]{2,1,0:T(8,128)} fusion(bf16[1,128,5120]{2,1,0:T(8,128)(2,1)S(1)} %copy-done.2, bf16[1,128,5120]{2,1,0:T(8,128)(2,1)S(1)} %copy-done.1, f32[5120]{0:T(1024)S(1)} %bitcast.82, f32[128]{0:T(128)S(1)} %add_rsqrt_fusion, bf16[1,16,5120]{2,1,0:T(8,128)(2,1)S(1)} %copy-done), kind=kOutput, calls=%fused_computation.2 | convolution fusion | flops 44648448 | bytes 3133952 | tf_op jit(solution)/shard_map/tk,td->kd/dot_general | solution.py:37
  7.4 1.1 pad_maximum_fusion
  8.5 1.6 %all_to_all.24 = f32[64,1,2560]{2,1,0:T(1,128)} reshape(f32[2,16,5120]{2,1,0:T(8,128)S(1)} %pad_maximum_fusion) | data formatting | bytes 1310720 | tf_op jit(solution)/shard_map/all_to_all | solution.py:132
  10.2 18.7 %all-to-all-start = ((f32[64,1,2560]{2,1,0:T(1,128)}), f32[64,1,2560]{2,1,0:T(1,128)S(1)}, u32[]{:S(2)}, u32[]{:S(2)}) async-start(f32[64,1,2560]{2,1,0:T(1,128)} %all_to_all.24), calls=%async_computation | async-start | bytes 1310720 | tf_op jit(solution)/shard_map/all_to_all | solution.py:132
  28.9 0.7 fusion.8
  29.6 1.9 %fusion.19 = bf16[1,128,5120]{2,1,0:T(8,128)(2,1)} fusion(f32[128,5120]{1,0:T(8,128)S(1)} %get-tuple-element.7, bf16[1,128,5120]{2,1,0:T(8,128)(2,1)S(1)} %copy-done.1, bf16[1,128,5120]{2,1,0:T(8,128)(2,1)S(1)} %copy-done.2, f32[128]{0:T(128)S(1)} %broadcast_multiply_fusion, f32[128]{0:T(128)S(1)} %add_rsqrt_fusion), kind=kLoop, calls=%fused_computation.23 | loop fusion | flops 5242880 | bytes 6554624 | tf_op jit(solution)/shard_map/broadcast_in_dim | solution.py:155
  31.5 1.9 %collective-permute-start = (bf16[1,128,5120]{2,1,0:T(8,128)(2,1)}, bf16[1,128,5120]{2,1,0:T(8,128)(2,1)S(1)}, u32[]{:S(2)}, u32[]{:S(2)}) collective-permute-start(bf16[1,128,5120]{2,1,0:T(8,128)(2,1)} %fusion.19), channel_id=1, source_target_pairs={{64,0},{128,64},{192,128},{256,192},{320,256},{384,320},{448,384},... | collective-permute-start | bytes 3932168 | tf_op jit(solution)/shard_map/ppermute | solution.py:23
  33.4 32.9 %all-to-all-done = f32[64,1,2560]{2,1,0:T(1,128)S(1)} async-done(((f32[64,1,2560]{2,1,0:T(1,128)}), f32[64,1,2560]{2,1,0:T(1,128)S(1)}, u32[]{:S(2)}, u32[]{:S(2)}) %all-to-all-start) | async-done | bytes 655392 | tf_op jit(solution)/shard_map/all_to_all | solution.py:132
  66.3 1.3 %fusion.43 = f32[64,64]{1,0:T(8,128)} fusion(f32[64,1,2560]{2,1,0:T(1,128)S(1)} %all-to-all-done), kind=kOutput, calls=%fused_computation.43 | convolution fusion | flops 125829120 | bytes 671744 | tf_op jit(solution)/shard_map/dot_general | solution.py:136
  67.6 6.5 %all-to-all-start.1 = ((f32[64,1,64]{2,1,0:T(1,128)}), f32[64,1,64]{2,1,0:T(1,128)S(1)}, u32[]{:S(2)}, u32[]{:S(2)}) async-start(f32[64,1,64]{2,1,0:T(1,128)} %bitcast.9), calls=%async_computation.1 | async-start | bytes 65536 | tf_op jit(solution)/shard_map/all_to_all | solution.py:137
  74.1 0.9 copy.13
  74.9 13.6 %all-to-all-done.1 = f32[64,1,64]{2,1,0:T(1,128)S(1)} async-done(((f32[64,1,64]{2,1,0:T(1,128)}), f32[64,1,64]{2,1,0:T(1,128)S(1)}, u32[]{:S(2)}, u32[]{:S(2)}) %all-to-all-start.1) | async-done | bytes 16416 | tf_op jit(solution)/shard_map/all_to_all | solution.py:137
  88.5 0.1 broadcast_in_dim.19
  88.6 0.0 collective-permute-done
  88.6 0.6 broadcast_in_dim.20
  89.2 4.5 %all-to-all-start.2 = ((f32[64,1,128]{2,1,0:T(1,128)}), f32[64,1,128]{2,1,0:T(1,128)S(1)}, u32[]{:S(2)}, u32[]{:S(2)}) async-start(f32[64,1,128]{2,1,0:T(1,128)} %bitcast.12), calls=%async_computation.2 | async-start | bytes 65536 | tf_op jit(solution)/shard_map/all_to_all | solution.py:143
  93.8 1.2 %broadcast_select_fusion = bf16[1,128,5120]{2,1,0:T(8,128)(2,1)} fusion(bf16[1,128,5120]{2,1,0:T(8,128)(2,1)S(1)} %collective-permute-done, pred[]{:T(512)S(6)} %lt.3), kind=kLoop, calls=%fused_computation.31 | loop fusion | flops 655360 | bytes 2621441 | tf_op jit(solution)/shard_map/jit(_where)/select_n | solution.py:142
  94.9 13.3 %all-to-all-done.2 = f32[64,1,128]{2,1,0:T(1,128)S(1)} async-done(((f32[64,1,128]{2,1,0:T(1,128)}), f32[64,1,128]{2,1,0:T(1,128)S(1)}, u32[]{:S(2)}, u32[]{:S(2)}) %all-to-all-start.2) | async-done | bytes 32800 | tf_op jit(solution)/shard_map/all_to_all | solution.py:143
  108.3 0.0 copy-start.3
  108.3 0.6 copy-done.3
  108.9 4.7 %shard_map.77 = bf16[1,2560]{1,0:T(2,128)(2,1)} custom-call(f32[64,64]{1,0:T(8,128)} %constant.29.clone.start_ref, f32[64,128]{1,0:T(8,128)} %bitcast.79, f32[64,2560]{1,0:T(8,128)} %bitcast.78), custom_call_target="tpu_custom_call" | custom-call | tf_op jit(solution)/shard_map/pallas_call | solution.py:121
  (3 shorter events, 0.0 us)
Async XLA Ops:
  0.6 4.9 %copy-start = (bf16[1,16,5120]{2,1,0:T(8,128)(2,1)S(1)}, bf16[1,16,5120]{2,1,0:T(8,128)(2,1)}, u32[]{:S(2)}) copy-start(bf16[1,16,5120]{2,1,0:T(8,128)(2,1)} %param.9) | copy-start | bytes 491524
  0.6 3.6 %copy-start.1 = (bf16[1,128,5120]{2,1,0:T(8,128)(2,1)S(1)}, bf16[1,128,5120]{2,1,0:T(8,128)(2,1)}, u32[]{:S(2)}) copy-start(bf16[1,128,5120]{2,1,0:T(8,128)(2,1)} %param.6) | copy-start | bytes 3932164
  0.7 4.8 %copy-start.2 = (bf16[1,128,5120]{2,1,0:T(8,128)(2,1)S(1)}, bf16[1,128,5120]{2,1,0:T(8,128)(2,1)}, u32[]{:S(2)}) copy-start(bf16[1,128,5120]{2,1,0:T(8,128)(2,1)} %param.7) | copy-start | bytes 3932164
  0.7 3.6 %copy-start.4 = (f32[1,5120]{1,0:T(1,128)S(1)}, f32[1,5120]{1,0:T(1,128)}, u32[]{:S(2)}) copy-start(f32[1,5120]{1,0:T(1,128)} %param.8) | copy-start | bytes 61444
  10.2 56.1 %all-to-all-start = ((f32[64,1,2560]{2,1,0:T(1,128)}), f32[64,1,2560]{2,1,0:T(1,128)S(1)}, u32[]{:S(2)}, u32[]{:S(2)}) async-start(f32[64,1,2560]{2,1,0:T(1,128)} %all_to_all.24), calls=%async_computation | async-start | bytes 1310720 | tf_op jit(solution)/shard_map/all_to_all | solution.py:132
  31.5 57.1 %collective-permute-start = (bf16[1,128,5120]{2,1,0:T(8,128)(2,1)}, bf16[1,128,5120]{2,1,0:T(8,128)(2,1)S(1)}, u32[]{:S(2)}, u32[]{:S(2)}) collective-permute-start(bf16[1,128,5120]{2,1,0:T(8,128)(2,1)} %fusion.19), channel_id=1, source_target_pairs={{64,0},{128,64},{192,128},{256,192},{320,256},{384,320},{448,384},... | collective-permute-start | bytes 3932168 | tf_op jit(solution)/shard_map/ppermute | solution.py:23
  67.6 20.9 %all-to-all-start.1 = ((f32[64,1,64]{2,1,0:T(1,128)}), f32[64,1,64]{2,1,0:T(1,128)S(1)}, u32[]{:S(2)}, u32[]{:S(2)}) async-start(f32[64,1,64]{2,1,0:T(1,128)} %bitcast.9), calls=%async_computation.1 | async-start | bytes 65536 | tf_op jit(solution)/shard_map/all_to_all | solution.py:137
  89.2 19.0 %all-to-all-start.2 = ((f32[64,1,128]{2,1,0:T(1,128)}), f32[64,1,128]{2,1,0:T(1,128)S(1)}, u32[]{:S(2)}, u32[]{:S(2)}) async-start(f32[64,1,128]{2,1,0:T(1,128)} %bitcast.12), calls=%async_computation.2 | async-start | bytes 65536 | tf_op jit(solution)/shard_map/all_to_all | solution.py:143
  108.3 0.6 copy-start.3

commit v11 on v6

--- a/solution.py
+++ b/solution.py
@@ -78,6 +78,42 @@
         take_coef = 1.0 - inner_sum / (2.0 * (far_square + pair_eps))
         coef = keep_coef * coef + take_coef * partner
     return coef[:, 0, :]
+
+
+def pair_kernel(x_ref, g_ref, gain_ref, down_ref, up_ref, out_ref):
+    widened = x_ref[...].astype(jnp.float32)
+    width = widened.shape[1]
+    rows = widened.shape[0]
+    inverse = lax.rsqrt(jnp.sum(widened * widened, axis=1, keepdims=True) / width + norm_eps)
+    normed = (widened * inverse * gain_ref[...]).astype(jnp.bfloat16)
+    contract_last = (((1,), (1,)), ((), ()))
+    contract_first = (((0,), (0,)), ((), ()))
+    reduced = lax.dot_general(
+        normed, down_ref[...], contract_last, preferred_element_type=jnp.float32
+    ).astype(jnp.bfloat16)
+    incoming = g_ref[...]
+    out_ref[1] = (
+        adapter_scale
+        * lax.dot_general(reduced, incoming, contract_first, preferred_element_type=jnp.float32)
+        / rows
+    )
+    backward_lowrank = (
+        adapter_scale
+        * lax.dot_general(incoming, up_ref[...], contract_last, preferred_element_type=jnp.float32)
+    ).astype(jnp.bfloat16)
+    out_ref[0] = (
+        lax.dot_general(backward_lowrank, normed, contract_first, preferred_element_type=jnp.float32)
+        / rows
+    )
+
+
+def gradient_pair(inputs, incoming_gradient, gain_row, down_rows, upward_rows, interpret=False):
+    rank, width = down_rows.shape
+    return pl.pallas_call(
+        pair_kernel,
+        out_shape=jax.ShapeDtypeStruct((2, rank, width), jnp.float32),
+        interpret=interpret,
+    )(inputs, incoming_gradient, gain_row[None], down_rows, upward_rows)
 
 
 def bit_reversed_eye(n):
@@ -150,6 +186,13 @@
         adapter_down_weight[0],
         adapter_up_weight[0],
     )
+    grad_pair = gradient_pair(
+        activations[0],
+        upstream[0],
+        section_norm_gain[0],
+        adapter_down_weight[0],
+        adapter_up_weight[0],
+    )
     shifted = from_behind(passed_local[None], "section", -1)
     merged_gradient = gram_adasum(grad_pair)
     return (shifted, merged_gradient)

time: 113 us -> 113 us (level)
  Pallas kernels: 4.71 us -> 10.2 us
  waiting for transfers between devices: 46.3 us -> 41.1 us
    pallas_call x0 -> x1, Pallas kernels: none -> 5.47 us  [gradient_pair(): pl.pallas_call(pair_kernel, out_shape=jax.ShapeDtypeStruct((2, rank, widt...]
    all_to_all x1, waiting for transfers between devices: 32.9 us -> 27.6 us  [gram_adasum(): chunks = lax.all_to_all(flat, 'dp', 0, 0, tiled=True)]
    dot_general x3 -> x0, matrix products: 4.18 us -> none  [the longest x1 1.93 us: replica_backward(): jnp.einsum('tk,td->kd', reduced_gradient, incoming_gradient, preferred_el...]
    dot_general x1, matrix products: 0.67 us -> 3.99 us  [replica_backward(): jnp.einsum('tk,kd->td', backward_lowrank, down_rows, preferred_element_ty...]
    broadcast_in_dim x1, other arithmetic: 1.89 us -> 3.55 us  [per_device(): shifted = from_behind(passed_local[None], 'section', -1)]
    reduce_sum x1, other arithmetic: 1.8 us -> 0.34 us  [replica_backward(): jnp.mean(widened * widened, axis=-1, keepdims=True) + norm_eps]
    all_to_all x1, local copies, waits for them, and re-layouts: 1.61 us -> 2.83 us  [gram_adasum(): chunks = lax.all_to_all(flat, 'dp', 0, 0, tiled=True)]
    unnamed x14 -> x12, local copies, waits for them, and re-layouts: 2.46 us -> 1.96 us
  transfers between devices with their start and end apart: 3 -> 3, of which waited for: 2 -> 2; matrix products, arithmetic and copies ran while one was open for 4% -> 9% of each run, Pallas kernels for 0% -> 0%
where the time goes in v11:
time: 113 us
  waiting for transfers between devices  41.1 us (36%)
  starting transfers between devices  25.2 us (22%)
  blocking collectives  20.7 us (18%)
  Pallas kernels  10.2 us (9%)
  local copies, waits for them, and re-layouts  6.1 us (5%)
  matrix products  4.65 us (4%)
  other arithmetic  3.92 us (3%)
    all_to_all x1, waiting for transfers between devices, gram_adasum(): chunks = lax.all_to_all(flat, 'dp', 0, 0, tiled=True)  27.6 us
    all_to_all x1, blocking collectives, gram_adasum(): rows = lax.all_to_all(partial[:, None, :], 'dp', 0, 0, tiled=True)  20.7 us
    all_to_all x1, starting transfers between devices, gram_adasum(): chunks = lax.all_to_all(flat, 'dp', 0, 0, tiled=True)  18.7 us
    all_to_all x1, waiting for transfers between devices, gram_adasum(): gram_rows = lax.all_to_all(spread, 'dp', 0, 0, tiled=True)  13.5 us
    pallas_call x1, Pallas kernels, gradient_pair(): pl.pallas_call(pair_kernel, out_shape=jax.ShapeDtypeStruct((2, rank, widt...  5.47 us
    pallas_call x1, Pallas kernels, combine(): pl.pallas_call(combine_kernel, out_shape=jax.ShapeDtypeStruct((1, chunks....  4.71 us
    all_to_all x1, starting transfers between devices, gram_adasum(): gram_rows = lax.all_to_all(spread, 'dp', 0, 0, tiled=True)  4.6 us
    dot_general x1, matrix products, replica_backward(): jnp.einsum('tk,kd->td', backward_lowrank, down_rows, preferred_element_ty...  3.99 us
  transfers between devices with their start and end apart: 3, of which 2 were waited for; matrix products, arithmetic and copies ran while one was open for 9% of the time, Pallas kernels for 0%

profile of v11, /device:TPU:6, one launch (start us, length us, event | category | flops | bytes accessed | tf_op | source)
XLA Modules:
  0.0 112.6 jit_solution(10694099490901229437)
XLA Ops:
  0.6 0.0 copy-start
  0.6 5.5 %shard_map.77 = f32[2,16,5120]{2,1,0:T(8,128)} custom-call(bf16[128,5120]{1,0:T(8,128)(2,1)} %bitcast.36, bf16[128,5120]{1,0:T(8,128)(2,1)} %bitcast.37, f32[1,5120]{1,0:T(1,128)} %gain_ref.1, bf16[16,5120]{1,0:T(8,128)(2,1)} %bitcast.39, bf16[16,5120]{1,0:T(8,128)(2,1)} %bitcast.40), custom_call_target="tpu_custom_call" | custom-call | tf_op jit(solution)/shard_map/pallas_call | solution.py:112
  6.1 0.0 copy-start.1
  6.1 0.0 copy-start.2
  6.1 0.0 copy-start.4
  6.1 2.8 %all_to_all.21 = f32[64,1,2560]{2,1,0:T(1,128)} reshape(f32[2,16,5120]{2,1,0:T(8,128)} %shard_map.77) | data formatting | bytes 1310720 | tf_op jit(solution)/shard_map/all_to_all | solution.py:169
  8.9 18.7 %all-to-all-start = ((f32[64,1,2560]{2,1,0:T(1,128)}), f32[64,1,2560]{2,1,0:T(1,128)S(1)}, u32[]{:S(2)}, u32[]{:S(2)}) async-start(f32[64,1,2560]{2,1,0:T(1,128)} %all_to_all.21), calls=%async_computation | async-start | bytes 1310720 | tf_op jit(solution)/shard_map/all_to_all | solution.py:169
  27.7 0.0 copy-done
  27.7 0.3 fusion.7
  28.0 0.0 copy-done.1
  28.1 0.0 copy-done.2
  28.1 0.0 copy-done.4
  28.1 4.0 %fusion.2 = (f32[128]{0:T(128)S(1)}, f32[128,5120]{1,0:T(8,128)}) fusion(f32[128]{0:T(128)S(1)} %add_rsqrt_fusion, bf16[1,128,5120]{2,1,0:T(8,128)(2,1)S(1)} %copy-done, f32[5120]{0:T(1024)S(1)} %bitcast.44, bf16[1,16,5120]{2,1,0:T(8,128)(2,1)S(1)} %copy-done.2, bf16[1,16,5120]{2,1,0:T(8,128)(2,1)} %param.10, bf16[1,128,5120]{2,1,0:T(8,128)(2,1)S(1)} %copy-done.1), kind=kOutput, calls=%fused_computation.5 | convolution fusion | flops 45223808 | bytes 5592064 | tf_op jit(solution)/shard_map/tk,kd->td/dot_general | solution.py:53
  32.1 3.6 %fusion.8 = bf16[1,128,5120]{2,1,0:T(8,128)(2,1)} fusion(f32[128,5120]{1,0:T(8,128)} %get-tuple-element.3, f32[128]{0:T(128)S(1)} %broadcast_multiply_fusion, f32[128]{0:T(128)S(1)} %add_rsqrt_fusion, bf16[1,128,5120]{2,1,0:T(8,128)(2,1)S(1)} %copy-done, bf16[1,128,5120]{2,1,0:T(8,128)(2,1)S(1)} %copy-done.1), kind=kLoop, calls=%fused_computation.11 | loop fusion | flops 5242880 | bytes 6554624 | tf_op jit(solution)/shard_map/broadcast_in_dim | solution.py:196
  35.6 1.9 %collective-permute-start = (bf16[1,128,5120]{2,1,0:T(8,128)(2,1)}, bf16[1,128,5120]{2,1,0:T(8,128)(2,1)S(1)}, u32[]{:S(2)}, u32[]{:S(2)}) collective-permute-start(bf16[1,128,5120]{2,1,0:T(8,128)(2,1)} %fusion.8), channel_id=1, source_target_pairs={{64,0},{128,64},{192,128},{256,192},{320,256},{384,320},{448,384},... | collective-permute-start | bytes 3932168 | tf_op jit(solution)/shard_map/ppermute | solution.py:23
  37.5 27.6 %all-to-all-done = f32[64,1,2560]{2,1,0:T(1,128)S(1)} async-done(((f32[64,1,2560]{2,1,0:T(1,128)}), f32[64,1,2560]{2,1,0:T(1,128)S(1)}, u32[]{:S(2)}, u32[]{:S(2)}) %all-to-all-start) | async-done | bytes 655392 | tf_op jit(solution)/shard_map/all_to_all | solution.py:169
  65.1 0.7 fusion.17
  65.8 20.7 %all_to_all.25 = f32[64,1,64]{2,1,0:T(1,128)S(1)} all-to-all(f32[64,1,64]{2,1,0:T(1,128)S(1)} %bitcast.43), channel_id=1, replica_groups=mesh['section'=8,'dp'=64] {'dp'}, dimensions={0} | all-to-all | bytes 32768 | tf_op jit(solution)/shard_map/all_to_all | solution.py:174
  86.5 0.1 broadcast_in_dim.20
  86.6 0.6 broadcast_in_dim.21
  87.2 4.6 %all-to-all-start.2 = ((f32[64,1,128]{2,1,0:T(1,128)}), f32[64,1,128]{2,1,0:T(1,128)S(1)}, u32[]{:S(2)}, u32[]{:S(2)}) async-start(f32[64,1,128]{2,1,0:T(1,128)} %broadcast_in_dim.21), calls=%async_computation.2 | async-start | bytes 65536 | tf_op jit(solution)/shard_map/all_to_all | solution.py:177
  91.8 0.0 collective-permute-done
  91.8 0.9 copy.13
  92.7 13.5 %all-to-all-done.2 = f32[64,1,128]{2,1,0:T(1,128)S(1)} async-done(((f32[64,1,128]{2,1,0:T(1,128)}), f32[64,1,128]{2,1,0:T(1,128)S(1)}, u32[]{:S(2)}, u32[]{:S(2)}) %all-to-all-start.2) | async-done | bytes 32800 | tf_op jit(solution)/shard_map/all_to_all | solution.py:177
  106.3 0.0 copy-start.3
  106.3 0.6 broadcast_in_dim.22.sel_ref
  106.9 0.0 copy-done.3
  106.9 4.7 %shard_map.78 = bf16[1,2560]{1,0:T(2,128)(2,1)} custom-call(f32[64,64]{1,0:T(8,128)} %constant.33.clone.start_ref, f32[64,128]{1,0:T(8,128)} %bitcast.41, f32[8,128]{1,0:T(8,128)} %broadcast_in_dim.22.sel_ref, f32[64,2560]{1,0:T(8,128)} %bitcast.38), custom_call_target="tpu_custom_call" | custom-call | tf_op jit(solution)/shard_map/pallas_call | solution.py:158
  111.6 1.1 copy.15
  (3 shorter events, 0.0 us)
Async XLA Ops:
  0.6 27.1 %copy-start = (bf16[1,128,5120]{2,1,0:T(8,128)(2,1)S(1)}, bf16[1,128,5120]{2,1,0:T(8,128)(2,1)}, u32[]{:S(2)}) copy-start(bf16[1,128,5120]{2,1,0:T(8,128)(2,1)} %param.6) | copy-start | bytes 3932164
  6.1 21.9 %copy-start.1 = (bf16[1,128,5120]{2,1,0:T(8,128)(2,1)S(1)}, bf16[1,128,5120]{2,1,0:T(8,128)(2,1)}, u32[]{:S(2)}) copy-start(bf16[1,128,5120]{2,1,0:T(8,128)(2,1)} %param.7) | copy-start | bytes 3932164
  6.1 21.9 %copy-start.2 = (bf16[1,16,5120]{2,1,0:T(8,128)(2,1)S(1)}, bf16[1,16,5120]{2,1,0:T(8,128)(2,1)}, u32[]{:S(2)}) copy-start(bf16[1,16,5120]{2,1,0:T(8,128)(2,1)} %param.9) | copy-start | bytes 491524
  6.1 21.9 %copy-start.4 = (f32[1,5120]{1,0:T(1,128)S(1)}, f32[1,5120]{1,0:T(1,128)}, u32[]{:S(2)}) copy-start(f32[1,5120]{1,0:T(1,128)} %gain_ref.1) | copy-start | bytes 61444
  8.9 56.1 %all-to-all-start = ((f32[64,1,2560]{2,1,0:T(1,128)}), f32[64,1,2560]{2,1,0:T(1,128)S(1)}, u32[]{:S(2)}, u32[]{:S(2)}) async-start(f32[64,1,2560]{2,1,0:T(1,128)} %all_to_all.21), calls=%async_computation | async-start | bytes 1310720 | tf_op jit(solution)/shard_map/all_to_all | solution.py:169
  35.6 56.2 %collective-permute-start = (bf16[1,128,5120]{2,1,0:T(8,128)(2,1)}, bf16[1,128,5120]{2,1,0:T(8,128)(2,1)S(1)}, u32[]{:S(2)}, u32[]{:S(2)}) collective-permute-start(bf16[1,128,5120]{2,1,0:T(8,128)(2,1)} %fusion.8), channel_id=1, source_target_pairs={{64,0},{128,64},{192,128},{256,192},{320,256},{384,320},{448,384},... | collective-permute-start | bytes 3932168 | tf_op jit(solution)/shard_map/ppermute | solution.py:23
  87.2 19.1 %all-to-all-start.2 = ((f32[64,1,128]{2,1,0:T(1,128)}), f32[64,1,128]{2,1,0:T(1,128)S(1)}, u32[]{:S(2)}, u32[]{:S(2)}) async-start(f32[64,1,128]{2,1,0:T(1,128)} %broadcast_in_dim.21), calls=%async_computation.2 | async-start | bytes 65536 | tf_op jit(solution)/shard_map/all_to_all | solution.py:177
  106.3 0.6 copy-start.3

commit v12 on v11

--- a/solution.py
+++ b/solution.py
@@ -87,24 +87,18 @@
     inverse = lax.rsqrt(jnp.sum(widened * widened, axis=1, keepdims=True) / width + norm_eps)
     normed = (widened * inverse * gain_ref[...]).astype(jnp.bfloat16)
     contract_last = (((1,), (1,)), ((), ()))
-    contract_first = (((0,), (0,)), ((), ()))
-    reduced = lax.dot_general(
-        normed, down_ref[...], contract_last, preferred_element_type=jnp.float32
-    ).astype(jnp.bfloat16)
     incoming = g_ref[...]
+    reduced_t = lax.dot_general(
+        down_ref[...], normed, contract_last, preferred_element_type=jnp.float32
+    ).astype(jnp.bfloat16)
     out_ref[1] = (
+        adapter_scale * jnp.dot(reduced_t, incoming, preferred_element_type=jnp.float32) / rows
+    )
+    backward_lowrank_t = (
         adapter_scale
-        * lax.dot_general(reduced, incoming, contract_first, preferred_element_type=jnp.float32)
-        / rows
-    )
-    backward_lowrank = (
-        adapter_scale
-        * lax.dot_general(incoming, up_ref[...], contract_last, preferred_element_type=jnp.float32)
-    ).astype(jnp.bfloat16)
-    out_ref[0] = (
-        lax.dot_general(backward_lowrank, normed, contract_first, preferred_element_type=jnp.float32)
-        / rows
-    )
+        * lax.dot_general(up_ref[...], incoming, contract_last, preferred_element_type=jnp.float32)
+    ).astype(jnp.bfloat16)
+    out_ref[0] = jnp.dot(backward_lowrank_t, normed, preferred_element_type=jnp.float32) / rows
 
 
 def gradient_pair(inputs, incoming_gradient, gain_row, down_rows, upward_rows, interpret=False):

time: 113 us -> 113 us (level)
  no operation moved by 1% of the time
where the time goes in v12:
time: 113 us
  waiting for transfers between devices  41.1 us (36%)
  starting transfers between devices  25.2 us (22%)
  blocking collectives  20.7 us (18%)
  Pallas kernels  10.1 us (9%)
  local copies, waits for them, and re-layouts  6.1 us (5%)
  matrix products  4.65 us (4%)
  other arithmetic  3.92 us (3%)
    all_to_all x1, waiting for transfers between devices, gram_adasum(): chunks = lax.all_to_all(flat, 'dp', 0, 0, tiled=True)  27.5 us
    all_to_all x1, blocking collectives, gram_adasum(): rows = lax.all_to_all(partial[:, None, :], 'dp', 0, 0, tiled=True)  20.7 us
    all_to_all x1, starting transfers between devices, gram_adasum(): chunks = lax.all_to_all(flat, 'dp', 0, 0, tiled=True)  18.7 us
    all_to_all x1, waiting for transfers between devices, gram_adasum(): gram_rows = lax.all_to_all(spread, 'dp', 0, 0, tiled=True)  13.5 us
    pallas_call x1, Pallas kernels, gradient_pair(): pl.pallas_call(pair_kernel, out_shape=jax.ShapeDtypeStruct((2, rank, widt...  5.39 us
    pallas_call x1, Pallas kernels, combine(): pl.pallas_call(combine_kernel, out_shape=jax.ShapeDtypeStruct((1, chunks....  4.71 us
    all_to_all x1, starting transfers between devices, gram_adasum(): gram_rows = lax.all_to_all(spread, 'dp', 0, 0, tiled=True)  4.6 us
    dot_general x1, matrix products, replica_backward(): jnp.einsum('tk,kd->td', backward_lowrank, down_rows, preferred_element_ty...  3.99 us
  transfers between devices with their start and end apart: 3, of which 2 were waited for; matrix products, arithmetic and copies ran while one was open for 9% of the time, Pallas kernels for 0%

profile of v12, /device:TPU:6, one launch (start us, length us, event | category | flops | bytes accessed | tf_op | source)
XLA Modules:
  0.0 112.5 jit_solution(14783746285033045943)
XLA Ops:
  0.6 0.0 copy-start
  0.6 5.4 %shard_map.77 = f32[2,16,5120]{2,1,0:T(8,128)} custom-call(bf16[128,5120]{1,0:T(8,128)(2,1)} %bitcast.36, bf16[128,5120]{1,0:T(8,128)(2,1)} %bitcast.37, f32[1,5120]{1,0:T(1,128)} %gain_ref.1, bf16[16,5120]{1,0:T(8,128)(2,1)} %bitcast.39, bf16[16,5120]{1,0:T(8,128)(2,1)} %bitcast.40), custom_call_target="tpu_custom_call" | custom-call | tf_op jit(solution)/shard_map/pallas_call | solution.py:106
  6.0 0.0 copy-start.1
  6.0 0.0 copy-start.2
  6.0 0.0 copy-start.4
  6.0 2.8 %all_to_all.21 = f32[64,1,2560]{2,1,0:T(1,128)} reshape(f32[2,16,5120]{2,1,0:T(8,128)} %shard_map.77) | data formatting | bytes 1310720 | tf_op jit(solution)/shard_map/all_to_all | solution.py:163
  8.9 18.7 %all-to-all-start = ((f32[64,1,2560]{2,1,0:T(1,128)}), f32[64,1,2560]{2,1,0:T(1,128)S(1)}, u32[]{:S(2)}, u32[]{:S(2)}) async-start(f32[64,1,2560]{2,1,0:T(1,128)} %all_to_all.21), calls=%async_computation | async-start | bytes 1310720 | tf_op jit(solution)/shard_map/all_to_all | solution.py:163
  27.6 0.0 copy-done
  27.6 0.3 fusion.7
  28.0 0.0 copy-done.1
  28.0 0.0 copy-done.2
  28.0 0.0 copy-done.4
  28.0 4.0 %fusion.2 = (f32[128]{0:T(128)S(1)}, f32[128,5120]{1,0:T(8,128)}) fusion(f32[128]{0:T(128)S(1)} %add_rsqrt_fusion, bf16[1,128,5120]{2,1,0:T(8,128)(2,1)S(1)} %copy-done, f32[5120]{0:T(1024)S(1)} %bitcast.44, bf16[1,16,5120]{2,1,0:T(8,128)(2,1)S(1)} %copy-done.2, bf16[1,16,5120]{2,1,0:T(8,128)(2,1)} %param.10, bf16[1,128,5120]{2,1,0:T(8,128)(2,1)S(1)} %copy-done.1), kind=kOutput, calls=%fused_computation.5 | convolution fusion | flops 45223808 | bytes 5592064 | tf_op jit(solution)/shard_map/tk,kd->td/dot_general | solution.py:53
  32.0 3.6 %fusion.8 = bf16[1,128,5120]{2,1,0:T(8,128)(2,1)} fusion(f32[128,5120]{1,0:T(8,128)} %get-tuple-element.3, f32[128]{0:T(128)S(1)} %broadcast_multiply_fusion, f32[128]{0:T(128)S(1)} %add_rsqrt_fusion, bf16[1,128,5120]{2,1,0:T(8,128)(2,1)S(1)} %copy-done, bf16[1,128,5120]{2,1,0:T(8,128)(2,1)S(1)} %copy-done.1), kind=kLoop, calls=%fused_computation.11 | loop fusion | flops 5242880 | bytes 6554624 | tf_op jit(solution)/shard_map/broadcast_in_dim | solution.py:190
  35.5 1.9 %collective-permute-start = (bf16[1,128,5120]{2,1,0:T(8,128)(2,1)}, bf16[1,128,5120]{2,1,0:T(8,128)(2,1)S(1)}, u32[]{:S(2)}, u32[]{:S(2)}) collective-permute-start(bf16[1,128,5120]{2,1,0:T(8,128)(2,1)} %fusion.8), channel_id=1, source_target_pairs={{64,0},{128,64},{192,128},{256,192},{320,256},{384,320},{448,384},... | collective-permute-start | bytes 3932168 | tf_op jit(solution)/shard_map/ppermute | solution.py:23
  37.5 27.5 %all-to-all-done = f32[64,1,2560]{2,1,0:T(1,128)S(1)} async-done(((f32[64,1,2560]{2,1,0:T(1,128)}), f32[64,1,2560]{2,1,0:T(1,128)S(1)}, u32[]{:S(2)}, u32[]{:S(2)}) %all-to-all-start) | async-done | bytes 655392 | tf_op jit(solution)/shard_map/all_to_all | solution.py:163
  65.0 0.7 fusion.17
  65.7 20.7 %all_to_all.25 = f32[64,1,64]{2,1,0:T(1,128)S(1)} all-to-all(f32[64,1,64]{2,1,0:T(1,128)S(1)} %bitcast.43), channel_id=1, replica_groups=mesh['section'=8,'dp'=64] {'dp'}, dimensions={0} | all-to-all | bytes 32768 | tf_op jit(solution)/shard_map/all_to_all | solution.py:168
  86.4 0.1 broadcast_in_dim.20
  86.5 0.6 broadcast_in_dim.21
  87.1 4.6 %all-to-all-start.2 = ((f32[64,1,128]{2,1,0:T(1,128)}), f32[64,1,128]{2,1,0:T(1,128)S(1)}, u32[]{:S(2)}, u32[]{:S(2)}) async-start(f32[64,1,128]{2,1,0:T(1,128)} %broadcast_in_dim.21), calls=%async_computation.2 | async-start | bytes 65536 | tf_op jit(solution)/shard_map/all_to_all | solution.py:171
  91.7 0.0 collective-permute-done
  91.8 0.9 copy.13
  92.6 13.5 %all-to-all-done.2 = f32[64,1,128]{2,1,0:T(1,128)S(1)} async-done(((f32[64,1,128]{2,1,0:T(1,128)}), f32[64,1,128]{2,1,0:T(1,128)S(1)}, u32[]{:S(2)}, u32[]{:S(2)}) %all-to-all-start.2) | async-done | bytes 32800 | tf_op jit(solution)/shard_map/all_to_all | solution.py:171
  106.2 0.0 copy-start.3
  106.2 0.6 broadcast_in_dim.22.sel_ref
  106.8 0.0 copy-done.3
  106.8 4.7 %shard_map.78 = bf16[1,2560]{1,0:T(2,128)(2,1)} custom-call(f32[64,64]{1,0:T(8,128)} %constant.33.clone.start_ref, f32[64,128]{1,0:T(8,128)} %bitcast.41, f32[8,128]{1,0:T(8,128)} %broadcast_in_dim.22.sel_ref, f32[64,2560]{1,0:T(8,128)} %bitcast.38), custom_call_target="tpu_custom_call" | custom-call | tf_op jit(solution)/shard_map/pallas_call | solution.py:152
  111.5 1.1 copy.15
  (3 shorter events, 0.0 us)
Async XLA Ops:
  0.6 27.0 %copy-start = (bf16[1,128,5120]{2,1,0:T(8,128)(2,1)S(1)}, bf16[1,128,5120]{2,1,0:T(8,128)(2,1)}, u32[]{:S(2)}) copy-start(bf16[1,128,5120]{2,1,0:T(8,128)(2,1)} %param.6) | copy-start | bytes 3932164
  6.0 21.9 %copy-start.1 = (bf16[1,128,5120]{2,1,0:T(8,128)(2,1)S(1)}, bf16[1,128,5120]{2,1,0:T(8,128)(2,1)}, u32[]{:S(2)}) copy-start(bf16[1,128,5120]{2,1,0:T(8,128)(2,1)} %param.7) | copy-start | bytes 3932164
  6.0 21.9 %copy-start.2 = (bf16[1,16,5120]{2,1,0:T(8,128)(2,1)S(1)}, bf16[1,16,5120]{2,1,0:T(8,128)(2,1)}, u32[]{:S(2)}) copy-start(bf16[1,16,5120]{2,1,0:T(8,128)(2,1)} %param.9) | copy-start | bytes 491524
  6.0 21.9 %copy-start.4 = (f32[1,5120]{1,0:T(1,128)S(1)}, f32[1,5120]{1,0:T(1,128)}, u32[]{:S(2)}) copy-start(f32[1,5120]{1,0:T(1,128)} %gain_ref.1) | copy-start | bytes 61444
  8.9 56.1 %all-to-all-start = ((f32[64,1,2560]{2,1,0:T(1,128)}), f32[64,1,2560]{2,1,0:T(1,128)S(1)}, u32[]{:S(2)}, u32[]{:S(2)}) async-start(f32[64,1,2560]{2,1,0:T(1,128)} %all_to_all.21), calls=%async_computation | async-start | bytes 1310720 | tf_op jit(solution)/shard_map/all_to_all | solution.py:163
  35.5 56.2 %collective-permute-start = (bf16[1,128,5120]{2,1,0:T(8,128)(2,1)}, bf16[1,128,5120]{2,1,0:T(8,128)(2,1)S(1)}, u32[]{:S(2)}, u32[]{:S(2)}) collective-permute-start(bf16[1,128,5120]{2,1,0:T(8,128)(2,1)} %fusion.8), channel_id=1, source_target_pairs={{64,0},{128,64},{192,128},{256,192},{320,256},{384,320},{448,384},... | collective-permute-start | bytes 3932168 | tf_op jit(solution)/shard_map/ppermute | solution.py:23
  87.1 19.1 %all-to-all-start.2 = ((f32[64,1,128]{2,1,0:T(1,128)}), f32[64,1,128]{2,1,0:T(1,128)S(1)}, u32[]{:S(2)}, u32[]{:S(2)}) async-start(f32[64,1,128]{2,1,0:T(1,128)} %broadcast_in_dim.21), calls=%async_computation.2 | async-start | bytes 65536 | tf_op jit(solution)/shard_map/all_to_all | solution.py:171
  106.2 0.6 copy-start.3

commit v13 on v10

--- a/solution.py
+++ b/solution.py
@@ -88,29 +88,25 @@
 
 def combine_kernel(start_ref, gram_ref, chunks_ref, out_ref):
     n = gram_ref.shape[0]
-    finals = []
-    for t in range(gram_ref.shape[1] // n):
-        gram = gram_ref[:, t * n:(t + 1) * n]
-        coef = start_ref[...]
-        while coef.shape[0] > 1:
-            half = coef.shape[0] // 2
-            first, second = coef[:half], coef[half:]
-            g_first = jnp.dot(first, gram, precision=HIGH, preferred_element_type=jnp.float32)
-            g_second = jnp.dot(second, gram, precision=HIGH, preferred_element_type=jnp.float32)
-            inner_sum = jnp.sum(g_first * second, axis=1, keepdims=True)
-            own_square = jnp.sum(g_first * first, axis=1, keepdims=True)
-            far_square = jnp.sum(g_second * second, axis=1, keepdims=True)
-            keep_coef = 1.0 - inner_sum / (2.0 * (own_square + pair_eps))
-            take_coef = 1.0 - inner_sum / (2.0 * (far_square + pair_eps))
-            coef = keep_coef * first + take_coef * second
-        finals.append(coef)
-    sel = jnp.where(lax.axis_index("dp") < lax.axis_size("dp") // 2, 1.0, 0.0)
-    row = sel * finals[0] + (1.0 - sel) * finals[1]
-    eye = start_ref[...] * 0.0 + (
+    first_tensor = lax.axis_index("dp") < lax.axis_size("dp") // 2
+    gram = jnp.where(first_tensor, gram_ref[:, 0:n], gram_ref[:, n:2 * n])
+    coef = start_ref[...]
+    while coef.shape[0] > 1:
+        half = coef.shape[0] // 2
+        first, second = coef[:half], coef[half:]
+        g_first = jnp.dot(first, gram, precision=HIGH, preferred_element_type=jnp.float32)
+        g_second = jnp.dot(second, gram, precision=HIGH, preferred_element_type=jnp.float32)
+        inner_sum = jnp.sum(g_first * second, axis=1, keepdims=True)
+        own_square = jnp.sum(g_first * first, axis=1, keepdims=True)
+        far_square = jnp.sum(g_second * second, axis=1, keepdims=True)
+        keep_coef = 1.0 - inner_sum / (2.0 * (own_square + pair_eps))
+        take_coef = 1.0 - inner_sum / (2.0 * (far_square + pair_eps))
+        coef = keep_coef * first + take_coef * second
+    eye = (
         lax.broadcasted_iota(jnp.int32, (n, n), 0) == lax.broadcasted_iota(jnp.int32, (n, n), 1)
     ).astype(jnp.float32)
     column = lax.dot_general(
-        eye, row, (((1,), (1,)), ((), ())), precision=HIGH, preferred_element_type=jnp.float32
+        eye, coef, (((1,), (1,)), ((), ())), precision=HIGH, preferred_element_type=jnp.float32
     )
     combined = jnp.sum(column * chunks_ref[...], axis=0, keepdims=True)
     out_ref[...] = combined.astype(out_ref.dtype)
@@ -125,7 +121,7 @@
     )(jnp.asarray(bit_reversed_eye(n)), gram_rows, chunks)
 
 
-def gram_adasum(grad_pair, passed):
+def gram_adasum(grad_pair):
     devices = lax.axis_size("dp")
     me = lax.axis_index("dp")
     flat = grad_pair.reshape(devices, -1)
@@ -137,11 +133,8 @@
     rows = lax.all_to_all(partial[:, None, :], "dp", 0, 0, tiled=True)
     rows = jnp.sum(rows.reshape(tensors, per_tensor, partial.shape[1]), axis=1)
     spread = jnp.broadcast_to(rows.reshape(1, -1), (devices, tensors * partial.shape[1]))
-    spread, passed = lax.optimization_barrier((spread, passed))
-    has_next = lax.axis_index("section") < lax.axis_size("section") - 1
-    passed = jnp.where(has_next, passed, jnp.zeros_like(passed))
     gram_rows = lax.all_to_all(spread, "dp", 0, 0, tiled=True)
-    return combine(gram_rows, chunks), passed
+    return combine(gram_rows, chunks)
 
 
 def per_device(activations, upstream, section_norm_gain, adapter_down_weight, adapter_up_weight):
@@ -153,7 +146,7 @@
         adapter_up_weight[0],
     )
     shifted = from_behind(passed_local[None], "section", -1)
-    merged_gradient, shifted = gram_adasum(grad_pair, shifted)
+    merged_gradient = gram_adasum(grad_pair)
     return (shifted, merged_gradient)
 
 

time: 114 us -> 111 us (0.974)
  blocking collectives: 0 us -> 20.7 us
  waiting for transfers between devices: 59.8 us -> 46.3 us
  starting transfers between devices: 31.6 us -> 25.2 us
  other arithmetic: 5.99 us -> 3.77 us
  local copies, waits for them, and re-layouts: 3.87 us -> 5.37 us
  matrix products: 6.85 us -> 5.52 us
  Pallas kernels: 4.7 us -> 3.46 us
    all_to_all x0 -> x1, blocking collectives: none -> 20.7 us  [gram_adasum(): rows = lax.all_to_all(partial[:, None, :], 'dp', 0, 0, tiled=True)]
    all_to_all x1 -> x0, waiting for transfers between devices: 13.6 us -> none  [gram_adasum(): rows = lax.all_to_all(partial[:, None, :], 'dp', 0, 0, tiled=True)]
    all_to_all x1 -> x0, starting transfers between devices: 6.46 us -> none  [gram_adasum(): rows = lax.all_to_all(partial[:, None, :], 'dp', 0, 0, tiled=True)]
    unnamed x11 -> x14, local copies, waits for them, and re-layouts: 1.54 us -> 3.06 us
    pallas_call x1, Pallas kernels: 4.7 us -> 3.46 us  [combine(): pl.pallas_call(combine_kernel, out_shape=jax.ShapeDtypeStruct((1, chunks....]
    select_n x1 -> x0, other arithmetic: 1.15 us -> none  [gram_adasum(): passed = jnp.where(has_next, passed, jnp.zeros_like(passed))]
  transfers between devices with their start and end apart: 4 -> 3, of which waited for: 3 -> 2; matrix products, arithmetic and copies ran while one was open for 5% -> 4% of each run, Pallas kernels for 0% -> 0%
where the time goes in v13:
time: 111 us
  waiting for transfers between devices  46.3 us (42%)
  starting transfers between devices  25.2 us (23%)
  blocking collectives  20.7 us (19%)
  matrix products  5.52 us (5%)
  local copies, waits for them, and re-layouts  5.37 us (5%)
  other arithmetic  3.77 us (3%)
  Pallas kernels  3.46 us (3%)
    all_to_all x1, waiting for transfers between devices, gram_adasum(): chunks = lax.all_to_all(flat, 'dp', 0, 0, tiled=True)  32.9 us
    all_to_all x1, blocking collectives, gram_adasum(): rows = lax.all_to_all(partial[:, None, :], 'dp', 0, 0, tiled=True)  20.7 us
    all_to_all x1, starting transfers between devices, gram_adasum(): chunks = lax.all_to_all(flat, 'dp', 0, 0, tiled=True)  18.7 us
    all_to_all x1, waiting for transfers between devices, gram_adasum(): gram_rows = lax.all_to_all(spread, 'dp', 0, 0, tiled=True)  13.4 us
    all_to_all x1, starting transfers between devices, gram_adasum(): gram_rows = lax.all_to_all(spread, 'dp', 0, 0, tiled=True)  4.57 us
    pallas_call x1, Pallas kernels, combine(): pl.pallas_call(combine_kernel, out_shape=jax.ShapeDtypeStruct((1, chunks....  3.46 us
    unnamed x14, local copies, waits for them, and re-layouts  3.06 us
  transfers between devices with their start and end apart: 3, of which 2 were waited for; matrix products, arithmetic and copies ran while one was open for 4% of the time, Pallas kernels for 0%

profile of v13, /device:TPU:6, one launch (start us, length us, event | category | flops | bytes accessed | tf_op | source)
XLA Modules:
  0.0 111.1 jit_solution(607686320790744974)
XLA Ops:
  0.6 0.0 copy-start
  0.6 0.0 copy-start.1
  0.7 0.0 copy-start.2
  0.7 0.0 copy-start.5
  0.7 1.8 %fusion.13 = f32[128]{0:T(128)S(1)} fusion(bf16[1,128,5120]{2,1,0:T(8,128)(2,1)} %param.6), kind=kLoop, calls=%fused_computation.18 | loop fusion | flops 1965952 | bytes 1311232 | tf_op jit(solution)/shard_map/reduce_sum | solution.py:28
  2.5 1.8 %fusion.34 = bf16[128,16]{0,1:T(8,128)(2,1)S(1)} fusion(bf16[1,128,5120]{2,1,0:T(8,128)(2,1)} %param.7, bf16[1,16,5120]{2,1,0:T(8,128)(2,1)} %param.10), kind=kOutput, calls=%fused_computation.33 | convolution fusion | flops 20975616 | bytes 1478656 | tf_op jit(solution)/shard_map/sh,gh->sg/dot_general | solution.py:44
  4.3 0.0 copy-done
  4.3 0.0 copy-done.1
  4.3 0.0 copy-done.2
  4.3 0.0 copy-done.5
  4.3 1.9 %fusion = f32[1,16,5120]{2,1,0:T(8,128)} fusion(bf16[1,128,5120]{2,1,0:T(8,128)(2,1)S(1)} %copy-done.2, bf16[1,128,5120]{2,1,0:T(8,128)(2,1)S(1)} %copy-done.1, f32[5120]{0:T(1024)S(1)} %bitcast.81, f32[128]{0:T(128)S(1)} %add_rsqrt_fusion, bf16[1,16,5120]{2,1,0:T(8,128)(2,1)S(1)} %copy-done), kind=kOutput, calls=%fused_computation.2 | convolution fusion | flops 44648448 | bytes 3133952 | tf_op jit(solution)/shard_map/tk,td->kd/dot_general | solution.py:37
  6.2 0.0 copy-start.3
  6.2 0.5 fusion.1
  6.7 0.5 copy-done.3
  7.3 1.6 %all_to_all.21 = f32[64,1,2560]{2,1,0:T(1,128)} reshape(f32[2,16,5120]{2,1,0:T(8,128)S(1)} %pad_maximum_fusion) | data formatting | bytes 1310720 | tf_op jit(solution)/shard_map/all_to_all | solution.py:128
  8.9 18.7 %all-to-all-start = ((f32[64,1,2560]{2,1,0:T(1,128)}), f32[64,1,2560]{2,1,0:T(1,128)S(1)}, u32[]{:S(2)}, u32[]{:S(2)}) async-start(f32[64,1,2560]{2,1,0:T(1,128)} %all_to_all.21), calls=%async_computation | async-start | bytes 1310720 | tf_op jit(solution)/shard_map/all_to_all | solution.py:128
  27.6 0.7 fusion.7
  28.3 1.9 %fusion.20 = bf16[1,128,5120]{2,1,0:T(8,128)(2,1)} fusion(f32[128,5120]{1,0:T(8,128)S(1)} %get-tuple-element.3, bf16[1,128,5120]{2,1,0:T(8,128)(2,1)S(1)} %copy-done.1, bf16[1,128,5120]{2,1,0:T(8,128)(2,1)S(1)} %copy-done.2, f32[128]{0:T(128)S(1)} %broadcast_multiply_fusion, f32[128]{0:T(128)S(1)} %add_rsqrt_fusion), kind=kLoop, calls=%fused_computation.23 | loop fusion | flops 5242880 | bytes 6554624 | tf_op jit(solution)/shard_map/broadcast_in_dim | solution.py:148
  30.2 1.9 %collective-permute-start = (bf16[1,128,5120]{2,1,0:T(8,128)(2,1)}, bf16[1,128,5120]{2,1,0:T(8,128)(2,1)S(1)}, u32[]{:S(2)}, u32[]{:S(2)}) collective-permute-start(bf16[1,128,5120]{2,1,0:T(8,128)(2,1)} %fusion.20), channel_id=1, source_target_pairs={{64,0},{128,64},{192,128},{256,192},{320,256},{384,320},{448,384},... | collective-permute-start | bytes 3932168 | tf_op jit(solution)/shard_map/ppermute | solution.py:23
  32.1 32.9 %all-to-all-done = f32[64,1,2560]{2,1,0:T(1,128)S(1)} async-done(((f32[64,1,2560]{2,1,0:T(1,128)}), f32[64,1,2560]{2,1,0:T(1,128)S(1)}, u32[]{:S(2)}, u32[]{:S(2)}) %all-to-all-start) | async-done | bytes 655392 | tf_op jit(solution)/shard_map/all_to_all | solution.py:128
  65.0 0.7 fusion.43
  65.7 20.7 %all_to_all.25 = f32[64,1,64]{2,1,0:T(1,128)S(1)} all-to-all(f32[64,1,64]{2,1,0:T(1,128)S(1)} %bitcast.80), channel_id=1, replica_groups=mesh['section'=8,'dp'=64] {'dp'}, dimensions={0} | all-to-all | bytes 32768 | tf_op jit(solution)/shard_map/all_to_all | solution.py:133
  86.4 0.1 broadcast_in_dim.17
  86.5 0.6 broadcast_in_dim.18
  87.1 4.6 %all-to-all-start.2 = ((f32[64,1,128]{2,1,0:T(1,128)}), f32[64,1,128]{2,1,0:T(1,128)S(1)}, u32[]{:S(2)}, u32[]{:S(2)}) async-start(f32[64,1,128]{2,1,0:T(1,128)} %broadcast_in_dim.18), calls=%async_computation.2 | async-start | bytes 65536 | tf_op jit(solution)/shard_map/all_to_all | solution.py:136
  91.7 0.0 collective-permute-done
  91.7 0.9 copy.13
  92.6 13.4 %all-to-all-done.2 = f32[64,1,128]{2,1,0:T(1,128)S(1)} async-done(((f32[64,1,128]{2,1,0:T(1,128)}), f32[64,1,128]{2,1,0:T(1,128)S(1)}, u32[]{:S(2)}, u32[]{:S(2)}) %all-to-all-start.2) | async-done | bytes 32800 | tf_op jit(solution)/shard_map/all_to_all | solution.py:136
  106.0 0.0 copy-start.4
  106.0 0.6 copy-done.4
  106.6 3.5 %shard_map.77 = bf16[1,2560]{1,0:T(2,128)(2,1)} custom-call(f32[64,64]{1,0:T(8,128)} %constant.19.clone.start_ref, f32[64,128]{1,0:T(8,128)} %bitcast.78, f32[64,2560]{1,0:T(8,128)} %bitcast.77), custom_call_target="tpu_custom_call" | custom-call | tf_op jit(solution)/shard_map/pallas_call | solution.py:117
  110.1 1.1 copy.15
  (4 shorter events, 0.1 us)
Async XLA Ops:
  0.6 3.6 %copy-start = (bf16[1,16,5120]{2,1,0:T(8,128)(2,1)S(1)}, bf16[1,16,5120]{2,1,0:T(8,128)(2,1)}, u32[]{:S(2)}) copy-start(bf16[1,16,5120]{2,1,0:T(8,128)(2,1)} %param.9) | copy-start | bytes 491524
  0.6 3.6 %copy-start.1 = (bf16[1,128,5120]{2,1,0:T(8,128)(2,1)S(1)}, bf16[1,128,5120]{2,1,0:T(8,128)(2,1)}, u32[]{:S(2)}) copy-start(bf16[1,128,5120]{2,1,0:T(8,128)(2,1)} %param.6) | copy-start | bytes 3932164
  0.7 3.6 %copy-start.2 = (bf16[1,128,5120]{2,1,0:T(8,128)(2,1)S(1)}, bf16[1,128,5120]{2,1,0:T(8,128)(2,1)}, u32[]{:S(2)}) copy-start(bf16[1,128,5120]{2,1,0:T(8,128)(2,1)} %param.7) | copy-start | bytes 3932164
  0.7 3.6 %copy-start.5 = (f32[1,5120]{1,0:T(1,128)S(1)}, f32[1,5120]{1,0:T(1,128)}, u32[]{:S(2)}) copy-start(f32[1,5120]{1,0:T(1,128)} %param.8) | copy-start | bytes 61444
  6.2 1.0 copy-start.3
  8.9 56.1 %all-to-all-start = ((f32[64,1,2560]{2,1,0:T(1,128)}), f32[64,1,2560]{2,1,0:T(1,128)S(1)}, u32[]{:S(2)}, u32[]{:S(2)}) async-start(f32[64,1,2560]{2,1,0:T(1,128)} %all_to_all.21), calls=%async_computation | async-start | bytes 1310720 | tf_op jit(solution)/shard_map/all_to_all | solution.py:128
  30.2 61.5 %collective-permute-start = (bf16[1,128,5120]{2,1,0:T(8,128)(2,1)}, bf16[1,128,5120]{2,1,0:T(8,128)(2,1)S(1)}, u32[]{:S(2)}, u32[]{:S(2)}) collective-permute-start(bf16[1,128,5120]{2,1,0:T(8,128)(2,1)} %fusion.20), channel_id=1, source_target_pairs={{64,0},{128,64},{192,128},{256,192},{320,256},{384,320},{448,384},... | collective-permute-start | bytes 3932168 | tf_op jit(solution)/shard_map/ppermute | solution.py:23
  87.1 18.9 %all-to-all-start.2 = ((f32[64,1,128]{2,1,0:T(1,128)}), f32[64,1,128]{2,1,0:T(1,128)S(1)}, u32[]{:S(2)}, u32[]{:S(2)}) async-start(f32[64,1,128]{2,1,0:T(1,128)} %broadcast_in_dim.18), calls=%async_computation.2 | async-start | bytes 65536 | tf_op jit(solution)/shard_map/all_to_all | solution.py:136
  106.0 0.6 copy-start.4

commit v14 on v13

--- a/solution.py
+++ b/solution.py
@@ -86,11 +86,17 @@
     return np.eye(n, dtype=np.float32)[order]
 
 
-def combine_kernel(start_ref, gram_ref, chunks_ref, out_ref):
+def combine_kernel(gram_ref, chunks_ref, out_ref):
     n = gram_ref.shape[0]
     first_tensor = lax.axis_index("dp") < lax.axis_size("dp") // 2
     gram = jnp.where(first_tensor, gram_ref[:, 0:n], gram_ref[:, n:2 * n])
-    coef = start_ref[...]
+    rows = lax.broadcasted_iota(jnp.int32, (n, n), 0)
+    cols = lax.broadcasted_iota(jnp.int32, (n, n), 1)
+    bits = n.bit_length() - 1
+    reversed_rows = jnp.zeros_like(rows)
+    for b in range(bits):
+        reversed_rows = reversed_rows + ((rows >> b) & 1) * (1 << (bits - 1 - b))
+    coef = (cols == reversed_rows).astype(jnp.float32)
     while coef.shape[0] > 1:
         half = coef.shape[0] // 2
         first, second = coef[:half], coef[half:]
@@ -102,9 +108,7 @@
         keep_coef = 1.0 - inner_sum / (2.0 * (own_square + pair_eps))
         take_coef = 1.0 - inner_sum / (2.0 * (far_square + pair_eps))
         coef = keep_coef * first + take_coef * second
-    eye = (
-        lax.broadcasted_iota(jnp.int32, (n, n), 0) == lax.broadcasted_iota(jnp.int32, (n, n), 1)
-    ).astype(jnp.float32)
+    eye = (rows == cols).astype(jnp.float32)
     column = lax.dot_general(
         eye, coef, (((1,), (1,)), ((), ())), precision=HIGH, preferred_element_type=jnp.float32
     )
@@ -118,10 +122,10 @@
         combine_kernel,
         out_shape=jax.ShapeDtypeStruct((1, chunks.shape[1]), jnp.bfloat16),
         interpret=interpret,
-    )(jnp.asarray(bit_reversed_eye(n)), gram_rows, chunks)
+    )(gram_rows, chunks)
 
 
-def gram_adasum(grad_pair):
+def gram_adasum(grad_pair, passed):
     devices = lax.axis_size("dp")
     me = lax.axis_index("dp")
     flat = grad_pair.reshape(devices, -1)
@@ -133,8 +137,11 @@
     rows = lax.all_to_all(partial[:, None, :], "dp", 0, 0, tiled=True)
     rows = jnp.sum(rows.reshape(tensors, per_tensor, partial.shape[1]), axis=1)
     spread = jnp.broadcast_to(rows.reshape(1, -1), (devices, tensors * partial.shape[1]))
+    spread, passed = lax.optimization_barrier((spread, passed))
+    has_next = lax.axis_index("section") < lax.axis_size("section") - 1
+    passed = jnp.where(has_next, passed, jnp.zeros_like(passed))
     gram_rows = lax.all_to_all(spread, "dp", 0, 0, tiled=True)
-    return combine(gram_rows, chunks)
+    return combine(gram_rows, chunks), passed
 
 
 def per_device(activations, upstream, section_norm_gain, adapter_down_weight, adapter_up_weight):
@@ -146,7 +153,7 @@
         adapter_up_weight[0],
     )
     shifted = from_behind(passed_local[None], "section", -1)
-    merged_gradient = gram_adasum(grad_pair)
+    merged_gradient, shifted = gram_adasum(grad_pair, shifted)
     return (shifted, merged_gradient)
 
 

time: 111 us -> 113 us (1.018)
  blocking collectives: 20.7 us -> 0 us
  waiting for transfers between devices: 46.3 us -> 59.8 us
  starting transfers between devices: 25.2 us -> 31.6 us
  other arithmetic: 3.77 us -> 5.99 us
  local copies, waits for them, and re-layouts: 5.37 us -> 3.87 us
  matrix products: 5.52 us -> 6.85 us
    all_to_all x1 -> x0, blocking collectives: 20.7 us -> none  [gram_adasum(): rows = lax.all_to_all(partial[:, None, :], 'dp', 0, 0, tiled=True)]
    all_to_all x0 -> x1, waiting for transfers between devices: none -> 13.6 us  [gram_adasum(): rows = lax.all_to_all(partial[:, None, :], 'dp', 0, 0, tiled=True)]
    all_to_all x0 -> x1, starting transfers between devices: none -> 6.46 us  [gram_adasum(): rows = lax.all_to_all(partial[:, None, :], 'dp', 0, 0, tiled=True)]
    unnamed x14 -> x11, local copies, waits for them, and re-layouts: 3.06 us -> 1.54 us
    select_n x0 -> x1, other arithmetic: none -> 1.15 us  [gram_adasum(): passed = jnp.where(has_next, passed, jnp.zeros_like(passed))]
  transfers between devices with their start and end apart: 3 -> 4, of which waited for: 2 -> 3; matrix products, arithmetic and copies ran while one was open for 4% -> 5% of each run, Pallas kernels for 0% -> 0%
where the time goes in v14:
time: 113 us; the launch traced here: 112 us
  waiting for transfers between devices  59.8 us (53%)
  starting transfers between devices  31.6 us (28%)
  matrix products  6.85 us (6%)
  other arithmetic  5.99 us (5%)
  local copies, waits for them, and re-layouts  3.87 us (3%)
  Pallas kernels  3.45 us (3%)
    all_to_all x1, waiting for transfers between devices, gram_adasum(): chunks = lax.all_to_all(flat, 'dp', 0, 0, tiled=True)  32.9 us
    all_to_all x1, starting transfers between devices, gram_adasum(): chunks = lax.all_to_all(flat, 'dp', 0, 0, tiled=True)  18.7 us
    all_to_all x1, waiting for transfers between devices, gram_adasum(): rows = lax.all_to_all(partial[:, None, :], 'dp', 0, 0, tiled=True)  13.6 us
    all_to_all x1, waiting for transfers between devices, gram_adasum(): gram_rows = lax.all_to_all(spread, 'dp', 0, 0, tiled=True)  13.3 us
    all_to_all x1, starting transfers between devices, gram_adasum(): rows = lax.all_to_all(partial[:, None, :], 'dp', 0, 0, tiled=True)  6.46 us
    all_to_all x1, starting transfers between devices, gram_adasum(): gram_rows = lax.all_to_all(spread, 'dp', 0, 0, tiled=True)  4.54 us
    pallas_call x1, Pallas kernels, combine(): pl.pallas_call(combine_kernel, out_shape=jax.ShapeDtypeStruct((1, chunks....  3.45 us
  transfers between devices with their start and end apart: 4, of which 3 were waited for; matrix products, arithmetic and copies ran while one was open for 5% of the time, Pallas kernels for 0%

profile of v14, /device:TPU:6, one launch (start us, length us, event | category | flops | bytes accessed | tf_op | source)
XLA Modules:
  0.0 112.3 jit_solution(14757236562313770217)
XLA Ops:
  0.6 0.0 copy-start
  0.6 0.0 copy-start.1
  0.7 0.0 copy-start.2
  0.7 0.0 copy-start.4
  0.7 1.8 %fusion.13 = f32[128]{0:T(128)S(1)} fusion(bf16[1,128,5120]{2,1,0:T(8,128)(2,1)} %param.5), kind=kLoop, calls=%fused_computation.18 | loop fusion | flops 1965952 | bytes 1311232 | tf_op jit(solution)/shard_map/reduce_sum | solution.py:28
  2.5 1.8 %fusion.34 = bf16[128,16]{0,1:T(8,128)(2,1)S(1)} fusion(bf16[1,128,5120]{2,1,0:T(8,128)(2,1)} %param.6, bf16[1,16,5120]{2,1,0:T(8,128)(2,1)} %param.9), kind=kOutput, calls=%fused_computation.34 | convolution fusion | flops 20975616 | bytes 1478656 | tf_op jit(solution)/shard_map/sh,gh->sg/dot_general | solution.py:44
  4.3 0.0 copy-done.1
  4.3 0.0 copy-done.4
  4.3 1.2 %fusion.1 = f32[1,16,5120]{2,1,0:T(8,128)} fusion(bf16[128,16]{0,1:T(8,128)(2,1)S(1)} %fusion.34, bf16[1,128,5120]{2,1,0:T(8,128)(2,1)S(1)} %copy-done.1, f32[5120]{0:T(1024)S(1)} %bitcast.81, f32[128]{0:T(128)S(1)} %add_rsqrt_fusion), kind=kOutput, calls=%fused_computation.4 | convolution fusion | flops 23674880 | bytes 1663488 | tf_op jit(solution)/shard_map/tk,td->kd/dot_general | solution.py:49
  5.5 0.0 copy-done
  5.5 0.0 copy-done.2
  5.5 1.9 %fusion = f32[1,16,5120]{2,1,0:T(8,128)} fusion(bf16[1,128,5120]{2,1,0:T(8,128)(2,1)S(1)} %copy-done.2, bf16[1,128,5120]{2,1,0:T(8,128)(2,1)S(1)} %copy-done.1, f32[5120]{0:T(1024)S(1)} %bitcast.82, f32[128]{0:T(128)S(1)} %add_rsqrt_fusion, bf16[1,16,5120]{2,1,0:T(8,128)(2,1)S(1)} %copy-done), kind=kOutput, calls=%fused_computation.2 | convolution fusion | flops 44648448 | bytes 3133952 | tf_op jit(solution)/shard_map/tk,td->kd/dot_general | solution.py:37
  7.4 1.1 pad_maximum_fusion
  8.5 1.6 %all_to_all.24 = f32[64,1,2560]{2,1,0:T(1,128)} reshape(f32[2,16,5120]{2,1,0:T(8,128)S(1)} %pad_maximum_fusion) | data formatting | bytes 1310720 | tf_op jit(solution)/shard_map/all_to_all | solution.py:132
  10.2 18.7 %all-to-all-start = ((f32[64,1,2560]{2,1,0:T(1,128)}), f32[64,1,2560]{2,1,0:T(1,128)S(1)}, u32[]{:S(2)}, u32[]{:S(2)}) async-start(f32[64,1,2560]{2,1,0:T(1,128)} %all_to_all.24), calls=%async_computation | async-start | bytes 1310720 | tf_op jit(solution)/shard_map/all_to_all | solution.py:132
  28.9 0.7 fusion.8
  29.6 1.9 %fusion.19 = bf16[1,128,5120]{2,1,0:T(8,128)(2,1)} fusion(f32[128,5120]{1,0:T(8,128)S(1)} %get-tuple-element.7, bf16[1,128,5120]{2,1,0:T(8,128)(2,1)S(1)} %copy-done.1, bf16[1,128,5120]{2,1,0:T(8,128)(2,1)S(1)} %copy-done.2, f32[128]{0:T(128)S(1)} %broadcast_multiply_fusion, f32[128]{0:T(128)S(1)} %add_rsqrt_fusion), kind=kLoop, calls=%fused_computation.23 | loop fusion | flops 5242880 | bytes 6554624 | tf_op jit(solution)/shard_map/broadcast_in_dim | solution.py:155
  31.5 1.9 %collective-permute-start = (bf16[1,128,5120]{2,1,0:T(8,128)(2,1)}, bf16[1,128,5120]{2,1,0:T(8,128)(2,1)S(1)}, u32[]{:S(2)}, u32[]{:S(2)}) collective-permute-start(bf16[1,128,5120]{2,1,0:T(8,128)(2,1)} %fusion.19), channel_id=1, source_target_pairs={{64,0},{128,64},{192,128},{256,192},{320,256},{384,320},{448,384},... | collective-permute-start | bytes 3932168 | tf_op jit(solution)/shard_map/ppermute | solution.py:23
  33.4 32.9 %all-to-all-done = f32[64,1,2560]{2,1,0:T(1,128)S(1)} async-done(((f32[64,1,2560]{2,1,0:T(1,128)}), f32[64,1,2560]{2,1,0:T(1,128)S(1)}, u32[]{:S(2)}, u32[]{:S(2)}) %all-to-all-start) | async-done | bytes 655392 | tf_op jit(solution)/shard_map/all_to_all | solution.py:132
  66.3 1.3 %fusion.43 = f32[64,64]{1,0:T(8,128)} fusion(f32[64,1,2560]{2,1,0:T(1,128)S(1)} %all-to-all-done), kind=kOutput, calls=%fused_computation.43 | convolution fusion | flops 125829120 | bytes 671744 | tf_op jit(solution)/shard_map/dot_general | solution.py:136
  67.6 6.5 %all-to-all-start.1 = ((f32[64,1,64]{2,1,0:T(1,128)}), f32[64,1,64]{2,1,0:T(1,128)S(1)}, u32[]{:S(2)}, u32[]{:S(2)}) async-start(f32[64,1,64]{2,1,0:T(1,128)} %bitcast.9), calls=%async_computation.1 | async-start | bytes 65536 | tf_op jit(solution)/shard_map/all_to_all | solution.py:137
  74.1 0.9 copy.12
  74.9 13.6 %all-to-all-done.1 = f32[64,1,64]{2,1,0:T(1,128)S(1)} async-done(((f32[64,1,64]{2,1,0:T(1,128)}), f32[64,1,64]{2,1,0:T(1,128)S(1)}, u32[]{:S(2)}, u32[]{:S(2)}) %all-to-all-start.1) | async-done | bytes 16416 | tf_op jit(solution)/shard_map/all_to_all | solution.py:137
  88.5 0.1 broadcast_in_dim.19
  88.6 0.0 collective-permute-done
  88.6 0.6 broadcast_in_dim.20
  89.2 4.5 %all-to-all-start.2 = ((f32[64,1,128]{2,1,0:T(1,128)}), f32[64,1,128]{2,1,0:T(1,128)S(1)}, u32[]{:S(2)}, u32[]{:S(2)}) async-start(f32[64,1,128]{2,1,0:T(1,128)} %bitcast.12), calls=%async_computation.2 | async-start | bytes 65536 | tf_op jit(solution)/shard_map/all_to_all | solution.py:143
  93.8 1.2 %broadcast_select_fusion = bf16[1,128,5120]{2,1,0:T(8,128)(2,1)} fusion(bf16[1,128,5120]{2,1,0:T(8,128)(2,1)S(1)} %collective-permute-done, pred[]{:T(512)S(6)} %lt.3), kind=kLoop, calls=%fused_computation.31 | loop fusion | flops 655360 | bytes 2621441 | tf_op jit(solution)/shard_map/jit(_where)/select_n | solution.py:142
  94.9 13.3 %all-to-all-done.2 = f32[64,1,128]{2,1,0:T(1,128)S(1)} async-done(((f32[64,1,128]{2,1,0:T(1,128)}), f32[64,1,128]{2,1,0:T(1,128)S(1)}, u32[]{:S(2)}, u32[]{:S(2)}) %all-to-all-start.2) | async-done | bytes 32800 | tf_op jit(solution)/shard_map/all_to_all | solution.py:143
  108.3 0.0 copy-start.3
  108.3 0.6 copy-done.3
  108.9 3.4 %shard_map.68 = bf16[1,2560]{1,0:T(2,128)(2,1)} custom-call(f32[64,128]{1,0:T(8,128)} %bitcast.79, f32[64,2560]{1,0:T(8,128)} %bitcast.78), custom_call_target="tpu_custom_call" | custom-call | tf_op jit(solution)/shard_map/pallas_call | solution.py:121
  (3 shorter events, 0.0 us)
Async XLA Ops:
  0.6 4.9 %copy-start = (bf16[1,16,5120]{2,1,0:T(8,128)(2,1)S(1)}, bf16[1,16,5120]{2,1,0:T(8,128)(2,1)}, u32[]{:S(2)}) copy-start(bf16[1,16,5120]{2,1,0:T(8,128)(2,1)} %param.8) | copy-start | bytes 491524
  0.6 3.6 %copy-start.1 = (bf16[1,128,5120]{2,1,0:T(8,128)(2,1)S(1)}, bf16[1,128,5120]{2,1,0:T(8,128)(2,1)}, u32[]{:S(2)}) copy-start(bf16[1,128,5120]{2,1,0:T(8,128)(2,1)} %param.5) | copy-start | bytes 3932164
  0.7 4.8 %copy-start.2 = (bf16[1,128,5120]{2,1,0:T(8,128)(2,1)S(1)}, bf16[1,128,5120]{2,1,0:T(8,128)(2,1)}, u32[]{:S(2)}) copy-start(bf16[1,128,5120]{2,1,0:T(8,128)(2,1)} %param.6) | copy-start | bytes 3932164
  0.7 3.6 %copy-start.4 = (f32[1,5120]{1,0:T(1,128)S(1)}, f32[1,5120]{1,0:T(1,128)}, u32[]{:S(2)}) copy-start(f32[1,5120]{1,0:T(1,128)} %param.7) | copy-start | bytes 61444
  10.2 56.1 %all-to-all-start = ((f32[64,1,2560]{2,1,0:T(1,128)}), f32[64,1,2560]{2,1,0:T(1,128)S(1)}, u32[]{:S(2)}, u32[]{:S(2)}) async-start(f32[64,1,2560]{2,1,0:T(1,128)} %all_to_all.24), calls=%async_computation | async-start | bytes 1310720 | tf_op jit(solution)/shard_map/all_to_all | solution.py:132
  31.5 57.1 %collective-permute-start = (bf16[1,128,5120]{2,1,0:T(8,128)(2,1)}, bf16[1,128,5120]{2,1,0:T(8,128)(2,1)S(1)}, u32[]{:S(2)}, u32[]{:S(2)}) collective-permute-start(bf16[1,128,5120]{2,1,0:T(8,128)(2,1)} %fusion.19), channel_id=1, source_target_pairs={{64,0},{128,64},{192,128},{256,192},{320,256},{384,320},{448,384},... | collective-permute-start | bytes 3932168 | tf_op jit(solution)/shard_map/ppermute | solution.py:23
  67.6 20.9 %all-to-all-start.1 = ((f32[64,1,64]{2,1,0:T(1,128)}), f32[64,1,64]{2,1,0:T(1,128)S(1)}, u32[]{:S(2)}, u32[]{:S(2)}) async-start(f32[64,1,64]{2,1,0:T(1,128)} %bitcast.9), calls=%async_computation.1 | async-start | bytes 65536 | tf_op jit(solution)/shard_map/all_to_all | solution.py:137
  89.2 19.0 %all-to-all-start.2 = ((f32[64,1,128]{2,1,0:T(1,128)}), f32[64,1,128]{2,1,0:T(1,128)S(1)}, u32[]{:S(2)}, u32[]{:S(2)}) async-start(f32[64,1,128]{2,1,0:T(1,128)} %bitcast.12), calls=%async_computation.2 | async-start | bytes 65536 | tf_op jit(solution)/shard_map/all_to_all | solution.py:143
  108.3 0.6 copy-start.3

commit v15 on v14

--- a/solution.py
+++ b/solution.py
@@ -4,6 +4,7 @@
 from jax import lax
 from jax.sharding import PartitionSpec as P
 from jax.experimental import pallas as pl
+from jax.experimental.pallas import tpu as pltpu
 
 norm_eps = 1e-05
 pair_eps = 1e-06
@@ -86,7 +87,9 @@
     return np.eye(n, dtype=np.float32)[order]
 
 
-def combine_kernel(gram_ref, chunks_ref, out_ref):
+def combine_kernel(gram_ref, chunks_hbm, out_ref, chunks_ref, copy_sem):
+    fetch = pltpu.make_async_copy(chunks_hbm, chunks_ref, copy_sem)
+    fetch.start()
     n = gram_ref.shape[0]
     first_tensor = lax.axis_index("dp") < lax.axis_size("dp") // 2
     gram = jnp.where(first_tensor, gram_ref[:, 0:n], gram_ref[:, n:2 * n])
@@ -112,6 +115,7 @@
     column = lax.dot_general(
         eye, coef, (((1,), (1,)), ((), ())), precision=HIGH, preferred_element_type=jnp.float32
     )
+    fetch.wait()
     combined = jnp.sum(column * chunks_ref[...], axis=0, keepdims=True)
     out_ref[...] = combined.astype(out_ref.dtype)
 
@@ -121,11 +125,17 @@
     return pl.pallas_call(
         combine_kernel,
         out_shape=jax.ShapeDtypeStruct((1, chunks.shape[1]), jnp.bfloat16),
+        in_specs=[
+            pl.BlockSpec(memory_space=pltpu.VMEM),
+            pl.BlockSpec(memory_space=pl.ANY),
+        ],
+        out_specs=pl.BlockSpec(memory_space=pltpu.VMEM),
+        scratch_shapes=[pltpu.VMEM(chunks.shape, chunks.dtype), pltpu.SemaphoreType.DMA],
         interpret=interpret,
     )(gram_rows, chunks)
 
 
-def gram_adasum(grad_pair, passed):
+def gram_adasum(grad_pair):
     devices = lax.axis_size("dp")
     me = lax.axis_index("dp")
     flat = grad_pair.reshape(devices, -1)
@@ -137,11 +147,8 @@
     rows = lax.all_to_all(partial[:, None, :], "dp", 0, 0, tiled=True)
     rows = jnp.sum(rows.reshape(tensors, per_tensor, partial.shape[1]), axis=1)
     spread = jnp.broadcast_to(rows.reshape(1, -1), (devices, tensors * partial.shape[1]))
-    spread, passed = lax.optimization_barrier((spread, passed))
-    has_next = lax.axis_index("section") < lax.axis_size("section") - 1
-    passed = jnp.where(has_next, passed, jnp.zeros_like(passed))
     gram_rows = lax.all_to_all(spread, "dp", 0, 0, tiled=True)
-    return combine(gram_rows, chunks), passed
+    return combine(gram_rows, chunks)
 
 
 def per_device(activations, upstream, section_norm_gain, adapter_down_weight, adapter_up_weight):
@@ -153,7 +160,7 @@
         adapter_up_weight[0],
     )
     shifted = from_behind(passed_local[None], "section", -1)
-    merged_gradient, shifted = gram_adasum(grad_pair, shifted)
+    merged_gradient = gram_adasum(grad_pair)
     return (shifted, merged_gradient)
 
 

time: 113 us -> 111 us (0.982)
  blocking collectives: 0 us -> 20.7 us
  waiting for transfers between devices: 59.8 us -> 46.3 us
  starting transfers between devices: 31.6 us -> 25.2 us
  other arithmetic: 5.99 us -> 3.77 us
  local copies, waits for them, and re-layouts: 3.87 us -> 5.38 us
  matrix products: 6.85 us -> 5.52 us
    all_to_all x0 -> x1, blocking collectives: none -> 20.7 us  [gram_adasum(): rows = lax.all_to_all(partial[:, None, :], 'dp', 0, 0, tiled=True)]
    all_to_all x1 -> x0, waiting for transfers between devices: 13.6 us -> none  [gram_adasum(): rows = lax.all_to_all(partial[:, None, :], 'dp', 0, 0, tiled=True)]
    all_to_all x1 -> x0, starting transfers between devices: 6.46 us -> none  [gram_adasum(): rows = lax.all_to_all(partial[:, None, :], 'dp', 0, 0, tiled=True)]
    unnamed x11 -> x14, local copies, waits for them, and re-layouts: 1.54 us -> 3.06 us
    select_n x1 -> x0, other arithmetic: 1.15 us -> none  [gram_adasum(): passed = jnp.where(has_next, passed, jnp.zeros_like(passed))]
  transfers between devices with their start and end apart: 4 -> 3, of which waited for: 3 -> 2; matrix products, arithmetic and copies ran while one was open for 5% -> 4% of each run, Pallas kernels for 0% -> 0%
where the time goes in v15:
time: 111 us
  waiting for transfers between devices  46.3 us (42%)
  starting transfers between devices  25.2 us (23%)
  blocking collectives  20.7 us (19%)
  matrix products  5.52 us (5%)
  local copies, waits for them, and re-layouts  5.38 us (5%)
  other arithmetic  3.77 us (3%)
  Pallas kernels  3.11 us (3%)
    all_to_all x1, waiting for transfers between devices, gram_adasum(): chunks = lax.all_to_all(flat, 'dp', 0, 0, tiled=True)  32.9 us
    all_to_all x1, blocking collectives, gram_adasum(): rows = lax.all_to_all(partial[:, None, :], 'dp', 0, 0, tiled=True)  20.7 us
    all_to_all x1, starting transfers between devices, gram_adasum(): chunks = lax.all_to_all(flat, 'dp', 0, 0, tiled=True)  18.7 us
    all_to_all x1, waiting for transfers between devices, gram_adasum(): gram_rows = lax.all_to_all(spread, 'dp', 0, 0, tiled=True)  13.4 us
    all_to_all x1, starting transfers between devices, gram_adasum(): gram_rows = lax.all_to_all(spread, 'dp', 0, 0, tiled=True)  4.57 us
    pallas_call x1, Pallas kernels, combine(): pl.pallas_call(combine_kernel, out_shape=jax.ShapeDtypeStruct((1, chunks....  3.11 us
    unnamed x14, local copies, waits for them, and re-layouts  3.06 us
  transfers between devices with their start and end apart: 3, of which 2 were waited for; matrix products, arithmetic and copies ran while one was open for 4% of the time, Pallas kernels for 0%

profile of v15, /device:TPU:6, one launch (start us, length us, event | category | flops | bytes accessed | tf_op | source)
XLA Modules:
  0.0 110.8 jit_solution(92355265925900602)
XLA Ops:
  0.6 0.0 copy-start
  0.6 0.0 copy-start.1
  0.7 0.0 copy-start.2
  0.7 0.0 copy-start.5
  0.7 1.8 %fusion.13 = f32[128]{0:T(128)S(1)} fusion(bf16[1,128,5120]{2,1,0:T(8,128)(2,1)} %param.5), kind=kLoop, calls=%fused_computation.18 | loop fusion | flops 1965952 | bytes 1311232 | tf_op jit(solution)/shard_map/reduce_sum | solution.py:29
  2.5 1.8 %fusion.34 = bf16[128,16]{0,1:T(8,128)(2,1)S(1)} fusion(bf16[1,128,5120]{2,1,0:T(8,128)(2,1)} %param.6, bf16[1,16,5120]{2,1,0:T(8,128)(2,1)} %param.9), kind=kOutput, calls=%fused_computation.33 | convolution fusion | flops 20975616 | bytes 1478656 | tf_op jit(solution)/shard_map/sh,gh->sg/dot_general | solution.py:45
  4.3 0.0 copy-done
  4.3 0.0 copy-done.1
  4.3 0.0 copy-done.2
  4.3 0.0 copy-done.5
  4.3 1.9 %fusion = f32[1,16,5120]{2,1,0:T(8,128)} fusion(bf16[1,128,5120]{2,1,0:T(8,128)(2,1)S(1)} %copy-done.2, bf16[1,128,5120]{2,1,0:T(8,128)(2,1)S(1)} %copy-done.1, f32[5120]{0:T(1024)S(1)} %bitcast.81, f32[128]{0:T(128)S(1)} %add_rsqrt_fusion, bf16[1,16,5120]{2,1,0:T(8,128)(2,1)S(1)} %copy-done), kind=kOutput, calls=%fused_computation.2 | convolution fusion | flops 44648448 | bytes 3133952 | tf_op jit(solution)/shard_map/tk,td->kd/dot_general | solution.py:38
  6.2 0.0 copy-start.3
  6.2 0.5 fusion.1
  6.7 0.5 copy-done.3
  7.3 1.6 %all_to_all.21 = f32[64,1,2560]{2,1,0:T(1,128)} reshape(f32[2,16,5120]{2,1,0:T(8,128)S(1)} %pad_maximum_fusion) | data formatting | bytes 1310720 | tf_op jit(solution)/shard_map/all_to_all | solution.py:142
  8.9 18.7 %all-to-all-start = ((f32[64,1,2560]{2,1,0:T(1,128)}), f32[64,1,2560]{2,1,0:T(1,128)S(1)}, u32[]{:S(2)}, u32[]{:S(2)}) async-start(f32[64,1,2560]{2,1,0:T(1,128)} %all_to_all.21), calls=%async_computation | async-start | bytes 1310720 | tf_op jit(solution)/shard_map/all_to_all | solution.py:142
  27.6 0.7 fusion.7
  28.3 1.9 %fusion.20 = bf16[1,128,5120]{2,1,0:T(8,128)(2,1)} fusion(f32[128,5120]{1,0:T(8,128)S(1)} %get-tuple-element.3, bf16[1,128,5120]{2,1,0:T(8,128)(2,1)S(1)} %copy-done.1, bf16[1,128,5120]{2,1,0:T(8,128)(2,1)S(1)} %copy-done.2, f32[128]{0:T(128)S(1)} %broadcast_multiply_fusion, f32[128]{0:T(128)S(1)} %add_rsqrt_fusion), kind=kLoop, calls=%fused_computation.23 | loop fusion | flops 5242880 | bytes 6554624 | tf_op jit(solution)/shard_map/broadcast_in_dim | solution.py:162
  30.2 1.9 %collective-permute-start = (bf16[1,128,5120]{2,1,0:T(8,128)(2,1)}, bf16[1,128,5120]{2,1,0:T(8,128)(2,1)S(1)}, u32[]{:S(2)}, u32[]{:S(2)}) collective-permute-start(bf16[1,128,5120]{2,1,0:T(8,128)(2,1)} %fusion.20), channel_id=1, source_target_pairs={{64,0},{128,64},{192,128},{256,192},{320,256},{384,320},{448,384},... | collective-permute-start | bytes 3932168 | tf_op jit(solution)/shard_map/ppermute | solution.py:24
  32.1 32.9 %all-to-all-done = f32[64,1,2560]{2,1,0:T(1,128)S(1)} async-done(((f32[64,1,2560]{2,1,0:T(1,128)}), f32[64,1,2560]{2,1,0:T(1,128)S(1)}, u32[]{:S(2)}, u32[]{:S(2)}) %all-to-all-start) | async-done | bytes 655392 | tf_op jit(solution)/shard_map/all_to_all | solution.py:142
  65.0 0.7 fusion.43
  65.7 20.7 %all_to_all.25 = f32[64,1,64]{2,1,0:T(1,128)S(1)} all-to-all(f32[64,1,64]{2,1,0:T(1,128)S(1)} %bitcast.80), channel_id=1, replica_groups=mesh['section'=8,'dp'=64] {'dp'}, dimensions={0} | all-to-all | bytes 32768 | tf_op jit(solution)/shard_map/all_to_all | solution.py:147
  86.4 0.1 broadcast_in_dim.17
  86.5 0.6 broadcast_in_dim.18
  87.1 4.6 %all-to-all-start.2 = ((f32[64,1,128]{2,1,0:T(1,128)}), f32[64,1,128]{2,1,0:T(1,128)S(1)}, u32[]{:S(2)}, u32[]{:S(2)}) async-start(f32[64,1,128]{2,1,0:T(1,128)} %broadcast_in_dim.18), calls=%async_computation.2 | async-start | bytes 65536 | tf_op jit(solution)/shard_map/all_to_all | solution.py:150
  91.7 0.0 collective-permute-done
  91.7 0.9 copy.12
  92.6 13.4 %all-to-all-done.2 = f32[64,1,128]{2,1,0:T(1,128)S(1)} async-done(((f32[64,1,128]{2,1,0:T(1,128)}), f32[64,1,128]{2,1,0:T(1,128)S(1)}, u32[]{:S(2)}, u32[]{:S(2)}) %all-to-all-start.2) | async-done | bytes 32800 | tf_op jit(solution)/shard_map/all_to_all | solution.py:150
  106.0 0.0 copy-start.4
  106.0 0.6 copy-done.4
  106.6 3.1 %shard_map.68 = bf16[1,2560]{1,0:T(2,128)(2,1)} custom-call(f32[64,128]{1,0:T(8,128)} %bitcast.78, f32[64,2560]{1,0:T(8,128)} %bitcast.77), custom_call_target="tpu_custom_call" | custom-call | tf_op jit(solution)/shard_map/pallas_call | solution.py:125
  109.7 1.1 copy.14
  (4 shorter events, 0.1 us)
Async XLA Ops:
  0.6 3.6 %copy-start = (bf16[1,16,5120]{2,1,0:T(8,128)(2,1)S(1)}, bf16[1,16,5120]{2,1,0:T(8,128)(2,1)}, u32[]{:S(2)}) copy-start(bf16[1,16,5120]{2,1,0:T(8,128)(2,1)} %param.8) | copy-start | bytes 491524
  0.6 3.6 %copy-start.1 = (bf16[1,128,5120]{2,1,0:T(8,128)(2,1)S(1)}, bf16[1,128,5120]{2,1,0:T(8,128)(2,1)}, u32[]{:S(2)}) copy-start(bf16[1,128,5120]{2,1,0:T(8,128)(2,1)} %param.5) | copy-start | bytes 3932164
  0.7 3.6 %copy-start.2 = (bf16[1,128,5120]{2,1,0:T(8,128)(2,1)S(1)}, bf16[1,128,5120]{2,1,0:T(8,128)(2,1)}, u32[]{:S(2)}) copy-start(bf16[1,128,5120]{2,1,0:T(8,128)(2,1)} %param.6) | copy-start | bytes 3932164
  0.7 3.6 %copy-start.5 = (f32[1,5120]{1,0:T(1,128)S(1)}, f32[1,5120]{1,0:T(1,128)}, u32[]{:S(2)}) copy-start(f32[1,5120]{1,0:T(1,128)} %param.7) | copy-start | bytes 61444
  6.2 1.0 copy-start.3
  8.9 56.1 %all-to-all-start = ((f32[64,1,2560]{2,1,0:T(1,128)}), f32[64,1,2560]{2,1,0:T(1,128)S(1)}, u32[]{:S(2)}, u32[]{:S(2)}) async-start(f32[64,1,2560]{2,1,0:T(1,128)} %all_to_all.21), calls=%async_computation | async-start | bytes 1310720 | tf_op jit(solution)/shard_map/all_to_all | solution.py:142
  30.2 61.5 %collective-permute-start = (bf16[1,128,5120]{2,1,0:T(8,128)(2,1)}, bf16[1,128,5120]{2,1,0:T(8,128)(2,1)S(1)}, u32[]{:S(2)}, u32[]{:S(2)}) collective-permute-start(bf16[1,128,5120]{2,1,0:T(8,128)(2,1)} %fusion.20), channel_id=1, source_target_pairs={{64,0},{128,64},{192,128},{256,192},{320,256},{384,320},{448,384},... | collective-permute-start | bytes 3932168 | tf_op jit(solution)/shard_map/ppermute | solution.py:24
  87.1 18.9 %all-to-all-start.2 = ((f32[64,1,128]{2,1,0:T(1,128)}), f32[64,1,128]{2,1,0:T(1,128)S(1)}, u32[]{:S(2)}, u32[]{:S(2)}) async-start(f32[64,1,128]{2,1,0:T(1,128)} %broadcast_in_dim.18), calls=%async_computation.2 | async-start | bytes 65536 | tf_op jit(solution)/shard_map/all_to_all | solution.py:150
  106.0 0.6 copy-start.4

commit v16 on v13

--- a/solution.py
+++ b/solution.py
@@ -94,8 +94,8 @@
     while coef.shape[0] > 1:
         half = coef.shape[0] // 2
         first, second = coef[:half], coef[half:]
-        g_first = jnp.dot(first, gram, precision=HIGH, preferred_element_type=jnp.float32)
-        g_second = jnp.dot(second, gram, precision=HIGH, preferred_element_type=jnp.float32)
+        g_both = jnp.dot(coef, gram, precision=HIGH, preferred_element_type=jnp.float32)
+        g_first, g_second = g_both[:half], g_both[half:]
         inner_sum = jnp.sum(g_first * second, axis=1, keepdims=True)
         own_square = jnp.sum(g_first * first, axis=1, keepdims=True)
         far_square = jnp.sum(g_second * second, axis=1, keepdims=True)

time: 111 us -> 112 us (level)
  no operation moved by 1% of the time
where the time goes in v16:
time: 112 us; the launch traced here: 111 us
  waiting for transfers between devices  46.3 us (41%)
  starting transfers between devices  25.2 us (22%)
  blocking collectives  20.7 us (18%)
  matrix products  5.52 us (5%)
  local copies, waits for them, and re-layouts  5.37 us (5%)
  other arithmetic  3.77 us (3%)
  Pallas kernels  3.67 us (3%)
    all_to_all x1, waiting for transfers between devices, gram_adasum(): chunks = lax.all_to_all(flat, 'dp', 0, 0, tiled=True)  32.9 us
    all_to_all x1, blocking collectives, gram_adasum(): rows = lax.all_to_all(partial[:, None, :], 'dp', 0, 0, tiled=True)  20.7 us
    all_to_all x1, starting transfers between devices, gram_adasum(): chunks = lax.all_to_all(flat, 'dp', 0, 0, tiled=True)  18.7 us
    all_to_all x1, waiting for transfers between devices, gram_adasum(): gram_rows = lax.all_to_all(spread, 'dp', 0, 0, tiled=True)  13.4 us
    all_to_all x1, starting transfers between devices, gram_adasum(): gram_rows = lax.all_to_all(spread, 'dp', 0, 0, tiled=True)  4.57 us
    pallas_call x1, Pallas kernels, combine(): pl.pallas_call(combine_kernel, out_shape=jax.ShapeDtypeStruct((1, chunks....  3.67 us
    unnamed x14, local copies, waits for them, and re-layouts  3.06 us
  transfers between devices with their start and end apart: 3, of which 2 were waited for; matrix products, arithmetic and copies ran while one was open for 4% of the time, Pallas kernels for 0%

profile of v16, /device:TPU:6, one launch (start us, length us, event | category | flops | bytes accessed | tf_op | source)
XLA Modules:
  0.0 111.3 jit_solution(7895102033280783618)
XLA Ops:
  0.6 0.0 copy-start
  0.6 0.0 copy-start.1
  0.7 0.0 copy-start.2
  0.7 0.0 copy-start.5
  0.7 1.8 %fusion.13 = f32[128]{0:T(128)S(1)} fusion(bf16[1,128,5120]{2,1,0:T(8,128)(2,1)} %param.6), kind=kLoop, calls=%fused_computation.18 | loop fusion | flops 1965952 | bytes 1311232 | tf_op jit(solution)/shard_map/reduce_sum | solution.py:28
  2.5 1.8 %fusion.34 = bf16[128,16]{0,1:T(8,128)(2,1)S(1)} fusion(bf16[1,128,5120]{2,1,0:T(8,128)(2,1)} %param.7, bf16[1,16,5120]{2,1,0:T(8,128)(2,1)} %param.10), kind=kOutput, calls=%fused_computation.33 | convolution fusion | flops 20975616 | bytes 1478656 | tf_op jit(solution)/shard_map/sh,gh->sg/dot_general | solution.py:44
  4.3 0.0 copy-done
  4.3 0.0 copy-done.1
  4.3 0.0 copy-done.2
  4.3 0.0 copy-done.5
  4.3 1.9 %fusion = f32[1,16,5120]{2,1,0:T(8,128)} fusion(bf16[1,128,5120]{2,1,0:T(8,128)(2,1)S(1)} %copy-done.2, bf16[1,128,5120]{2,1,0:T(8,128)(2,1)S(1)} %copy-done.1, f32[5120]{0:T(1024)S(1)} %bitcast.81, f32[128]{0:T(128)S(1)} %add_rsqrt_fusion, bf16[1,16,5120]{2,1,0:T(8,128)(2,1)S(1)} %copy-done), kind=kOutput, calls=%fused_computation.2 | convolution fusion | flops 44648448 | bytes 3133952 | tf_op jit(solution)/shard_map/tk,td->kd/dot_general | solution.py:37
  6.2 0.0 copy-start.3
  6.2 0.5 fusion.1
  6.7 0.5 copy-done.3
  7.3 1.6 %all_to_all.21 = f32[64,1,2560]{2,1,0:T(1,128)} reshape(f32[2,16,5120]{2,1,0:T(8,128)S(1)} %pad_maximum_fusion) | data formatting | bytes 1310720 | tf_op jit(solution)/shard_map/all_to_all | solution.py:128
  8.9 18.7 %all-to-all-start = ((f32[64,1,2560]{2,1,0:T(1,128)}), f32[64,1,2560]{2,1,0:T(1,128)S(1)}, u32[]{:S(2)}, u32[]{:S(2)}) async-start(f32[64,1,2560]{2,1,0:T(1,128)} %all_to_all.21), calls=%async_computation | async-start | bytes 1310720 | tf_op jit(solution)/shard_map/all_to_all | solution.py:128
  27.6 0.7 fusion.7
  28.3 1.9 %fusion.20 = bf16[1,128,5120]{2,1,0:T(8,128)(2,1)} fusion(f32[128,5120]{1,0:T(8,128)S(1)} %get-tuple-element.3, bf16[1,128,5120]{2,1,0:T(8,128)(2,1)S(1)} %copy-done.1, bf16[1,128,5120]{2,1,0:T(8,128)(2,1)S(1)} %copy-done.2, f32[128]{0:T(128)S(1)} %broadcast_multiply_fusion, f32[128]{0:T(128)S(1)} %add_rsqrt_fusion), kind=kLoop, calls=%fused_computation.23 | loop fusion | flops 5242880 | bytes 6554624 | tf_op jit(solution)/shard_map/broadcast_in_dim | solution.py:148
  30.2 1.9 %collective-permute-start = (bf16[1,128,5120]{2,1,0:T(8,128)(2,1)}, bf16[1,128,5120]{2,1,0:T(8,128)(2,1)S(1)}, u32[]{:S(2)}, u32[]{:S(2)}) collective-permute-start(bf16[1,128,5120]{2,1,0:T(8,128)(2,1)} %fusion.20), channel_id=1, source_target_pairs={{64,0},{128,64},{192,128},{256,192},{320,256},{384,320},{448,384},... | collective-permute-start | bytes 3932168 | tf_op jit(solution)/shard_map/ppermute | solution.py:23
  32.1 32.9 %all-to-all-done = f32[64,1,2560]{2,1,0:T(1,128)S(1)} async-done(((f32[64,1,2560]{2,1,0:T(1,128)}), f32[64,1,2560]{2,1,0:T(1,128)S(1)}, u32[]{:S(2)}, u32[]{:S(2)}) %all-to-all-start) | async-done | bytes 655392 | tf_op jit(solution)/shard_map/all_to_all | solution.py:128
  65.0 0.7 fusion.43
  65.7 20.7 %all_to_all.25 = f32[64,1,64]{2,1,0:T(1,128)S(1)} all-to-all(f32[64,1,64]{2,1,0:T(1,128)S(1)} %bitcast.80), channel_id=1, replica_groups=mesh['section'=8,'dp'=64] {'dp'}, dimensions={0} | all-to-all | bytes 32768 | tf_op jit(solution)/shard_map/all_to_all | solution.py:133
  86.4 0.1 broadcast_in_dim.17
  86.5 0.6 broadcast_in_dim.18
  87.1 4.6 %all-to-all-start.2 = ((f32[64,1,128]{2,1,0:T(1,128)}), f32[64,1,128]{2,1,0:T(1,128)S(1)}, u32[]{:S(2)}, u32[]{:S(2)}) async-start(f32[64,1,128]{2,1,0:T(1,128)} %broadcast_in_dim.18), calls=%async_computation.2 | async-start | bytes 65536 | tf_op jit(solution)/shard_map/all_to_all | solution.py:136
  91.7 0.0 collective-permute-done
  91.7 0.9 copy.13
  92.6 13.4 %all-to-all-done.2 = f32[64,1,128]{2,1,0:T(1,128)S(1)} async-done(((f32[64,1,128]{2,1,0:T(1,128)}), f32[64,1,128]{2,1,0:T(1,128)S(1)}, u32[]{:S(2)}, u32[]{:S(2)}) %all-to-all-start.2) | async-done | bytes 32800 | tf_op jit(solution)/shard_map/all_to_all | solution.py:136
  106.0 0.0 copy-start.4
  106.0 0.6 copy-done.4
  106.6 3.7 %shard_map.77 = bf16[1,2560]{1,0:T(2,128)(2,1)} custom-call(f32[64,64]{1,0:T(8,128)} %constant.19.clone.start_ref, f32[64,128]{1,0:T(8,128)} %bitcast.78, f32[64,2560]{1,0:T(8,128)} %bitcast.77), custom_call_target="tpu_custom_call" | custom-call | tf_op jit(solution)/shard_map/pallas_call | solution.py:117
  110.3 1.1 copy.15
  (4 shorter events, 0.1 us)
Async XLA Ops:
  0.6 3.6 %copy-start = (bf16[1,16,5120]{2,1,0:T(8,128)(2,1)S(1)}, bf16[1,16,5120]{2,1,0:T(8,128)(2,1)}, u32[]{:S(2)}) copy-start(bf16[1,16,5120]{2,1,0:T(8,128)(2,1)} %param.9) | copy-start | bytes 491524
  0.6 3.6 %copy-start.1 = (bf16[1,128,5120]{2,1,0:T(8,128)(2,1)S(1)}, bf16[1,128,5120]{2,1,0:T(8,128)(2,1)}, u32[]{:S(2)}) copy-start(bf16[1,128,5120]{2,1,0:T(8,128)(2,1)} %param.6) | copy-start | bytes 3932164
  0.7 3.6 %copy-start.2 = (bf16[1,128,5120]{2,1,0:T(8,128)(2,1)S(1)}, bf16[1,128,5120]{2,1,0:T(8,128)(2,1)}, u32[]{:S(2)}) copy-start(bf16[1,128,5120]{2,1,0:T(8,128)(2,1)} %param.7) | copy-start | bytes 3932164
  0.7 3.6 %copy-start.5 = (f32[1,5120]{1,0:T(1,128)S(1)}, f32[1,5120]{1,0:T(1,128)}, u32[]{:S(2)}) copy-start(f32[1,5120]{1,0:T(1,128)} %param.8) | copy-start | bytes 61444
  6.2 1.0 copy-start.3
  8.9 56.1 %all-to-all-start = ((f32[64,1,2560]{2,1,0:T(1,128)}), f32[64,1,2560]{2,1,0:T(1,128)S(1)}, u32[]{:S(2)}, u32[]{:S(2)}) async-start(f32[64,1,2560]{2,1,0:T(1,128)} %all_to_all.21), calls=%async_computation | async-start | bytes 1310720 | tf_op jit(solution)/shard_map/all_to_all | solution.py:128
  30.2 61.5 %collective-permute-start = (bf16[1,128,5120]{2,1,0:T(8,128)(2,1)}, bf16[1,128,5120]{2,1,0:T(8,128)(2,1)S(1)}, u32[]{:S(2)}, u32[]{:S(2)}) collective-permute-start(bf16[1,128,5120]{2,1,0:T(8,128)(2,1)} %fusion.20), channel_id=1, source_target_pairs={{64,0},{128,64},{192,128},{256,192},{320,256},{384,320},{448,384},... | collective-permute-start | bytes 3932168 | tf_op jit(solution)/shard_map/ppermute | solution.py:23
  87.1 18.9 %all-to-all-start.2 = ((f32[64,1,128]{2,1,0:T(1,128)}), f32[64,1,128]{2,1,0:T(1,128)S(1)}, u32[]{:S(2)}, u32[]{:S(2)}) async-start(f32[64,1,128]{2,1,0:T(1,128)} %broadcast_in_dim.18), calls=%async_computation.2 | async-start | bytes 65536 | tf_op jit(solution)/shard_map/all_to_all | solution.py:136
  106.0 0.6 copy-start.4
